TPU v7x, 128 devices: a whole 4x4x4 slice. The times are simulated.
128 devices in a mesh: gx: 8 (over x, core), yz: 16 (over z, y).
Axes of the slice: x: 4, y: 4, z: 4, core: 2. Of those that a mesh axis runs over, the one named last changes fastest.
Arguments:
- hidden_in: bfloat16 [2, 128, 8192], P(None, ('gx', 'yz')), may hold values from -6 to 6
- k_cache: bfloat16 [128, 1024, 1024], P(('gx', 'yz'))
- v_cache: bfloat16 [128, 1024, 1024], P(('gx', 'yz')), may hold values from -6 to 6
- lengths: int32 [128], P(('gx', 'yz')), may hold values from 1 to 1024, as said below
- counts: int32 [128, 16], P(('gx', 'yz')), may hold values from 0 to 3
- token_elem: int32 [512], replicated, may hold values from 0 to 16, as said below
- tokens: int32 [128], P(('gx', 'yz')), may hold values from 0 to 511
- attn_gain: float32 [8192], replicated, may hold values from 0.5 to 1.5
- qkv_weight: bfloat16 [8192, 10240], P('gx', 'yz'), may hold values from -0.0625 to 0.0625
- o_weight: bfloat16 [8192, 8192], P('gx', 'yz'), may hold values from -0.0625 to 0.0625
- ffn_gain: float32 [8192], replicated, may hold values from 0.5 to 1.5
- gate_up_weight: bfloat16 [8192, 57344], P('gx', 'yz'), may hold values from -0.0625 to 0.0625
- down_weight: bfloat16 [28672, 8192], P('gx', 'yz'), may hold values from -0.03125 to 0.03125
- final_gain: float32 [8192], replicated, may hold values from 0.5 to 1.5
- lm_weight: bfloat16 [8192, 512], P(('gx', 'yz'))
Outputs:
- layer_out: bfloat16 [2, 128, 8192], P(None, ('gx', 'yz'))
- log_probs: float32 [2, 128, 512], P(None, ('gx', 'yz'))
Inputs may be any that keep to these rules, and one draw needn't show every extreme that they name: `lengths`: some spectrum uses all 1024 positions. `token_elem`: some token has no element (value 16).
All inputs are finite; a program needn't handle non-finite values.
Results may differ from a plain program's by a relative error of at most 0.022.
Values may be sent and summed in bfloat16 or wider, within the bound.
No kernel may reach another device: no remote copies, remote signals or barrier semaphores. Data moves between devices by JAX's collectives and lax.ppermute only.
A program may use at most 128 MiB of HBM per device.

v0:
```python
import math

import jax
import jax.numpy as jnp
from jax import lax
from jax.sharding import PartitionSpec as P

FF = 28672
HEADS = 64
KV_HEADS = 8
HEAD = 128
VOCAB = 512
ELEMENTS = 16


NORM_EPS = 1e-05
ROPE_THETA = 500000.0


def norm_rows(values, gain_vec):
    wide = values.astype(jnp.float32)
    inverse = lax.rsqrt(jnp.mean(wide * wide, axis=-1, keepdims=True) + NORM_EPS)
    return (wide * inverse * gain_vec).astype(jnp.bfloat16)


def rotate(heads_in, positions):
    half_width = heads_in.shape[-1] // 2
    frequency = jnp.power(
        ROPE_THETA, -(jnp.arange(half_width, dtype=jnp.float32) * 2.0 / heads_in.shape[-1])
    )
    angles = positions.astype(jnp.float32)[:, None] * frequency[None, :]
    cos_part = jnp.cos(angles)[:, None, :]
    sin_part = jnp.sin(angles)[:, None, :]
    wide = heads_in.astype(jnp.float32)
    first_half = wide[..., :half_width]
    second_half = wide[..., half_width:]
    joined = jnp.concatenate(
        [
            first_half * cos_part - second_half * sin_part,
            second_half * cos_part + first_half * sin_part,
        ],
        -1,
    )
    return joined.astype(jnp.bfloat16)


def spread_rows(inputs):
    gathered = lax.all_gather(inputs, "yz", axis=0, tiled=True)
    return lax.all_to_all(gathered, "gx", split_axis=1, concat_axis=0, tiled=True)


def project(inputs, weight):
    spread = spread_rows(inputs)
    summed = lax.psum_scatter(
        jnp.dot(spread, weight, preferred_element_type=jnp.float32),
        "gx",
        scatter_dimension=0,
        tiled=True,
    )
    return lax.all_to_all(
        summed.astype(jnp.bfloat16), "yz", split_axis=0, concat_axis=1, tiled=True
    )


def head_logits(normed, lm_weight):
    slice_width = lm_weight.shape[0]
    offset_cols = lax.axis_index("yz") * slice_width
    spread = spread_rows(normed)
    own_cols = lax.dynamic_slice_in_dim(spread, offset_cols, slice_width, 1)
    return lax.psum_scatter(
        jnp.dot(own_cols, lm_weight, preferred_element_type=jnp.float32),
        ("gx", "yz"),
        scatter_dimension=0,
        tiled=True,
    )


def attend(queries, k_cache, v_cache, lengths, keys_new, values_new):
    groups = HEADS // KV_HEADS
    factor = 1.0 / math.sqrt(HEAD)
    rows_here = queries.shape[0]
    cache_len = k_cache.shape[1]
    fresh = keys_new.shape[1]
    query_heads = queries.reshape(rows_here, KV_HEADS, groups, HEAD)
    kcache_heads = k_cache.reshape(rows_here, cache_len, KV_HEADS, HEAD)
    vcache_heads = v_cache.reshape(rows_here, cache_len, KV_HEADS, HEAD)
    knew_heads = keys_new.reshape(rows_here, fresh, KV_HEADS, HEAD)
    vnew_heads = values_new.reshape(rows_here, fresh, KV_HEADS, HEAD)
    scores_cache = (
        jnp.einsum("rkgd,rlkd->rkgl", query_heads, kcache_heads, preferred_element_type=jnp.float32)
        * factor
    )
    valid = jnp.arange(cache_len)[None, None, None, :] < lengths[:, None, None, None]
    scores_cache = jnp.where(valid, scores_cache, -jnp.inf)
    scores_new = (
        jnp.einsum("rkgd,rnkd->rkgn", query_heads, knew_heads, preferred_element_type=jnp.float32)
        * factor
    )
    largest = jnp.maximum(jnp.max(scores_cache, -1), jnp.max(scores_new, -1))[..., None]
    exp_cache = jnp.where(valid, jnp.exp(scores_cache - largest), 0.0)
    exp_new = jnp.exp(scores_new - largest)
    denominator = jnp.sum(exp_cache, -1, keepdims=True) + jnp.sum(exp_new, -1, keepdims=True)
    weights_cache = (exp_cache / denominator).astype(jnp.bfloat16)
    weights_new = (exp_new / denominator).astype(jnp.bfloat16)
    result = jnp.einsum(
        "rkgl,rlkd->rkgd", weights_cache, vcache_heads, preferred_element_type=jnp.float32
    )
    result = result + jnp.einsum(
        "rkgn,rnkd->rkgd", weights_new, vnew_heads, preferred_element_type=jnp.float32
    )
    return result.reshape(rows_here, HEADS * HEAD).astype(jnp.bfloat16)


def element_table(token_elem):
    return (token_elem[:, None] == jnp.arange(ELEMENTS, dtype=jnp.int32)[None, :]).astype(
        jnp.float32
    )


def masked_log_probs(logits, remaining, token_elem):
    element_hot = element_table(token_elem)
    per_token = jnp.dot(remaining, element_hot.T)
    allowed = (per_token > 0.5) | (token_elem == ELEMENTS)[None, :]
    largest = jnp.max(jnp.where(allowed, logits, -jnp.inf), -1, keepdims=True)
    shifted = logits - largest
    denominator = jnp.sum(jnp.where(allowed, jnp.exp(shifted), 0.0), -1, keepdims=True)
    return jnp.where(allowed, shifted - jnp.log(denominator), 0.0)


def used_elements(tokens, token_elem):
    token_hot = (tokens[:, None] == jnp.arange(VOCAB, dtype=jnp.int32)[None, :]).astype(jnp.float32)
    return jnp.dot(token_hot, element_table(token_elem))


def per_device(
    hidden_in,
    k_cache,
    v_cache,
    lengths,
    counts,
    token_elem,
    tokens,
    attn_gain,
    qkv_weight,
    o_weight,
    ffn_gain,
    gate_up_weight,
    down_weight,
    final_gain,
    lm_weight,
):
    q_width = HEADS * HEAD
    kv_width = KV_HEADS * HEAD
    key_list = []
    value_list = []
    result_list = []
    logit_steps = []
    for which_step in range(2):
        positions = lengths + which_step
        mixed = project(norm_rows(hidden_in[which_step], attn_gain), qkv_weight)
        queries = rotate(mixed[:, :q_width].reshape(-1, HEADS, HEAD), positions).reshape(
            -1, q_width
        )
        keys_now = rotate(
            mixed[:, q_width : q_width + kv_width].reshape(-1, KV_HEADS, HEAD), positions
        ).reshape(-1, kv_width)
        queries, keys_now, values_now = (queries, keys_now, mixed[:, q_width + kv_width :])
        key_list.append(keys_now)
        value_list.append(values_now)
        attended = attend(
            queries, k_cache, v_cache, lengths, jnp.stack(key_list, 1), jnp.stack(value_list, 1)
        )
        projected = project(attended, o_weight)
        residual = (
            hidden_in[which_step].astype(jnp.float32) + projected.astype(jnp.float32)
        ).astype(jnp.bfloat16)
        gate_up = project(norm_rows(residual, ffn_gain), gate_up_weight)
        hidden_units = (
            jax.nn.silu(gate_up[:, :FF].astype(jnp.float32)) * gate_up[:, FF:].astype(jnp.float32)
        ).astype(jnp.bfloat16)
        lowered = project(hidden_units, down_weight)
        result = (residual.astype(jnp.float32) + lowered.astype(jnp.float32)).astype(jnp.bfloat16)
        logits = head_logits(norm_rows(result, final_gain), lm_weight)
        result, logits = (result, logits)
        result_list.append(result)
        logit_steps.append(logits)
    outputs = jnp.stack(result_list)
    remaining = counts.astype(jnp.float32)
    first_log = masked_log_probs(logit_steps[0], remaining, token_elem)
    remaining = remaining - used_elements(tokens, token_elem)
    second_log = masked_log_probs(logit_steps[1], remaining, token_elem)
    return (outputs, jnp.stack([first_log, second_log]))


def solution(mesh):
    return jax.shard_map(
        per_device,
        mesh=mesh,
        in_specs=(
            P(None, ("gx", "yz"), None),
            P(("gx", "yz"), None, None),
            P(("gx", "yz"), None, None),
            P(("gx", "yz")),
            P(("gx", "yz"), None),
            P(),
            P(("gx", "yz")),
            P(),
            P("gx", "yz"),
            P("gx", "yz"),
            P(),
            P("gx", "yz"),
            P("gx", "yz"),
            P(),
            P(("gx", "yz"), None),
        ),
        out_specs=(P(None, ("gx", "yz"), None), P(None, ("gx", "yz"), None)),
        check_vma=False,
    )
```

profile of v0, /device:TPU:1, one launch (start us, length us, event | category | flops | bytes accessed | tf_op | source)
XLA Modules:
  0.0 964.6 jit_solution(5913646445156775769)
XLA Ops:
  8.2 1.4 fusion.59
  11.1 20.9 %all-gather = bf16[131072]{0:T(1024)(128)(2,1)S(1)} all-gather(bf16[8192]{0:T(1024)(128)(2,1)S(1)} %multiply_convert_fusion.3), channel_id=2, replica_groups=mesh['gx'=8,'yz'=16] {'yz'}, dimensions={0}, use_global_device_ids=true | all-gather | bytes 278528 | tf_op jit(solution)/shard_map/all_gather | solution.py:48
  32.2 16.4 %all_to_all.306 = bf16[16,8,1024]{2,0,1:T(8,128)(2,1)S(1)} all-to-all(bf16[16,8,1024]{2,0,1:T(8,128)(2,1)S(1)} %copy.63), channel_id=1, replica_groups=mesh['gx'=8,'yz'=16] {'gx'}, dimensions={1} | all-to-all | bytes 524288 | tf_op jit(solution)/shard_map/all_to_all | solution.py:49
  50.5 25.7 %reduce-scatter.9.cloned.1.call-done = f32[16,640]{1,0:T(8,128)} async-done(((f32[128,640]{1,0:T(8,128)}), f32[16,640]{1,0:T(8,128)}) %reduce-scatter.9.cloned.1.call-update) | async-done | bytes 40976 | tf_op jit(solution)/shard_map/reduce_scatter | solution.py:54
  78.7 6.8 all-to-all-start.1
  85.5 2.4 copy.97
  87.9 2.0 copy.98
  89.9 2.0 all-to-all-done.1
  94.9 18.7 %all-gather.6 = bf16[16,1,8192]{2,1,0:T(2,128)(2,1)} all-gather(bf16[1,1,8192]{2,1,0:T(2,128)(2,1)S(1)} %reshape.875), channel_id=1, replica_groups=mesh['gx'=8,'yz'=16] {'yz'}, dimensions={0}, use_global_device_ids=true | all-gather | bytes 278528 | tf_op jit(solution)/shard_map/all_gather | solution.py:48
  113.7 3.3 reduce.22
  117.9 18.7 %all_to_all.307 = bf16[16,8,1024]{2,0,1:T(8,128)(2,1)S(1)} all-to-all(bf16[16,8,1024]{2,0,1:T(8,128)(2,1)S(1)} %bitcast.213), channel_id=1, replica_groups=mesh['gx'=8,'yz'=16] {'gx'}, dimensions={1} | all-to-all | bytes 524288 | tf_op jit(solution)/shard_map/all_to_all | solution.py:49
  136.6 2.3 fusion.104
  138.9 25.7 %reduce-scatter.11.cloned.1.call-done = f32[16,512]{1,0:T(8,128)} async-done(((f32[128,512]{1,0:T(8,128)}), f32[16,512]{1,0:T(8,128)}) %reduce-scatter.11.cloned.1.call-update) | async-done | bytes 32784 | tf_op jit(solution)/shard_map/reduce_scatter | solution.py:54
  166.0 13.0 %all_to_all.308 = bf16[16,2,256]{2,1,0:T(2,128)(2,1)S(1)} all-to-all(bf16[16,2,256]{2,1,0:T(2,128)(2,1)S(1)} %reshape.903), channel_id=1, replica_groups=mesh['gx'=8,'yz'=16] {'yz'}, dimensions={0} | all-to-all | bytes 32768 | tf_op jit(solution)/shard_map/all_to_all | solution.py:60
  183.2 18.3 %all-gather.1 = bf16[131072]{0:T(1024)(128)(2,1)} all-gather(bf16[8192]{0:T(1024)(128)(2,1)S(1)} %get-tuple-element.10), channel_id=3, replica_groups=mesh['gx'=8,'yz'=16] {'yz'}, dimensions={0}, use_global_device_ids=true | all-gather | bytes 278528 | tf_op jit(solution)/shard_map/all_gather | solution.py:48
  201.4 1.8 all_to_all.241
  204.3 18.9 %all_to_all.309 = bf16[16,8,1024]{2,0,1:T(8,128)(2,1)S(1)} all-to-all(bf16[16,8,1024]{2,0,1:T(8,128)(2,1)S(1)} %copy.70), channel_id=1, replica_groups=mesh['gx'=8,'yz'=16] {'gx'}, dimensions={1} | all-to-all | bytes 524288 | tf_op jit(solution)/shard_map/all_to_all | solution.py:49
  223.2 5.5 fusion.105
  228.7 27.9 %reduce-scatter.13.cloned.1.call-done = f32[16,3584]{1,0:T(8,128)} async-done(((f32[128,3584]{1,0:T(8,128)}), f32[16,3584]{1,0:T(8,128)}) %reduce-scatter.13.cloned.1.call-update) | async-done | bytes 229392 | tf_op jit(solution)/shard_map/reduce_scatter | solution.py:54
  256.6 1.6 convert_bitcast_fusion.3
  258.2 2.1 reduce.28
  260.3 1.6 reshape.905
  261.9 13.7 %all_to_all.310 = bf16[16,2,1792]{2,1,0:T(2,128)(2,1)} all-to-all(bf16[16,2,1792]{2,1,0:T(2,128)(2,1)} %reshape.905), channel_id=1, replica_groups=mesh['gx'=8,'yz'=16] {'yz'}, dimensions={0} | all-to-all | bytes 229376 | tf_op jit(solution)/shard_map/all_to_all | solution.py:60
  275.6 1.7 reshape.906
  278.5 21.8 %all-gather.7 = bf16[16,1,28672]{2,1,0:T(2,128)(2,1)} all-gather(bf16[1,1,28672]{2,1,0:T(2,128)(2,1)S(1)} %convert_bitcast_fusion.2), channel_id=1, replica_groups=mesh['gx'=8,'yz'=16] {'yz'}, dimensions={0}, use_global_device_ids=true | all-gather | bytes 974848 | tf_op jit(solution)/shard_map/all_gather | solution.py:48
  300.3 7.8 reduce.23
  309.5 25.2 %all_to_all.311 = bf16[16,8,3584]{2,0,1:T(8,128)(2,1)S(1)} all-to-all(bf16[16,8,3584]{2,0,1:T(8,128)(2,1)S(1)} %bitcast.204), channel_id=1, replica_groups=mesh['gx'=8,'yz'=16] {'gx'}, dimensions={1} | all-to-all | bytes 1835008 | tf_op jit(solution)/shard_map/all_to_all | solution.py:49
  336.2 25.6 %reduce-scatter.15.cloned.1.call-done = f32[16,512]{1,0:T(8,128)} async-done(((f32[128,512]{1,0:T(8,128)}), f32[16,512]{1,0:T(8,128)}) %reduce-scatter.15.cloned.1.call-update) | async-done | bytes 32784 | tf_op jit(solution)/shard_map/reduce_scatter | solution.py:54
  363.1 13.0 %all_to_all.312 = bf16[16,2,256]{2,1,0:T(2,128)(2,1)S(1)} all-to-all(bf16[16,2,256]{2,1,0:T(2,128)(2,1)S(1)} %reshape.907), channel_id=1, replica_groups=mesh['gx'=8,'yz'=16] {'yz'}, dimensions={0} | all-to-all | bytes 32768 | tf_op jit(solution)/shard_map/all_to_all | solution.py:60
  379.8 18.3 %all-gather.2 = bf16[131072]{0:T(1024)(128)(2,1)} all-gather(bf16[8192]{0:T(1024)(128)(2,1)S(1)} %multiply_convert_fusion.2), channel_id=4, replica_groups=mesh['gx'=8,'yz'=16] {'yz'}, dimensions={0}, use_global_device_ids=true | all-gather | bytes 278528 | tf_op jit(solution)/shard_map/all_gather | solution.py:48
  398.1 1.8 all_to_all.254
  400.9 18.9 %all_to_all.313 = bf16[16,8,1024]{2,0,1:T(8,128)(2,1)S(1)} all-to-all(bf16[16,8,1024]{2,0,1:T(8,128)(2,1)S(1)} %copy.75), channel_id=1, replica_groups=mesh['gx'=8,'yz'=16] {'gx'}, dimensions={1} | all-to-all | bytes 524288 | tf_op jit(solution)/shard_map/all_to_all | solution.py:49
  421.6 25.1 %reduce-scatter.17.cloned.1.call-done = f32[16,640]{1,0:T(8,128)} async-done(((f32[128,640]{1,0:T(8,128)}), f32[16,640]{1,0:T(8,128)}) %reduce-scatter.17.cloned.1.call-update) | async-done | bytes 40976 | tf_op jit(solution)/shard_map/reduce_scatter | solution.py:54
  448.1 1.9 reduce.30
  451.4 6.9 all-to-all-start.9
  459.0 5.8 all-to-all-done.9
  464.8 1.5 reshape.910
  471.5 16.9 %all-gather.8 = bf16[16,1,8192]{2,1,0:T(2,128)(2,1)S(1)} all-gather(bf16[1,1,8192]{2,1,0:T(2,128)(2,1)S(1)} %reshape.879), channel_id=1, replica_groups=mesh['gx'=8,'yz'=16] {'yz'}, dimensions={0}, use_global_device_ids=true | all-gather | bytes 278528 | tf_op jit(solution)/shard_map/all_gather | solution.py:48
  488.5 1.5 reduce.24
  490.1 18.7 %all_to_all.314 = bf16[16,8,1024]{2,0,1:T(8,128)(2,1)S(1)} all-to-all(bf16[16,8,1024]{2,0,1:T(8,128)(2,1)S(1)} %bitcast.214), channel_id=1, replica_groups=mesh['gx'=8,'yz'=16] {'gx'}, dimensions={1} | all-to-all | bytes 524288 | tf_op jit(solution)/shard_map/all_to_all | solution.py:49
  509.9 25.7 %reduce-scatter.19.cloned.1.call-done = f32[16,512]{1,0:T(8,128)} async-done(((f32[128,512]{1,0:T(8,128)}), f32[16,512]{1,0:T(8,128)}) %reduce-scatter.19.cloned.1.call-update) | async-done | bytes 32784 | tf_op jit(solution)/shard_map/reduce_scatter | solution.py:54
  536.9 13.0 %all_to_all.315 = bf16[16,2,256]{2,1,0:T(2,128)(2,1)S(1)} all-to-all(bf16[16,2,256]{2,1,0:T(2,128)(2,1)S(1)} %reshape.911), channel_id=1, replica_groups=mesh['gx'=8,'yz'=16] {'yz'}, dimensions={0} | all-to-all | bytes 32768 | tf_op jit(solution)/shard_map/all_to_all | solution.py:60
  551.4 16.7 %all-gather.3 = bf16[131072]{0:T(1024)(128)(2,1)S(1)} all-gather(bf16[8192]{0:T(1024)(128)(2,1)S(1)} %get-tuple-element.8), channel_id=5, replica_groups=mesh['gx'=8,'yz'=16] {'yz'}, dimensions={0}, use_global_device_ids=true | all-gather | bytes 278528 | tf_op jit(solution)/shard_map/all_gather | solution.py:48
  568.3 18.6 %all_to_all.316 = bf16[16,8,1024]{2,0,1:T(8,128)(2,1)S(1)} all-to-all(bf16[16,8,1024]{2,0,1:T(8,128)(2,1)S(1)} %copy.84), channel_id=1, replica_groups=mesh['gx'=8,'yz'=16] {'gx'}, dimensions={1} | all-to-all | bytes 524288 | tf_op jit(solution)/shard_map/all_to_all | solution.py:49
  586.9 5.5 fusion.109
  592.4 28.0 %reduce-scatter.21.cloned.1.call-done = f32[16,3584]{1,0:T(8,128)} async-done(((f32[128,3584]{1,0:T(8,128)}), f32[16,3584]{1,0:T(8,128)}) %reduce-scatter.21.cloned.1.call-update) | async-done | bytes 229392 | tf_op jit(solution)/shard_map/reduce_scatter | solution.py:54
  621.9 13.3 %all_to_all.317 = bf16[16,2,1792]{2,1,0:T(2,128)(2,1)S(1)} all-to-all(bf16[16,2,1792]{2,1,0:T(2,128)(2,1)S(1)} %reshape.913), channel_id=1, replica_groups=mesh['gx'=8,'yz'=16] {'yz'}, dimensions={0} | all-to-all | bytes 229376 | tf_op jit(solution)/shard_map/all_to_all | solution.py:60
  635.7 18.4 %all-gather.9 = bf16[16,1,28672]{2,1,0:T(2,128)(2,1)S(1)} all-gather(bf16[1,1,28672]{2,1,0:T(2,128)(2,1)S(1)} %convert_bitcast_fusion), channel_id=1, replica_groups=mesh['gx'=8,'yz'=16] {'yz'}, dimensions={0}, use_global_device_ids=true | all-gather | bytes 974848 | tf_op jit(solution)/shard_map/all_gather | solution.py:48
  654.1 6.5 reduce.25
  660.6 2.2 copy.133
  662.8 13.4 %all-to-all-start.14 = ((bf16[16,8,3584]{2,0,1:T(8,128)(2,1)}), bf16[16,8,3584]{2,0,1:T(8,128)(2,1)S(1)}, u32[]{:S(2)}, u32[]{:S(2)}) async-start(bf16[16,8,3584]{2,0,1:T(8,128)(2,1)} %bitcast.194), calls=%async_computation.21 | async-start | bytes 1835008 | tf_op jit(solution)/shard_map/all_to_all | solution.py:49
  677.2 12.7 %all-to-all-done.14 = bf16[16,8,3584]{2,0,1:T(8,128)(2,1)S(1)} async-done(((bf16[16,8,3584]{2,0,1:T(8,128)(2,1)}), bf16[16,8,3584]{2,0,1:T(8,128)(2,1)S(1)}, u32[]{:S(2)}, u32[]{:S(2)}) %all-to-all-start.14) | async-done | bytes 917536 | tf_op jit(solution)/shard_map/all_to_all | solution.py:49
  689.9 3.4 fusion.110
  693.7 25.7 %reduce-scatter.23.cloned.1.call-done = f32[16,512]{1,0:T(8,128)} async-done(((f32[128,512]{1,0:T(8,128)}), f32[16,512]{1,0:T(8,128)}) %reduce-scatter.23.cloned.1.call-update) | async-done | bytes 32784 | tf_op jit(solution)/shard_map/reduce_scatter | solution.py:54
  721.3 6.8 all-to-all-start.15
  728.8 5.8 all-to-all-done.15
  736.0 16.7 %all-gather.4 = bf16[131072]{0:T(1024)(128)(2,1)S(1)} all-gather(bf16[8192]{0:T(1024)(128)(2,1)S(1)} %get-tuple-element.21), channel_id=6, replica_groups=mesh['gx'=8,'yz'=16] {'yz'}, dimensions={0}, use_global_device_ids=true | all-gather | bytes 278528 | tf_op jit(solution)/shard_map/all_gather | solution.py:48
  753.7 13.0 %all-to-all-start.16 = ((bf16[16,8,1024]{2,0,1:T(8,128)(2,1)}), bf16[16,8,1024]{2,0,1:T(8,128)(2,1)S(1)}, u32[]{:S(2)}, u32[]{:S(2)}) async-start(bf16[16,8,1024]{2,0,1:T(8,128)(2,1)} %copy.89), calls=%async_computation.24 | async-start | bytes 524288 | tf_op jit(solution)/shard_map/all_to_all | solution.py:49
  766.8 17.9 %all-gather.5 = bf16[131072]{0:T(1024)(128)(2,1)S(1)} all-gather(bf16[8192]{0:T(1024)(128)(2,1)S(1)} %get-tuple-element.22), channel_id=7, replica_groups=mesh['gx'=8,'yz'=16] {'yz'}, dimensions={0}, use_global_device_ids=true | all-gather | bytes 278528 | tf_op jit(solution)/shard_map/all_gather | solution.py:48
  785.6 9.7 %all-to-all-start.17 = ((bf16[16,8,1024]{2,0,1:T(8,128)(2,1)}), bf16[16,8,1024]{2,0,1:T(8,128)(2,1)S(1)}, u32[]{:S(2)}, u32[]{:S(2)}) async-start(bf16[16,8,1024]{2,0,1:T(8,128)(2,1)} %copy.90), calls=%async_computation.25 | async-start | bytes 524288 | tf_op jit(solution)/shard_map/all_to_all | solution.py:49
  796.3 5.5 all-to-all-done.17
  803.5 143.1 %all-reduce.5.cloned.1.call-done = (f32[128,512]{1,0:T(8,128)}, f32[128,512]{1,0:T(8,128)}) async-done(((f32[128,512]{1,0:T(8,128)}, f32[128,512]{1,0:T(8,128)}), (f32[128,512]{1,0:T(8,128)}, f32[128,512]{1,0:T(8,128)})) %all-reduce.5.cloned.1.call-update) | async-done | bytes 524304
  947.9 2.1 fusion.82
  953.4 2.0 fusion.85
  (168 shorter events, 54.9 us)
Async XLA Ops:
  7.2 41.5 %copy-start = (bf16[1024,640]{1,0:T(8,128)(2,1)S(1)}, bf16[1024,640]{1,0:T(8,128)(2,1)}, u32[]{:S(2)}) copy-start(bf16[1024,640]{1,0:T(8,128)(2,1)} %param.23) | copy-start | bytes 3932164
  7.2 69.0 %reduce-scatter.9.cloned.1.call-start = ((), (), s32[]{:S(2)}) async-start(), calls=%async_computation.26 | async-start | bytes 368640 | tf_op jit(solution)/shard_map/reduce_scatter | solution.py:54
  78.7 13.2 %all-to-all-start.1 = ((bf16[16,2,320]{2,1,0:T(2,128)(2,1)}), bf16[16,2,320]{2,1,0:T(2,128)(2,1)S(1)}, u32[]{:S(2)}, u32[]{:S(2)}) async-start(bf16[16,2,320]{2,1,0:T(2,128)(2,1)} %reshape.901), calls=%async_computation.2 | async-start | bytes 49152 | tf_op jit(solution)/shard_map/all_to_all | solution.py:60
  85.4 79.2 %reduce-scatter.11.cloned.1.call-start = ((), (), s32[]{:S(2)}) async-start(), calls=%async_computation.27 | async-start | bytes 294912 | tf_op jit(solution)/shard_map/reduce_scatter | solution.py:54
  85.5 8.8 copy-start.15
  85.5 2.4 copy-start.4
  92.0 2.3 copy-start.5
  92.7 0.6 copy-start.11
  92.7 2.2 copy-start.13
  113.7 66.8 %copy-start.3 = (bf16[2,1,8192]{2,0,1:T(2,128)(2,1)S(1)}, bf16[2,1,8192]{2,0,1:T(2,128)(2,1)}, u32[]{:S(2)}) copy-start(bf16[2,1,8192]{2,0,1:T(2,128)(2,1)} %param.15) | copy-start | bytes 98308
  138.9 117.8 %reduce-scatter.13.cloned.1.call-start = ((), (), s32[]{:S(2)}) async-start(), calls=%async_computation.28 | async-start | bytes 2064384 | tf_op jit(solution)/shard_map/reduce_scatter | solution.py:54
  228.7 133.1 %reduce-scatter.15.cloned.1.call-start = ((), (), s32[]{:S(2)}) async-start(), calls=%async_computation.29 | async-start | bytes 294912 | tf_op jit(solution)/shard_map/reduce_scatter | solution.py:54
  308.1 26.6 %copy-start.1 = (bf16[3584,512]{1,0:T(8,128)(2,1)S(1)}, bf16[3584,512]{1,0:T(8,128)(2,1)}, u32[]{:S(2)}) copy-start(bf16[3584,512]{1,0:T(8,128)(2,1)} %param.27) | copy-start | bytes 11010052
  336.1 110.6 %reduce-scatter.17.cloned.1.call-start = ((), (), s32[]{:S(2)}) async-start(), calls=%async_computation.30 | async-start | bytes 368640 | tf_op jit(solution)/shard_map/reduce_scatter | solution.py:54
  379.8 78.6 %copy-start.12 = (bf16[1,8,64]{2,1,0:T(8,128)(2,1)S(1)}, bf16[1,8,64]{2,1,0:T(8,128)(2,1)}, u32[]{:S(2)}) copy-start(bf16[1,8,64]{2,1,0:T(8,128)(2,1)} %copy-done.11) | copy-start | bytes 3076
  379.8 78.6 %copy-start.14 = (bf16[1,8,64]{2,1,0:T(8,128)(2,1)S(1)}, bf16[1,8,64]{2,1,0:T(8,128)(2,1)}, u32[]{:S(2)}) copy-start(bf16[1,8,64]{2,1,0:T(8,128)(2,1)} %copy-done.13) | copy-start | bytes 3076
  398.1 71.4 %copy-start.16 = (pred[1024]{0:T(1024)(128)(4,1)S(1)}, pred[1024]{0:T(1024)(128)(4,1)}, u32[]{:S(2)}) copy-start(pred[1024]{0:T(1024)(128)(4,1)} %copy-done.15) | copy-start | bytes 3076
  421.0 49.7 %copy-start.17 = (bf16[1,1,8,128]{3,1,2,0:T(2,128)(2,1)S(1)}, bf16[1,1,8,128]{3,1,2,0:T(2,128)(2,1)}, u32[]{:S(2)}) copy-start(bf16[1,1,8,128]{3,1,2,0:T(2,128)(2,1)} %get-tuple-element.12) | copy-start | bytes 6148
  451.4 13.4 %all-to-all-start.9 = ((bf16[16,2,320]{2,1,0:T(2,128)(2,1)}), bf16[16,2,320]{2,1,0:T(2,128)(2,1)}, u32[]{:S(2)}, u32[]{:S(2)}) async-start(bf16[16,2,320]{2,1,0:T(2,128)(2,1)} %reshape.909), calls=%async_computation.14 | async-start | bytes 49152 | tf_op jit(solution)/shard_map/all_to_all | solution.py:60
  458.3 77.3 %reduce-scatter.19.cloned.1.call-start = ((), (), s32[]{:S(2)}) async-start(), calls=%async_computation.31 | async-start | bytes 294912 | tf_op jit(solution)/shard_map/reduce_scatter | solution.py:54
  466.3 4.0 copy-start.18
  466.3 4.7 copy-start.6
  470.9 37.9 %copy-start.2 = (bf16[1024,512]{1,0:T(8,128)(2,1)S(1)}, bf16[1024,512]{1,0:T(8,128)(2,1)}, u32[]{:S(2)}) copy-start(bf16[1024,512]{1,0:T(8,128)(2,1)} %param.24) | copy-start | bytes 3145732
  488.5 62.9 %copy-start.8 = (f32[8192]{0:T(1024)S(1)}, f32[8192]{0:T(1024)}, u32[]{:S(2)}) copy-start(f32[8192]{0:T(1024)} %param.25) | copy-start | bytes 98308
  509.8 110.5 %reduce-scatter.21.cloned.1.call-start = ((), (), s32[]{:S(2)}) async-start(), calls=%async_computation.32 | async-start | bytes 2064384 | tf_op jit(solution)/shard_map/reduce_scatter | solution.py:54
  660.6 16.3 %copy-start.19 = (s32[512]{0:T(512)S(1)}, s32[512]{0:T(512)}, u32[]{:S(2)}) copy-start(s32[512]{0:T(512)} %param.20) | copy-start | bytes 6148
  660.6 16.3 %copy-start.20 = (s32[1,16]{1,0:T(1,128)S(1)}, s32[1,16]{1,0:T(1,128)}, u32[]{:S(2)}) copy-start(s32[1,16]{1,0:T(1,128)} %param.19) | copy-start | bytes 196
  662.8 27.0 %all-to-all-start.14 = ((bf16[16,8,3584]{2,0,1:T(8,128)(2,1)}), bf16[16,8,3584]{2,0,1:T(8,128)(2,1)S(1)}, u32[]{:S(2)}, u32[]{:S(2)}) async-start(bf16[16,8,3584]{2,0,1:T(8,128)(2,1)} %bitcast.194), calls=%async_computation.21 | async-start | bytes 1835008 | tf_op jit(solution)/shard_map/all_to_all | solution.py:49
  676.3 43.1 %reduce-scatter.23.cloned.1.call-start = ((), (), s32[]{:S(2)}) async-start(), calls=%async_computation.33 | async-start | bytes 294912 | tf_op jit(solution)/shard_map/reduce_scatter | solution.py:54
  689.9 46.1 %copy-start.9 = (bf16[8192]{0:T(1024)(128)(2,1)S(1)}, bf16[8192]{0:T(1024)(128)(2,1)}, u32[]{:S(2)}) copy-start(bf16[8192]{0:T(1024)(128)(2,1)} %get-tuple-element.11) | copy-start | bytes 49156
  689.9 46.1 %copy-start.10 = (f32[8192]{0:T(1024)S(1)}, f32[8192]{0:T(1024)}, u32[]{:S(2)}) copy-start(f32[8192]{0:T(1024)} %param.28) | copy-start | bytes 98308
  721.3 13.2 %all-to-all-start.15 = ((bf16[16,2,256]{2,1,0:T(2,128)(2,1)}), bf16[16,2,256]{2,1,0:T(2,128)(2,1)S(1)}, u32[]{:S(2)}, u32[]{:S(2)}) async-start(bf16[16,2,256]{2,1,0:T(2,128)(2,1)} %reshape.915), calls=%async_computation.23 | async-start | bytes 32768 | tf_op jit(solution)/shard_map/all_to_all | solution.py:60
  735.3 60.1 %copy-start.7 = (bf16[64,512]{1,0:T(8,128)(2,1)S(1)}, bf16[64,512]{1,0:T(8,128)(2,1)}, u32[]{:S(2)}) copy-start(bf16[64,512]{1,0:T(8,128)(2,1)} %param.29) | copy-start | bytes 196612
  753.7 32.0 %all-to-all-start.16 = ((bf16[16,8,1024]{2,0,1:T(8,128)(2,1)}), bf16[16,8,1024]{2,0,1:T(8,128)(2,1)S(1)}, u32[]{:S(2)}, u32[]{:S(2)}) async-start(bf16[16,8,1024]{2,0,1:T(8,128)(2,1)} %copy.89), calls=%async_computation.24 | async-start | bytes 524288 | tf_op jit(solution)/shard_map/all_to_all | solution.py:49
  785.6 16.2 %all-to-all-start.17 = ((bf16[16,8,1024]{2,0,1:T(8,128)(2,1)}), bf16[16,8,1024]{2,0,1:T(8,128)(2,1)S(1)}, u32[]{:S(2)}, u32[]{:S(2)}) async-start(bf16[16,8,1024]{2,0,1:T(8,128)(2,1)} %copy.90), calls=%async_computation.25 | async-start | bytes 524288 | tf_op jit(solution)/shard_map/all_to_all | solution.py:49
  795.4 151.2 %all-reduce.5.cloned.1.call-start = ((), (), s32[]{:S(2)}) async-start(), calls=%async_computation.34 | async-start | bytes 1048576
Sparse Core Ops, SparseCore 0:
  49.9 26.2 reduce-scatter.8
  139.0 25.6 reduce-scatter.10
  228.8 27.7 reduce-scatter.12
  336.2 25.5 reduce-scatter.14
  421.1 25.5 reduce-scatter.16
  510.0 25.6 reduce-scatter.18
  592.5 27.7 reduce-scatter.20
  693.4 25.8 reduce-scatter.22
  802.9 143.5 all-reduce.4
where the time goes:
time: 968 us; the launch traced here: 965 us
  blocking collectives  386 us (40%)
  waiting for transfers between devices  384 us (40%)
  other arithmetic  61.6 us (6%)
  starting transfers between devices  56.9 us (6%)
  local copies, waits for them, and re-layouts  27.6 us (3%)
  matrix products  27 us (3%)
  between operations  21.2 us (2%)
    reduce_scatter x8, waiting for transfers between devices, project(): lax.psum_scatter(jnp.dot(spread, weight, preferred_element_type=jnp.float...  209 us
    all_gather x10, blocking collectives, spread_rows(): gathered = lax.all_gather(inputs, 'yz', axis=0, tiled=True)  185 us
    unnamed x10, waiting for transfers between devices  143 us
    all_to_all x7, blocking collectives, spread_rows(): lax.all_to_all(gathered, 'gx', split_axis=1, concat_axis=0, tiled=True)  135 us
    all_to_all x5, blocking collectives, project(): lax.all_to_all(summed.astype(jnp.bfloat16), 'yz', split_axis=0, concat_ax...  66.1 us
    all_to_all x3, starting transfers between devices, spread_rows(): lax.all_to_all(gathered, 'gx', split_axis=1, concat_axis=0, tiled=True)  36.2 us
    dot_general x8, matrix products, project(): jnp.dot(spread, weight, preferred_element_type=jnp.float32)  21.2 us
    all_to_all x3, starting transfers between devices, project(): lax.all_to_all(summed.astype(jnp.bfloat16), 'yz', split_axis=0, concat_ax...  20.4 us
  transfers between devices with their start and end apart: 15, of which 14 were waited for; matrix products, arithmetic and copies ran while one was open for 1% of the time, Pallas kernels for 0%

commit v1 on v0

--- a/solution.py
+++ b/solution.py
@@ -78,37 +78,40 @@
 def attend(queries, k_cache, v_cache, lengths, keys_new, values_new):
     groups = HEADS // KV_HEADS
     factor = 1.0 / math.sqrt(HEAD)
-    rows_here = queries.shape[0]
+    steps = queries.shape[0]
     cache_len = k_cache.shape[1]
-    fresh = keys_new.shape[1]
-    query_heads = queries.reshape(rows_here, KV_HEADS, groups, HEAD)
-    kcache_heads = k_cache.reshape(rows_here, cache_len, KV_HEADS, HEAD)
-    vcache_heads = v_cache.reshape(rows_here, cache_len, KV_HEADS, HEAD)
-    knew_heads = keys_new.reshape(rows_here, fresh, KV_HEADS, HEAD)
-    vnew_heads = values_new.reshape(rows_here, fresh, KV_HEADS, HEAD)
+    query_heads = queries.reshape(steps, KV_HEADS, groups, HEAD)
+    kcache_heads = k_cache.reshape(cache_len, KV_HEADS, HEAD)
+    vcache_heads = v_cache.reshape(cache_len, KV_HEADS, HEAD)
+    knew_heads = keys_new.reshape(steps, KV_HEADS, HEAD)
+    vnew_heads = values_new.reshape(steps, KV_HEADS, HEAD)
     scores_cache = (
-        jnp.einsum("rkgd,rlkd->rkgl", query_heads, kcache_heads, preferred_element_type=jnp.float32)
+        jnp.einsum("skgd,lkd->skgl", query_heads, kcache_heads, preferred_element_type=jnp.float32)
         * factor
     )
-    valid = jnp.arange(cache_len)[None, None, None, :] < lengths[:, None, None, None]
+    valid = jnp.arange(cache_len)[None, None, None, :] < lengths[0]
     scores_cache = jnp.where(valid, scores_cache, -jnp.inf)
     scores_new = (
-        jnp.einsum("rkgd,rnkd->rkgn", query_heads, knew_heads, preferred_element_type=jnp.float32)
+        jnp.einsum("skgd,nkd->skgn", query_heads, knew_heads, preferred_element_type=jnp.float32)
         * factor
     )
+    causal = (
+        jnp.arange(steps)[None, None, None, :] <= jnp.arange(steps)[:, None, None, None]
+    )
+    scores_new = jnp.where(causal, scores_new, -jnp.inf)
     largest = jnp.maximum(jnp.max(scores_cache, -1), jnp.max(scores_new, -1))[..., None]
     exp_cache = jnp.where(valid, jnp.exp(scores_cache - largest), 0.0)
-    exp_new = jnp.exp(scores_new - largest)
+    exp_new = jnp.where(causal, jnp.exp(scores_new - largest), 0.0)
     denominator = jnp.sum(exp_cache, -1, keepdims=True) + jnp.sum(exp_new, -1, keepdims=True)
     weights_cache = (exp_cache / denominator).astype(jnp.bfloat16)
     weights_new = (exp_new / denominator).astype(jnp.bfloat16)
     result = jnp.einsum(
-        "rkgl,rlkd->rkgd", weights_cache, vcache_heads, preferred_element_type=jnp.float32
+        "skgl,lkd->skgd", weights_cache, vcache_heads, preferred_element_type=jnp.float32
     )
     result = result + jnp.einsum(
-        "rkgn,rnkd->rkgd", weights_new, vnew_heads, preferred_element_type=jnp.float32
-    )
-    return result.reshape(rows_here, HEADS * HEAD).astype(jnp.bfloat16)
+        "skgn,nkd->skgd", weights_new, vnew_heads, preferred_element_type=jnp.float32
+    )
+    return result.reshape(steps, HEADS * HEAD).astype(jnp.bfloat16)
 
 
 def element_table(token_elem):
@@ -151,45 +154,30 @@
 ):
     q_width = HEADS * HEAD
     kv_width = KV_HEADS * HEAD
-    key_list = []
-    value_list = []
-    result_list = []
-    logit_steps = []
-    for which_step in range(2):
-        positions = lengths + which_step
-        mixed = project(norm_rows(hidden_in[which_step], attn_gain), qkv_weight)
-        queries = rotate(mixed[:, :q_width].reshape(-1, HEADS, HEAD), positions).reshape(
-            -1, q_width
-        )
-        keys_now = rotate(
-            mixed[:, q_width : q_width + kv_width].reshape(-1, KV_HEADS, HEAD), positions
-        ).reshape(-1, kv_width)
-        queries, keys_now, values_now = (queries, keys_now, mixed[:, q_width + kv_width :])
-        key_list.append(keys_now)
-        value_list.append(values_now)
-        attended = attend(
-            queries, k_cache, v_cache, lengths, jnp.stack(key_list, 1), jnp.stack(value_list, 1)
-        )
-        projected = project(attended, o_weight)
-        residual = (
-            hidden_in[which_step].astype(jnp.float32) + projected.astype(jnp.float32)
-        ).astype(jnp.bfloat16)
-        gate_up = project(norm_rows(residual, ffn_gain), gate_up_weight)
-        hidden_units = (
-            jax.nn.silu(gate_up[:, :FF].astype(jnp.float32)) * gate_up[:, FF:].astype(jnp.float32)
-        ).astype(jnp.bfloat16)
-        lowered = project(hidden_units, down_weight)
-        result = (residual.astype(jnp.float32) + lowered.astype(jnp.float32)).astype(jnp.bfloat16)
-        logits = head_logits(norm_rows(result, final_gain), lm_weight)
-        result, logits = (result, logits)
-        result_list.append(result)
-        logit_steps.append(logits)
-    outputs = jnp.stack(result_list)
+    steps = hidden_in.shape[0]
+    layer_in = hidden_in[:, 0, :]
+    positions = lengths[0] + jnp.arange(steps, dtype=jnp.int32)
+    mixed = project(norm_rows(layer_in, attn_gain), qkv_weight)
+    queries = rotate(mixed[:, :q_width].reshape(-1, HEADS, HEAD), positions).reshape(-1, q_width)
+    keys_now = rotate(
+        mixed[:, q_width : q_width + kv_width].reshape(-1, KV_HEADS, HEAD), positions
+    ).reshape(-1, kv_width)
+    values_now = mixed[:, q_width + kv_width :]
+    attended = attend(queries, k_cache[0], v_cache[0], lengths, keys_now, values_now)
+    projected = project(attended, o_weight)
+    residual = (layer_in.astype(jnp.float32) + projected.astype(jnp.float32)).astype(jnp.bfloat16)
+    gate_up = project(norm_rows(residual, ffn_gain), gate_up_weight)
+    hidden_units = (
+        jax.nn.silu(gate_up[:, :FF].astype(jnp.float32)) * gate_up[:, FF:].astype(jnp.float32)
+    ).astype(jnp.bfloat16)
+    lowered = project(hidden_units, down_weight)
+    result = (residual.astype(jnp.float32) + lowered.astype(jnp.float32)).astype(jnp.bfloat16)
+    logits = head_logits(norm_rows(result, final_gain), lm_weight)
     remaining = counts.astype(jnp.float32)
-    first_log = masked_log_probs(logit_steps[0], remaining, token_elem)
+    first_log = masked_log_probs(logits[0:1], remaining, token_elem)
     remaining = remaining - used_elements(tokens, token_elem)
-    second_log = masked_log_probs(logit_steps[1], remaining, token_elem)
-    return (outputs, jnp.stack([first_log, second_log]))
+    second_log = masked_log_probs(logits[1:2], remaining, token_elem)
+    return (result[:, None, :], jnp.stack([first_log, second_log]))
 
 
 def solution(mesh):

time: 968 us -> 594 us (0.61)
  blocking collectives: 386 us -> 191 us
  waiting for transfers between devices: 384 us -> 312 us
  other arithmetic: 61.6 us -> 15.5 us
  starting transfers between devices: 56.9 us -> 27.2 us
  local copies, waits for them, and re-layouts: 27.6 us -> 14.4 us
  matrix products: 27 us -> 15.3 us
    all_gather x10 -> x4, blocking collectives: 185 us -> 71.5 us  [spread_rows(): gathered = lax.all_gather(inputs, 'yz', axis=0, tiled=True)]
    reduce_scatter x8 -> x4, waiting for transfers between devices: 209 us -> 110 us  [project(): lax.psum_scatter(jnp.dot(spread, weight, preferred_element_type=jnp.float...]
    all_to_all x7 -> x4, blocking collectives: 135 us -> 92.2 us  [spread_rows(): lax.all_to_all(gathered, 'gx', split_axis=1, concat_axis=0, tiled=True)]
    all_gather x0 -> x1, waiting for transfers between devices: none -> 42.5 us  [spread_rows(): gathered = lax.all_gather(inputs, 'yz', axis=0, tiled=True)]
    all_to_all x5 -> x2, blocking collectives: 66.1 us -> 27 us  [project(): lax.all_to_all(summed.astype(jnp.bfloat16), 'yz', split_axis=0, concat_ax...]
    all_to_all x3 -> x1, starting transfers between devices: 36.2 us -> 13.3 us  [spread_rows(): lax.all_to_all(gathered, 'gx', split_axis=1, concat_axis=0, tiled=True)]
    all_gather x4 -> x0, other arithmetic: 19.1 us -> none  [spread_rows(): gathered = lax.all_gather(inputs, 'yz', axis=0, tiled=True)]
    all_to_all x16 -> x0, other arithmetic: 15.1 us -> none  [project(): lax.all_to_all(summed.astype(jnp.bfloat16), 'yz', split_axis=0, concat_ax...]
  transfers between devices with their start and end apart: 15 -> 9, of which waited for: 14 -> 9; matrix products, arithmetic and copies ran while one was open for 1% -> 1% of each run, Pallas kernels for 0% -> 0%
where the time goes in v1:
time: 594 us; the launch traced here: 593 us
  waiting for transfers between devices  312 us (53%)
  blocking collectives  191 us (32%)
  starting transfers between devices  27.2 us (5%)
  between operations  17.1 us (3%)
  other arithmetic  15.5 us (3%)
  matrix products  15.3 us (3%)
  local copies, waits for them, and re-layouts  14.4 us (2%)
    unnamed x7, waiting for transfers between devices  143 us
    reduce_scatter x4, waiting for transfers between devices, project(): lax.psum_scatter(jnp.dot(spread, weight, preferred_element_type=jnp.float...  110 us
    all_to_all x4, blocking collectives, spread_rows(): lax.all_to_all(gathered, 'gx', split_axis=1, concat_axis=0, tiled=True)  92.2 us
    all_gather x4, blocking collectives, spread_rows(): gathered = lax.all_gather(inputs, 'yz', axis=0, tiled=True)  71.5 us
    all_gather x1, waiting for transfers between devices, spread_rows(): gathered = lax.all_gather(inputs, 'yz', axis=0, tiled=True)  42.5 us
    all_to_all x2, blocking collectives, project(): lax.all_to_all(summed.astype(jnp.bfloat16), 'yz', split_axis=0, concat_ax...  27 us
    all_to_all x2, starting transfers between devices, project(): lax.all_to_all(summed.astype(jnp.bfloat16), 'yz', split_axis=0, concat_ax...  13.6 us
    all_to_all x1, starting transfers between devices, spread_rows(): lax.all_to_all(gathered, 'gx', split_axis=1, concat_axis=0, tiled=True)  13.3 us
  transfers between devices with their start and end apart: 9, of which 9 were waited for; matrix products, arithmetic and copies ran while one was open for 1% of the time, Pallas kernels for 0%

profile of v1, /device:TPU:1, one launch (start us, length us, event | category | flops | bytes accessed | tf_op | source)
XLA Modules:
  0.0 592.5 jit_solution(9030125574101462868)
XLA Ops:
  7.2 1.0 fusion.39
  8.3 0.9 fusion.57
  9.2 21.1 %all-gather = bf16[16,2,8192]{2,1,0:T(2,128)(2,1)S(1)} all-gather(bf16[1,2,8192]{2,1,0:T(2,128)(2,1)S(1)} %fusion.57), channel_id=1, replica_groups=mesh['gx'=8,'yz'=16] {'yz'}, dimensions={0}, use_global_device_ids=true | all-gather | bytes 557056 | tf_op jit(solution)/shard_map/all_gather | solution.py:48
  30.3 0.4 all_to_all.118
  30.7 0.3 copy.60
  31.0 19.3 %all_to_all.159 = bf16[32,8,1024]{2,0,1:T(8,128)(2,1)S(1)} all-to-all(bf16[32,8,1024]{2,0,1:T(8,128)(2,1)S(1)} %copy.60), channel_id=1, replica_groups=mesh['gx'=8,'yz'=16] {'gx'}, dimensions={1} | all-to-all | bytes 1048576 | tf_op jit(solution)/shard_map/all_to_all | solution.py:49
  50.3 1.4 fusion.81
  52.4 0.1 multiply_cosine_fusion
  52.5 26.1 %reduce-scatter.5.cloned.1.call-done = f32[32,640]{1,0:T(8,128)} async-done(((f32[256,640]{1,0:T(8,128)}), f32[32,640]{1,0:T(8,128)}) %reduce-scatter.5.cloned.1.call-update) | async-done | bytes 81936 | tf_op jit(solution)/shard_map/reduce_scatter | solution.py:54
  78.6 0.9 convert_element_type.152
  79.5 0.6 all_to_all.122
  80.2 6.8 %all-to-all-start.1 = ((bf16[16,2,640]{2,1,0:T(2,128)(2,1)}), bf16[16,2,640]{2,1,0:T(2,128)(2,1)S(1)}, u32[]{:S(2)}, u32[]{:S(2)}) async-start(bf16[16,2,640]{2,1,0:T(2,128)(2,1)} %all_to_all.122), calls=%async_computation.2 | async-start | bytes 81920 | tf_op jit(solution)/shard_map/all_to_all | solution.py:60
  87.0 2.4 copy.80
  89.4 2.0 copy.81
  91.4 2.0 all-to-all-done.1
  93.7 0.8 fusion.79
  94.5 0.4 fusion.80
  94.9 0.2 fusion.22
  95.2 0.7 fusion.14
  95.9 0.3 fusion.17
  96.2 16.8 %all-gather.1 = bf16[16,2,8192]{2,1,0:T(2,128)(2,1)S(1)} all-gather(bf16[1,2,8192]{2,1,0:T(2,128)(2,1)S(1)} %reshape.246), channel_id=1, replica_groups=mesh['gx'=8,'yz'=16] {'yz'}, dimensions={0}, use_global_device_ids=true | all-gather | bytes 557056 | tf_op jit(solution)/shard_map/all_gather | solution.py:48
  113.1 0.4 all_to_all.126
  113.5 0.3 copy.66
  113.8 21.6 %all_to_all.160 = bf16[32,8,1024]{2,0,1:T(8,128)(2,1)S(1)} all-to-all(bf16[32,8,1024]{2,0,1:T(8,128)(2,1)S(1)} %copy.66), channel_id=1, replica_groups=mesh['gx'=8,'yz'=16] {'gx'}, dimensions={1} | all-to-all | bytes 1048576 | tf_op jit(solution)/shard_map/all_to_all | solution.py:49
  135.4 1.2 fusion.82
  136.7 25.9 %reduce-scatter.7.cloned.1.call-done = f32[32,512]{1,0:T(8,128)} async-done(((f32[256,512]{1,0:T(8,128)}), f32[32,512]{1,0:T(8,128)}) %reduce-scatter.7.cloned.1.call-update) | async-done | bytes 65552 | tf_op jit(solution)/shard_map/reduce_scatter | solution.py:54
  162.6 0.8 convert_element_type.162
  163.5 13.0 %all_to_all.161 = bf16[16,2,512]{2,1,0:T(2,128)(2,1)S(1)} all-to-all(bf16[16,2,512]{2,1,0:T(2,128)(2,1)S(1)} %all_to_all.130), channel_id=1, replica_groups=mesh['gx'=8,'yz'=16] {'yz'}, dimensions={0} | all-to-all | bytes 65536 | tf_op jit(solution)/shard_map/all_to_all | solution.py:60
  176.6 0.2 fusion.47
  176.9 16.8 %all-gather.2 = bf16[16,2,8192]{2,1,0:T(2,128)(2,1)S(1)} all-gather(bf16[1,2,8192]{2,1,0:T(2,128)(2,1)S(1)} %fusion.55), channel_id=1, replica_groups=mesh['gx'=8,'yz'=16] {'yz'}, dimensions={0}, use_global_device_ids=true | all-gather | bytes 557056 | tf_op jit(solution)/shard_map/all_gather | solution.py:48
  193.7 0.4 all_to_all.132
  194.1 0.3 copy.67
  194.4 21.6 %all_to_all.162 = bf16[32,8,1024]{2,0,1:T(8,128)(2,1)S(1)} all-to-all(bf16[32,8,1024]{2,0,1:T(8,128)(2,1)S(1)} %copy.67), channel_id=1, replica_groups=mesh['gx'=8,'yz'=16] {'gx'}, dimensions={1} | all-to-all | bytes 1048576 | tf_op jit(solution)/shard_map/all_to_all | solution.py:49
  216.0 7.0 %fusion.83 = f32[256,3584]{1,0:T(8,128)} fusion(bf16[256,1024]{1,0:T(8,128)(2,1)S(1)} %bitcast.158, bf16[1024,3584]{1,0:T(8,128)(2,1)} %param.26), kind=kOutput, calls=%fused_computation.123 | convolution fusion | flops 1879048192 | bytes 11534336 | tf_op jit(solution)/shard_map/dot_general | solution.py:55
  223.0 31.3 %reduce-scatter.9.cloned.1.call-done = f32[32,3584]{1,0:T(8,128)} async-done(((f32[256,3584]{1,0:T(8,128)}), f32[32,3584]{1,0:T(8,128)}) %reduce-scatter.9.cloned.1.call-update) | async-done | bytes 458768 | tf_op jit(solution)/shard_map/reduce_scatter | solution.py:54
  254.3 1.0 convert_element_type.173
  255.4 14.0 %all_to_all.163 = bf16[16,2,3584]{2,1,0:T(2,128)(2,1)S(1)} all-to-all(bf16[16,2,3584]{2,1,0:T(2,128)(2,1)S(1)} %all_to_all.136), channel_id=1, replica_groups=mesh['gx'=8,'yz'=16] {'yz'}, dimensions={0} | all-to-all | bytes 458752 | tf_op jit(solution)/shard_map/all_to_all | solution.py:60
  269.4 0.9 fusion.35
  270.3 0.2 reduce-scatter.11.cloned.1.call-start
  270.6 42.5 %all-gather.7.cloned.1.call-done = bf16[16,2,28672]{2,1,0:T(2,128)(2,1)} async-done(((bf16[1,2,28672]{2,1,0:T(2,128)(2,1)}), bf16[16,2,28672]{2,1,0:T(2,128)(2,1)}) %all-gather.7.cloned.1.call-update) | async-done | bytes 1835024 | tf_op jit(solution)/shard_map/all_gather | solution.py:48
  313.0 4.5 all_to_all.140
  317.6 0.5 copy.68
  318.1 29.7 %all_to_all.164 = bf16[32,8,3584]{2,0,1:T(8,128)(2,1)S(1)} all-to-all(bf16[32,8,3584]{2,0,1:T(8,128)(2,1)S(1)} %copy.68), channel_id=1, replica_groups=mesh['gx'=8,'yz'=16] {'gx'}, dimensions={1} | all-to-all | bytes 3670016 | tf_op jit(solution)/shard_map/all_to_all | solution.py:49
  347.8 1.9 fusion.84
  349.8 0.2 fusion.23
  350.0 26.3 %reduce-scatter.11.cloned.1.call-done = f32[32,512]{1,0:T(8,128)} async-done(((f32[256,512]{1,0:T(8,128)}), f32[32,512]{1,0:T(8,128)}) %reduce-scatter.11.cloned.1.call-update) | async-done | bytes 65552 | tf_op jit(solution)/shard_map/reduce_scatter | solution.py:54
  376.4 0.8 convert_element_type.177
  377.2 0.6 all_to_all.144
  377.9 6.8 %all-to-all-start.7 = ((bf16[16,2,512]{2,1,0:T(2,128)(2,1)}), bf16[16,2,512]{2,1,0:T(2,128)(2,1)S(1)}, u32[]{:S(2)}, u32[]{:S(2)}) async-start(bf16[16,2,512]{2,1,0:T(2,128)(2,1)} %all_to_all.144), calls=%async_computation.11 | async-start | bytes 65536 | tf_op jit(solution)/shard_map/all_to_all | solution.py:60
  385.3 5.8 all-to-all-done.7
  391.2 0.2 fusion.44
  391.5 16.8 %all-gather.4 = bf16[16,2,8192]{2,1,0:T(2,128)(2,1)S(1)} all-gather(bf16[1,2,8192]{2,1,0:T(2,128)(2,1)S(1)} %fusion.56), channel_id=1, replica_groups=mesh['gx'=8,'yz'=16] {'yz'}, dimensions={0}, use_global_device_ids=true | all-gather | bytes 557056 | tf_op jit(solution)/shard_map/all_gather | solution.py:48
  408.3 0.4 all_to_all.146
  408.7 1.1 copy.69
  409.7 13.3 %all-to-all-start.8 = ((bf16[32,8,1024]{2,0,1:T(8,128)(2,1)}), bf16[32,8,1024]{2,0,1:T(8,128)(2,1)S(1)}, u32[]{:S(2)}, u32[]{:S(2)}) async-start(bf16[32,8,1024]{2,0,1:T(8,128)(2,1)} %copy.69), calls=%async_computation.12 | async-start | bytes 1048576 | tf_op jit(solution)/shard_map/all_to_all | solution.py:49
  423.0 0.4 fusion.21
  423.4 9.0 %all-to-all-done.8 = bf16[32,8,1024]{2,0,1:T(8,128)(2,1)S(1)} async-done(((bf16[32,8,1024]{2,0,1:T(8,128)(2,1)}), bf16[32,8,1024]{2,0,1:T(8,128)(2,1)S(1)}, u32[]{:S(2)}, u32[]{:S(2)}) %all-to-all-start.8) | async-done | bytes 524320 | tf_op jit(solution)/shard_map/all_to_all | solution.py:49
  432.4 1.1 fusion.51
  433.5 0.7 add_convert_fusion
  434.2 143.2 %all-reduce.3.cloned.1.call-done = f32[256,512]{1,0:T(8,128)} async-done(((f32[256,512]{1,0:T(8,128)}), f32[256,512]{1,0:T(8,128)}) %all-reduce.3.cloned.1.call-update) | async-done | bytes 524304
  577.4 1.5 fusion.64
  578.8 2.8 fusion.65
  583.0 2.1 fusion.66
  585.1 0.6 pad_maximum_fusion.1
  (60 shorter events, 1.2 us)
Async XLA Ops:
  7.2 43.1 %copy-start = (bf16[1024,640]{1,0:T(8,128)(2,1)S(1)}, bf16[1024,640]{1,0:T(8,128)(2,1)}, u32[]{:S(2)}) copy-start(bf16[1024,640]{1,0:T(8,128)(2,1)} %param.23) | copy-start | bytes 3932164
  7.2 71.4 %reduce-scatter.5.cloned.1.call-start = ((), (), s32[]{:S(2)}) async-start(), calls=%async_computation.13 | async-start | bytes 737280 | tf_op jit(solution)/shard_map/reduce_scatter | solution.py:54
  80.2 13.3 %all-to-all-start.1 = ((bf16[16,2,640]{2,1,0:T(2,128)(2,1)}), bf16[16,2,640]{2,1,0:T(2,128)(2,1)S(1)}, u32[]{:S(2)}, u32[]{:S(2)}) async-start(bf16[16,2,640]{2,1,0:T(2,128)(2,1)} %all_to_all.122), calls=%async_computation.2 | async-start | bytes 81920 | tf_op jit(solution)/shard_map/all_to_all | solution.py:60
  87.0 75.7 %reduce-scatter.7.cloned.1.call-start = ((), (), s32[]{:S(2)}) async-start(), calls=%async_computation.14 | async-start | bytes 589824 | tf_op jit(solution)/shard_map/reduce_scatter | solution.py:54
  87.0 2.4 copy-start.1
  93.7 1.6 copy-start.2
  95.9 39.4 %copy-start.3 = (bf16[1024,512]{1,0:T(8,128)(2,1)S(1)}, bf16[1024,512]{1,0:T(8,128)(2,1)}, u32[]{:S(2)}) copy-start(bf16[1024,512]{1,0:T(8,128)(2,1)} %param.24) | copy-start | bytes 3145732
  113.8 62.8 %copy-start.4 = (bf16[2,1,8192]{2,0,1:T(2,128)(2,1)S(1)}, bf16[2,1,8192]{2,0,1:T(2,128)(2,1)}, u32[]{:S(2)}) copy-start(bf16[2,1,8192]{2,0,1:T(2,128)(2,1)} %param.15) | copy-start | bytes 98308
  113.8 63.0 %copy-start.6 = (f32[8192]{0:T(1024)S(1)}, f32[8192]{0:T(1024)}, u32[]{:S(2)}) copy-start(f32[8192]{0:T(1024)} %param.25) | copy-start | bytes 98308
  136.6 117.6 %reduce-scatter.9.cloned.1.call-start = ((), (), s32[]{:S(2)}) async-start(), calls=%async_computation.15 | async-start | bytes 4128768 | tf_op jit(solution)/shard_map/reduce_scatter | solution.py:54
  223.0 90.1 %all-gather.7.cloned.1.call-start = ((), (), s32[]{:S(2)}) async-start(), calls=%async_computation.17 | async-start | bytes 1949696 | tf_op jit(solution)/shard_map/all_gather | solution.py:48
  270.3 106.1 %reduce-scatter.11.cloned.1.call-start = ((), (), s32[]{:S(2)}) async-start(), calls=%async_computation.16 | async-start | bytes 589824 | tf_op jit(solution)/shard_map/reduce_scatter | solution.py:54
  318.1 29.7 %copy-start.9 = (bf16[3584,512]{1,0:T(8,128)(2,1)S(1)}, bf16[3584,512]{1,0:T(8,128)(2,1)}, u32[]{:S(2)}) copy-start(bf16[3584,512]{1,0:T(8,128)(2,1)} %param.27) | copy-start | bytes 11010052
  347.8 1.9 copy-start.8
  347.8 2.0 copy-start.10
  347.8 43.5 %copy-start.7 = (f32[8192]{0:T(1024)S(1)}, f32[8192]{0:T(1024)}, u32[]{:S(2)}) copy-start(f32[8192]{0:T(1024)} %param.28) | copy-start | bytes 98308
  377.9 13.3 %all-to-all-start.7 = ((bf16[16,2,512]{2,1,0:T(2,128)(2,1)}), bf16[16,2,512]{2,1,0:T(2,128)(2,1)S(1)}, u32[]{:S(2)}, u32[]{:S(2)}) async-start(bf16[16,2,512]{2,1,0:T(2,128)(2,1)} %all_to_all.144), calls=%async_computation.11 | async-start | bytes 65536 | tf_op jit(solution)/shard_map/all_to_all | solution.py:60
  391.1 41.2 %copy-start.5 = (bf16[64,512]{1,0:T(8,128)(2,1)S(1)}, bf16[64,512]{1,0:T(8,128)(2,1)}, u32[]{:S(2)}) copy-start(bf16[64,512]{1,0:T(8,128)(2,1)} %param.29) | copy-start | bytes 196612
  409.7 22.6 %all-to-all-start.8 = ((bf16[32,8,1024]{2,0,1:T(8,128)(2,1)}), bf16[32,8,1024]{2,0,1:T(8,128)(2,1)S(1)}, u32[]{:S(2)}, u32[]{:S(2)}) async-start(bf16[32,8,1024]{2,0,1:T(8,128)(2,1)} %copy.69), calls=%async_computation.12 | async-start | bytes 1048576 | tf_op jit(solution)/shard_map/all_to_all | solution.py:49
  423.0 154.4 %all-reduce.3.cloned.1.call-start = ((), (), s32[]{:S(2)}) async-start(), calls=%async_computation.18 | async-start | bytes 1048576
Sparse Core Ops, SparseCore 0:
  51.9 26.7 reduce-scatter.4
  136.8 25.8 reduce-scatter.6
  223.1 31.1 reduce-scatter.8
  270.5 42.5 all-gather.6
  349.9 26.4 reduce-scatter.10
  433.6 143.6 all-reduce.2

commit v2 on v1

--- a/solution.py
+++ b/solution.py
@@ -44,35 +44,39 @@
     return joined.astype(jnp.bfloat16)
 
 
-def spread_rows(inputs):
-    gathered = lax.all_gather(inputs, "yz", axis=0, tiled=True)
-    return lax.all_to_all(gathered, "gx", split_axis=1, concat_axis=0, tiled=True)
+ALL = ("gx", "yz")
+
+
+def spread_rows(inputs, groups):
+    rows_here, width = inputs.shape
+    block = width // groups
+    blocks = inputs.reshape(rows_here, groups, block).transpose(1, 0, 2)
+    devices = lax.psum(1, ALL)
+    send = jnp.broadcast_to(
+        blocks[:, None], (groups, devices // groups, rows_here, block)
+    ).reshape(devices, rows_here, block)
+    got = lax.all_to_all(send, ALL, 0, 0, tiled=True)
+    return got.reshape(devices * rows_here, block)
+
+
+def gather_rows(partial, groups):
+    rows, width = partial.shape
+    devices = lax.psum(1, ALL)
+    rows_here = rows // devices
+    got = lax.all_to_all(partial.reshape(devices, rows_here, width), ALL, 0, 0, tiled=True)
+    summed = jnp.sum(got.reshape(groups, devices // groups, rows_here, width), axis=0)
+    return summed.transpose(1, 0, 2).reshape(rows_here, (devices // groups) * width)
 
 
 def project(inputs, weight):
-    spread = spread_rows(inputs)
-    summed = lax.psum_scatter(
-        jnp.dot(spread, weight, preferred_element_type=jnp.float32),
-        "gx",
-        scatter_dimension=0,
-        tiled=True,
-    )
-    return lax.all_to_all(
-        summed.astype(jnp.bfloat16), "yz", split_axis=0, concat_axis=1, tiled=True
-    )
-
-
-def head_logits(normed, lm_weight):
-    slice_width = lm_weight.shape[0]
-    offset_cols = lax.axis_index("yz") * slice_width
-    spread = spread_rows(normed)
-    own_cols = lax.dynamic_slice_in_dim(spread, offset_cols, slice_width, 1)
-    return lax.psum_scatter(
-        jnp.dot(own_cols, lm_weight, preferred_element_type=jnp.float32),
-        ("gx", "yz"),
-        scatter_dimension=0,
-        tiled=True,
-    )
+    groups = lax.psum(1, "gx")
+    spread = spread_rows(inputs, groups)
+    partial = jnp.dot(spread, weight, preferred_element_type=jnp.float32)
+    return gather_rows(partial, groups).astype(jnp.bfloat16)
+
+
+def head_logits(normed, lm_full):
+    return jnp.dot(normed, lm_full, preferred_element_type=jnp.float32)
 
 
 def attend(queries, k_cache, v_cache, lengths, keys_new, values_new):
@@ -155,6 +159,7 @@
     q_width = HEADS * HEAD
     kv_width = KV_HEADS * HEAD
     steps = hidden_in.shape[0]
+    lm_full = lax.all_gather(lm_weight, ALL, axis=0, tiled=True)
     layer_in = hidden_in[:, 0, :]
     positions = lengths[0] + jnp.arange(steps, dtype=jnp.int32)
     mixed = project(norm_rows(layer_in, attn_gain), qkv_weight)
@@ -172,7 +177,7 @@
     ).astype(jnp.bfloat16)
     lowered = project(hidden_units, down_weight)
     result = (residual.astype(jnp.float32) + lowered.astype(jnp.float32)).astype(jnp.bfloat16)
-    logits = head_logits(norm_rows(result, final_gain), lm_weight)
+    logits = head_logits(norm_rows(result, final_gain), lm_full)
     remaining = counts.astype(jnp.float32)
     first_log = masked_log_probs(logits[0:1], remaining, token_elem)
     remaining = remaining - used_elements(tokens, token_elem)

time: 594 us -> 261 us (0.44)
  waiting for transfers between devices: 312 us -> 77.4 us
  blocking collectives: 191 us -> 86.8 us
    unnamed x7 -> x1, waiting for transfers between devices: 143 us -> 0.68 us
    reduce_scatter x4 -> x0, waiting for transfers between devices: 110 us -> none  [project(): lax.psum_scatter(jnp.dot(spread, weight, preferred_element_type=jnp.float...]
    all_gather x4 -> x0, blocking collectives: 71.5 us -> none  [spread_rows(): gathered = lax.all_gather(inputs, 'yz', axis=0, tiled=True)]
    all_to_all x3 -> x5, waiting for transfers between devices: 16.8 us -> 76.7 us  [the longest x3 42.3 us: gather_rows(): lax.all_to_all(partial.reshape(devices, rows_here, width), ALL, 0, 0, til...]
    all_gather x1, waiting for transfers between devices: 42.5 us -> 0.01 us  [per_device(): lm_full = lax.all_gather(lm_weight, ALL, axis=0, tiled=True)]
    all_to_all x6 -> x3, blocking collectives: 119 us -> 86.8 us  [the longest x1 50.8 us: gather_rows(): lax.all_to_all(partial.reshape(devices, rows_here, width), ALL, 0, 0, til...]
    all_to_all x14 -> x0, local copies, waits for them, and re-layouts: 9.96 us -> none  [the longest x10 8.58 us: spread_rows(): lax.all_to_all(gathered, 'gx', split_axis=1, concat_axis=0, tiled=True)]
    dot_general x0 -> x4, local copies, waits for them, and re-layouts: none -> 6.7 us  [project(): partial = jnp.dot(spread, weight, preferred_element_type=jnp.float32)]
  transfers between devices with their start and end apart: 9 -> 6, of which waited for: 9 -> 5; matrix products, arithmetic and copies ran while one was open for 1% -> 10% of each run, Pallas kernels for 0% -> 0%
where the time goes in v2:
time: 261 us; the launch traced here: 260 us
  blocking collectives  86.8 us (33%)
  waiting for transfers between devices  77.4 us (30%)
  starting transfers between devices  31.2 us (12%)
  matrix products  17.7 us (7%)
  between operations  17 us (7%)
  local copies, waits for them, and re-layouts  15.9 us (6%)
  other arithmetic  13.8 us (5%)
    all_to_all x1, blocking collectives, gather_rows(): lax.all_to_all(partial.reshape(devices, rows_here, width), ALL, 0, 0, til...  50.8 us
    all_to_all x3, waiting for transfers between devices, gather_rows(): lax.all_to_all(partial.reshape(devices, rows_here, width), ALL, 0, 0, til...  42.3 us
    all_to_all x2, blocking collectives, spread_rows(): got = lax.all_to_all(send, ALL, 0, 0, tiled=True)  36 us
    all_to_all x2, waiting for transfers between devices, spread_rows(): got = lax.all_to_all(send, ALL, 0, 0, tiled=True)  34.4 us
    all_to_all x2, starting transfers between devices, spread_rows(): got = lax.all_to_all(send, ALL, 0, 0, tiled=True)  17.3 us
    all_to_all x3, starting transfers between devices, gather_rows(): lax.all_to_all(partial.reshape(devices, rows_here, width), ALL, 0, 0, til...  13.9 us
    dot_general x4, matrix products, project(): partial = jnp.dot(spread, weight, preferred_element_type=jnp.float32)  10.4 us
    dot_general x4, local copies, waits for them, and re-layouts, project(): partial = jnp.dot(spread, weight, preferred_element_type=jnp.float32)  6.7 us
  transfers between devices with their start and end apart: 6, of which 5 were waited for; matrix products, arithmetic and copies ran while one was open for 10% of the time, Pallas kernels for 0%

profile of v2, /device:TPU:1, one launch (start us, length us, event | category | flops | bytes accessed | tf_op | source)
XLA Modules:
  0.0 259.8 jit_solution(5340417025211532013)
XLA Ops:
  7.2 0.0 copy-start
  7.2 1.0 fusion.55
  8.2 0.8 convert.42
  9.0 0.8 mul.177
  9.8 0.1 fusion.62
  9.9 1.1 broadcast_in_dim.61
  11.0 11.9 %all-to-all-start = ((bf16[128,2,1024]{2,1,0:T(2,128)(2,1)}), bf16[128,2,1024]{2,1,0:T(2,128)(2,1)}, u32[]{:S(2)}, u32[]{:S(2)}) async-start(bf16[128,2,1024]{2,1,0:T(2,128)(2,1)} %bitcast.3), calls=%async_computation | async-start | bytes 1048576 | tf_op jit(solution)/shard_map/all_to_all | solution.py:58
  23.6 0.0 copy-start.1
  23.6 2.4 copy.79
  26.0 0.0 copy-done.1
  26.0 2.0 copy.80
  28.0 8.7 %all-to-all-done = bf16[128,2,1024]{2,1,0:T(2,128)(2,1)} async-done(((bf16[128,2,1024]{2,1,0:T(2,128)(2,1)}), bf16[128,2,1024]{2,1,0:T(2,128)(2,1)}, u32[]{:S(2)}, u32[]{:S(2)}) %all-to-all-start) | async-done | bytes 524320 | tf_op jit(solution)/shard_map/all_to_all | solution.py:58
  36.7 1.6 fusion.9
  38.3 1.4 copy.55
  39.7 5.0 %all-to-all-start.1 = ((f32[128,2,640]{2,1,0:T(2,128)}), f32[128,2,640]{2,1,0:T(2,128)}, u32[]{:S(2)}, u32[]{:S(2)}) async-start(f32[128,2,640]{2,1,0:T(2,128)} %copy.55), calls=%async_computation.1 | async-start | bytes 1310720 | tf_op jit(solution)/shard_map/all_to_all | solution.py:66
  44.7 0.1 multiply_cosine_fusion
  44.8 15.1 %all-to-all-done.1 = f32[128,2,640]{2,1,0:T(2,128)} async-done(((f32[128,2,640]{2,1,0:T(2,128)}), f32[128,2,640]{2,1,0:T(2,128)}, u32[]{:S(2)}, u32[]{:S(2)}) %all-to-all-start.1) | async-done | bytes 655392 | tf_op jit(solution)/shard_map/all_to_all | solution.py:66
  59.9 1.3 reduce_sum.100
  61.3 0.1 fusion.59
  61.4 0.1 subtract_convert_fusion.1
  61.5 0.8 fusion.86
  62.2 0.4 fusion.87
  62.6 0.1 fusion.79
  62.7 0.2 fusion.34
  63.0 0.1 copy-done.2
  63.0 0.7 fusion.21
  63.7 0.3 fusion.24
  64.0 0.3 broadcast_in_dim.67
  64.3 17.8 %all_to_all.40 = bf16[128,2,1024]{2,1,0:T(2,128)(2,1)S(1)} all-to-all(bf16[128,2,1024]{2,1,0:T(2,128)(2,1)S(1)} %bitcast.160), channel_id=1, replica_groups=mesh['gx'=8,'yz'=16] {'gx','yz'}, dimensions={0} | all-to-all | bytes 1048576 | tf_op jit(solution)/shard_map/all_to_all | solution.py:58
  82.1 0.4 fusion.29
  82.6 0.0 copy-start.4
  82.6 1.3 copy.61
  83.8 4.0 %all-to-all-start.3 = ((f32[128,2,512]{2,1,0:T(2,128)}), f32[128,2,512]{2,1,0:T(2,128)S(1)}, u32[]{:S(2)}, u32[]{:S(2)}) async-start(f32[128,2,512]{2,1,0:T(2,128)} %copy.61), calls=%async_computation.3 | async-start | bytes 1048576 | tf_op jit(solution)/shard_map/all_to_all | solution.py:66
  87.8 0.0 all-gather.2.cloned.1.call-start
  87.9 0.7 all-gather.2.cloned.1.call-update
  88.6 13.4 %all-to-all-done.3 = f32[128,2,512]{2,1,0:T(2,128)S(1)} async-done(((f32[128,2,512]{2,1,0:T(2,128)}), f32[128,2,512]{2,1,0:T(2,128)S(1)}, u32[]{:S(2)}, u32[]{:S(2)}) %all-to-all-start.3) | async-done | bytes 524320 | tf_op jit(solution)/shard_map/all_to_all | solution.py:66
  102.0 0.2 reduce_sum.103
  102.3 0.2 fusion.47
  102.5 0.1 fusion.61
  102.7 0.3 broadcast_in_dim.68
  102.9 18.2 %all_to_all.41 = bf16[128,2,1024]{2,1,0:T(2,128)(2,1)S(1)} all-to-all(bf16[128,2,1024]{2,1,0:T(2,128)(2,1)S(1)} %bitcast.161), channel_id=1, replica_groups=mesh['gx'=8,'yz'=16] {'gx','yz'}, dimensions={0} | all-to-all | bytes 1048576 | tf_op jit(solution)/shard_map/all_to_all | solution.py:58
  121.1 5.1 %fusion = f32[128,2,3584]{2,0,1:T(8,128)S(1)} fusion(bf16[1024,3584]{1,0:T(8,128)(2,1)} %param.26, bf16[128,2,1024]{2,1,0:T(2,128)(2,1)S(1)} %all_to_all.41), kind=kOutput, calls=%fused_computation | convolution fusion | flops 1879048192 | bytes 11534336 | tf_op jit(solution)/shard_map/dot_general | solution.py:74
  126.3 2.8 %copy.65 = f32[128,2,3584]{2,1,0:T(2,128)S(1)} copy(f32[128,2,3584]{2,0,1:T(8,128)S(1)} %fusion) | data formatting | bytes 7340032 | tf_op jit(solution)/shard_map/dot_general | solution.py:74
  129.1 50.8 %all_to_all.42 = f32[128,2,3584]{2,1,0:T(2,128)} all-to-all(f32[128,2,3584]{2,1,0:T(2,128)S(1)} %copy.65), channel_id=1, replica_groups=mesh['gx'=8,'yz'=16] {'gx','yz'}, dimensions={0} | all-to-all | bytes 7340032 | tf_op jit(solution)/shard_map/all_to_all | solution.py:66
  179.9 3.4 %reduce_sum.105 = bf16[16,2,3584]{2,1,0:T(2,128)(2,1)S(1)} reduce(f32[8,16,2,3584]{3,2,1,0:T(2,128)} %bitcast.154, f32[]{:T(128)} %constant.10.clone.1), dimensions={0}, to_apply=%region_8.9 | reduce | flops 802816 | bytes 3899396 | tf_op jit(solution)/shard_map/reduce_sum | solution.py:67
  183.3 0.3 fusion.43
  183.6 2.3 broadcast_in_dim.120
  185.8 5.3 %all-to-all-start.6 = ((bf16[128,2,3584]{2,1,0:T(2,128)(2,1)}), bf16[128,2,3584]{2,1,0:T(2,128)(2,1)S(1)}, u32[]{:S(2)}, u32[]{:S(2)}) async-start(bf16[128,2,3584]{2,1,0:T(2,128)(2,1)} %bitcast.40), calls=%async_computation.6 | async-start | bytes 3670016 | tf_op jit(solution)/shard_map/all_to_all | solution.py:58
  191.8 0.2 fusion.35
  192.1 25.7 %all-to-all-done.6 = bf16[128,2,3584]{2,1,0:T(2,128)(2,1)S(1)} async-done(((bf16[128,2,3584]{2,1,0:T(2,128)(2,1)}), bf16[128,2,3584]{2,1,0:T(2,128)(2,1)S(1)}, u32[]{:S(2)}, u32[]{:S(2)}) %all-to-all-start.6) | async-done | bytes 1835040 | tf_op jit(solution)/shard_map/all_to_all | solution.py:58
  217.8 3.1 %fusion.2 = f32[128,2,512]{2,0,1:T(8,128)S(1)} fusion(bf16[3584,512]{1,0:T(8,128)(2,1)} %param.27, bf16[128,2,3584]{2,1,0:T(2,128)(2,1)S(1)} %all-to-all-done.6), kind=kOutput, calls=%fused_computation.2 | convolution fusion | flops 939524096 | bytes 6029312 | tf_op jit(solution)/shard_map/dot_general | solution.py:74
  221.0 0.0 copy-start.5
  221.0 1.3 copy.67
  222.2 4.9 %all-to-all-start.7 = ((f32[128,2,512]{2,1,0:T(2,128)}), f32[128,2,512]{2,1,0:T(2,128)S(1)}, u32[]{:S(2)}, u32[]{:S(2)}) async-start(f32[128,2,512]{2,1,0:T(2,128)} %copy.67), calls=%async_computation.7 | async-start | bytes 1048576 | tf_op jit(solution)/shard_map/all_to_all | solution.py:66
  227.2 0.4 fusion.28
  227.6 13.8 %all-to-all-done.7 = f32[128,2,512]{2,1,0:T(2,128)S(1)} async-done(((f32[128,2,512]{2,1,0:T(2,128)}), f32[128,2,512]{2,1,0:T(2,128)S(1)}, u32[]{:S(2)}, u32[]{:S(2)}) %all-to-all-start.7) | async-done | bytes 524320 | tf_op jit(solution)/shard_map/all_to_all | solution.py:66
  241.4 0.2 reduce_sum.106
  241.6 0.2 fusion.49
  241.8 0.7 add_convert_fusion
  242.5 4.6 %fusion.57 = f32[2,512]{1,0:T(2,128)S(1)} fusion(bf16[8192,512]{1,0:T(8,128)(2,1)} %all-gather.2.cloned.1.call-done, bf16[2,8192]{1,0:T(2,128)(2,1)S(1)} %get-tuple-element.7, f32[2]{0:T(128)S(1)} %add_rsqrt_fusion, f32[8192]{0:T(1024)S(1)} %copy-done.5), kind=kOutput, calls=%fused_computation.71 | convolution fusion | flops 16842752 | bytes 8458248 | tf_op jit(solution)/shard_map/dot_general | solution.py:79
  247.1 0.7 fusion.70
  247.8 2.0 fusion.71
  251.0 1.3 fusion.72
  252.4 0.6 pad_maximum_fusion.1
  (37 shorter events, 0.4 us)
Async XLA Ops:
  7.2 29.5 %copy-start = (bf16[1024,640]{1,0:T(8,128)(2,1)S(1)}, bf16[1024,640]{1,0:T(8,128)(2,1)}, u32[]{:S(2)}) copy-start(bf16[1024,640]{1,0:T(8,128)(2,1)} %param.23) | copy-start | bytes 3932164
  11.0 25.7 %all-to-all-start = ((bf16[128,2,1024]{2,1,0:T(2,128)(2,1)}), bf16[128,2,1024]{2,1,0:T(2,128)(2,1)}, u32[]{:S(2)}, u32[]{:S(2)}) async-start(bf16[128,2,1024]{2,1,0:T(2,128)(2,1)} %bitcast.3), calls=%async_computation | async-start | bytes 1048576 | tf_op jit(solution)/shard_map/all_to_all | solution.py:58
  23.6 2.4 copy-start.1
  39.7 20.2 %all-to-all-start.1 = ((f32[128,2,640]{2,1,0:T(2,128)}), f32[128,2,640]{2,1,0:T(2,128)}, u32[]{:S(2)}, u32[]{:S(2)}) async-start(f32[128,2,640]{2,1,0:T(2,128)} %copy.55), calls=%async_computation.1 | async-start | bytes 1310720 | tf_op jit(solution)/shard_map/all_to_all | solution.py:66
  61.4 1.6 copy-start.2
  63.7 18.4 %copy-start.3 = (bf16[1024,512]{1,0:T(8,128)(2,1)S(1)}, bf16[1024,512]{1,0:T(8,128)(2,1)}, u32[]{:S(2)}) copy-start(bf16[1024,512]{1,0:T(8,128)(2,1)} %param.24) | copy-start | bytes 3145732
  82.1 6.5 %copy-start.6 = (f32[8192]{0:T(1024)S(1)}, f32[8192]{0:T(1024)}, u32[]{:S(2)}) copy-start(f32[8192]{0:T(1024)} %param.25) | copy-start | bytes 98308
  82.6 19.8 %copy-start.4 = (bf16[2,1,8192]{2,0,1:T(2,128)(2,1)S(1)}, bf16[2,1,8192]{2,0,1:T(2,128)(2,1)}, u32[]{:S(2)}) copy-start(bf16[2,1,8192]{2,0,1:T(2,128)(2,1)} %param.15) | copy-start | bytes 98308
  83.8 18.2 %all-to-all-start.3 = ((f32[128,2,512]{2,1,0:T(2,128)}), f32[128,2,512]{2,1,0:T(2,128)S(1)}, u32[]{:S(2)}, u32[]{:S(2)}) async-start(f32[128,2,512]{2,1,0:T(2,128)} %copy.61), calls=%async_computation.3 | async-start | bytes 1048576 | tf_op jit(solution)/shard_map/all_to_all | solution.py:66
  87.8 154.6 %all-gather.2.cloned.1.call-start = ((), (), s32[]{:S(2)}) async-start(), calls=%async_computation.8 | async-start | bytes 8454144 | tf_op jit(solution)/shard_map/all_gather | solution.py:162
  185.8 6.0 %copy-start.7 = (s32[512]{0:T(512)S(1)}, s32[512]{0:T(512)}, u32[]{:S(2)}) copy-start(s32[512]{0:T(512)} %param.20) | copy-start | bytes 6148
  185.8 6.0 %copy-start.8 = (s32[1,16]{1,0:T(1,128)S(1)}, s32[1,16]{1,0:T(1,128)}, u32[]{:S(2)}) copy-start(s32[1,16]{1,0:T(1,128)} %param.19) | copy-start | bytes 196
  185.8 32.0 %all-to-all-start.6 = ((bf16[128,2,3584]{2,1,0:T(2,128)(2,1)}), bf16[128,2,3584]{2,1,0:T(2,128)(2,1)S(1)}, u32[]{:S(2)}, u32[]{:S(2)}) async-start(bf16[128,2,3584]{2,1,0:T(2,128)(2,1)} %bitcast.40), calls=%async_computation.6 | async-start | bytes 3670016 | tf_op jit(solution)/shard_map/all_to_all | solution.py:58
  221.0 21.5 %copy-start.5 = (f32[8192]{0:T(1024)S(1)}, f32[8192]{0:T(1024)}, u32[]{:S(2)}) copy-start(f32[8192]{0:T(1024)} %param.28) | copy-start | bytes 98308
  222.2 19.1 %all-to-all-start.7 = ((f32[128,2,512]{2,1,0:T(2,128)}), f32[128,2,512]{2,1,0:T(2,128)S(1)}, u32[]{:S(2)}, u32[]{:S(2)}) async-start(f32[128,2,512]{2,1,0:T(2,128)} %copy.67), calls=%async_computation.7 | async-start | bytes 1048576 | tf_op jit(solution)/shard_map/all_to_all | solution.py:66
Sparse Core Ops, SparseCore 0:
  91.8 104.0 all-gather.1

commit v3 on v2

--- a/solution.py
+++ b/solution.py
@@ -59,20 +59,23 @@
     return got.reshape(devices * rows_here, block)
 
 
-def gather_rows(partial, groups):
+def gather_rows(partial, groups, link_type=jnp.float32):
     rows, width = partial.shape
+    partial = partial.astype(link_type)
     devices = lax.psum(1, ALL)
     rows_here = rows // devices
     got = lax.all_to_all(partial.reshape(devices, rows_here, width), ALL, 0, 0, tiled=True)
-    summed = jnp.sum(got.reshape(groups, devices // groups, rows_here, width), axis=0)
+    summed = jnp.sum(
+        got.reshape(groups, devices // groups, rows_here, width).astype(jnp.float32), axis=0
+    )
     return summed.transpose(1, 0, 2).reshape(rows_here, (devices // groups) * width)
 
 
-def project(inputs, weight):
+def project(inputs, weight, link_type=jnp.float32):
     groups = lax.psum(1, "gx")
     spread = spread_rows(inputs, groups)
     partial = jnp.dot(spread, weight, preferred_element_type=jnp.float32)
-    return gather_rows(partial, groups).astype(jnp.bfloat16)
+    return gather_rows(partial, groups, link_type).astype(jnp.bfloat16)
 
 
 def head_logits(normed, lm_full):
@@ -171,7 +174,7 @@
     attended = attend(queries, k_cache[0], v_cache[0], lengths, keys_now, values_now)
     projected = project(attended, o_weight)
     residual = (layer_in.astype(jnp.float32) + projected.astype(jnp.float32)).astype(jnp.bfloat16)
-    gate_up = project(norm_rows(residual, ffn_gain), gate_up_weight)
+    gate_up = project(norm_rows(residual, ffn_gain), gate_up_weight, jnp.bfloat16)
     hidden_units = (
         jax.nn.silu(gate_up[:, :FF].astype(jnp.float32)) * gate_up[:, FF:].astype(jnp.float32)
     ).astype(jnp.bfloat16)

time: 261 us -> 247 us (0.946)
  blocking collectives: 86.8 us -> 67.7 us
  waiting for transfers between devices: 77.4 us -> 82.3 us
    all_to_all x1, blocking collectives: 50.8 us -> 31.2 us  [gather_rows(): lax.all_to_all(partial.reshape(devices, rows_here, width), ALL, 0, 0, til...]
    all_to_all x3, waiting for transfers between devices: 42.3 us -> 47.9 us  [gather_rows(): lax.all_to_all(partial.reshape(devices, rows_here, width), ALL, 0, 0, til...]
    dot_general x4 -> x3, local copies, waits for them, and re-layouts: 6.7 us -> 3.85 us  [project(): partial = jnp.dot(spread, weight, preferred_element_type=jnp.float32)]
    reshape x0 -> x2, local copies, waits for them, and re-layouts: none -> 2.72 us  [the longest x1 1.67 us: gather_rows(): partial.reshape(devices, rows_here, width)]
  transfers between devices with their start and end apart: 6 -> 6, of which waited for: 5 -> 5; matrix products, arithmetic and copies ran while one was open for 10% -> 14% of each run, Pallas kernels for 0% -> 0%
where the time goes in v3:
time: 247 us; the launch traced here: 246 us
  waiting for transfers between devices  82.3 us (33%)
  blocking collectives  67.7 us (27%)
  starting transfers between devices  31.1 us (13%)
  matrix products  18.6 us (8%)
  between operations  17 us (7%)
  local copies, waits for them, and re-layouts  16.4 us (7%)
  other arithmetic  12.6 us (5%)
    all_to_all x3, waiting for transfers between devices, gather_rows(): lax.all_to_all(partial.reshape(devices, rows_here, width), ALL, 0, 0, til...  47.9 us
    all_to_all x2, blocking collectives, spread_rows(): got = lax.all_to_all(send, ALL, 0, 0, tiled=True)  36.4 us
    all_to_all x2, waiting for transfers between devices, spread_rows(): got = lax.all_to_all(send, ALL, 0, 0, tiled=True)  33.8 us
    all_to_all x1, blocking collectives, gather_rows(): lax.all_to_all(partial.reshape(devices, rows_here, width), ALL, 0, 0, til...  31.2 us
    all_to_all x2, starting transfers between devices, spread_rows(): got = lax.all_to_all(send, ALL, 0, 0, tiled=True)  17.1 us
    all_to_all x3, starting transfers between devices, gather_rows(): lax.all_to_all(partial.reshape(devices, rows_here, width), ALL, 0, 0, til...  14 us
    dot_general x4, matrix products, project(): partial = jnp.dot(spread, weight, preferred_element_type=jnp.float32)  10.5 us
    unnamed x23, local copies, waits for them, and re-layouts  5.06 us
  transfers between devices with their start and end apart: 6, of which 5 were waited for; matrix products, arithmetic and copies ran while one was open for 14% of the time, Pallas kernels for 0%

profile of v3, /device:TPU:1, one launch (start us, length us, event | category | flops | bytes accessed | tf_op | source)
XLA Modules:
  0.0 245.7 jit_solution(14366834374780422437)
XLA Ops:
  7.2 0.0 copy-start
  7.2 1.0 fusion.52
  8.2 0.8 convert.44
  9.0 0.8 mul.177
  9.8 0.1 fusion.59
  9.9 1.1 broadcast_in_dim.61
  11.0 11.9 %all-to-all-start = ((bf16[128,2,1024]{2,1,0:T(2,128)(2,1)}), bf16[128,2,1024]{2,1,0:T(2,128)(2,1)}, u32[]{:S(2)}, u32[]{:S(2)}) async-start(bf16[128,2,1024]{2,1,0:T(2,128)(2,1)} %bitcast.3), calls=%async_computation | async-start | bytes 1048576 | tf_op jit(solution)/shard_map/all_to_all | solution.py:58
  22.9 0.0 all-gather.2.cloned.1.call-start
  23.0 0.7 all-gather.2.cloned.1.call-update
  24.3 0.0 copy-start.1
  24.3 2.4 copy.75
  26.7 2.0 copy.76
  28.7 7.9 %all-to-all-done = bf16[128,2,1024]{2,1,0:T(2,128)(2,1)} async-done(((bf16[128,2,1024]{2,1,0:T(2,128)(2,1)}), bf16[128,2,1024]{2,1,0:T(2,128)(2,1)}, u32[]{:S(2)}, u32[]{:S(2)}) %all-to-all-start) | async-done | bytes 524320 | tf_op jit(solution)/shard_map/all_to_all | solution.py:58
  36.6 1.6 fusion.7
  38.3 1.3 copy.53
  39.6 5.0 %all-to-all-start.1 = ((f32[128,2,640]{2,1,0:T(2,128)}), f32[128,2,640]{2,1,0:T(2,128)}, u32[]{:S(2)}, u32[]{:S(2)}) async-start(f32[128,2,640]{2,1,0:T(2,128)} %copy.53), calls=%async_computation.1 | async-start | bytes 1310720 | tf_op jit(solution)/shard_map/all_to_all | solution.py:67
  44.7 0.1 multiply_cosine_fusion
  44.8 15.3 %all-to-all-done.1 = f32[128,2,640]{2,1,0:T(2,128)} async-done(((f32[128,2,640]{2,1,0:T(2,128)}), f32[128,2,640]{2,1,0:T(2,128)}, u32[]{:S(2)}, u32[]{:S(2)}) %all-to-all-start.1) | async-done | bytes 655392 | tf_op jit(solution)/shard_map/all_to_all | solution.py:67
  60.1 1.3 reduce_sum.100
  61.4 0.6 copy-done.6
  62.0 0.1 fusion.56
  62.1 0.1 subtract_convert_fusion.1
  62.2 0.8 fusion.83
  63.0 0.4 fusion.84
  63.4 0.1 fusion.76
  63.5 0.2 fusion.31
  63.7 0.1 copy-done.2
  63.8 0.7 fusion.19
  64.5 1.0 fusion.22
  65.5 0.3 broadcast_in_dim.67
  65.8 18.1 %all_to_all.40 = bf16[128,2,1024]{2,1,0:T(2,128)(2,1)S(1)} all-to-all(bf16[128,2,1024]{2,1,0:T(2,128)(2,1)S(1)} %bitcast.159), channel_id=1, replica_groups=mesh['gx'=8,'yz'=16] {'gx','yz'}, dimensions={0} | all-to-all | bytes 1048576 | tf_op jit(solution)/shard_map/all_to_all | solution.py:58
  83.9 0.4 fusion.27
  84.3 0.0 copy-start.4
  84.3 1.3 copy.59
  85.6 4.1 %all-to-all-start.3 = ((f32[128,2,512]{2,1,0:T(2,128)}), f32[128,2,512]{2,1,0:T(2,128)S(1)}, u32[]{:S(2)}, u32[]{:S(2)}) async-start(f32[128,2,512]{2,1,0:T(2,128)} %copy.59), calls=%async_computation.3 | async-start | bytes 1048576 | tf_op jit(solution)/shard_map/all_to_all | solution.py:67
  89.7 18.8 %all-to-all-done.3 = f32[128,2,512]{2,1,0:T(2,128)S(1)} async-done(((f32[128,2,512]{2,1,0:T(2,128)}), f32[128,2,512]{2,1,0:T(2,128)S(1)}, u32[]{:S(2)}, u32[]{:S(2)}) %all-to-all-start.3) | async-done | bytes 524320 | tf_op jit(solution)/shard_map/all_to_all | solution.py:67
  108.5 0.2 reduce_sum.103
  108.8 0.2 fusion.44
  109.0 0.1 fusion.58
  109.1 0.3 broadcast_in_dim.68
  109.4 18.4 %all_to_all.41 = bf16[128,2,1024]{2,1,0:T(2,128)(2,1)S(1)} all-to-all(bf16[128,2,1024]{2,1,0:T(2,128)(2,1)S(1)} %bitcast.160), channel_id=1, replica_groups=mesh['gx'=8,'yz'=16] {'gx','yz'}, dimensions={0} | all-to-all | bytes 1048576 | tf_op jit(solution)/shard_map/all_to_all | solution.py:58
  127.8 1.0 reshape.310
  128.8 5.3 %convolution_convert_fusion = bf16[256,3584]{1,0:T(8,128)(2,1)S(1)} fusion(bf16[256,1024]{1,0:T(8,128)(2,1)} %reshape.310, bf16[1024,3584]{1,0:T(8,128)(2,1)} %param.26), kind=kOutput, calls=%fused_computation | convolution fusion | flops 1879965696 | bytes 9699328 | tf_op jit(solution)/shard_map/dot_general | solution.py:77
  134.1 1.7 reshape.311
  135.8 31.2 %all_to_all.42 = bf16[128,2,3584]{2,1,0:T(2,128)(2,1)S(1)} all-to-all(bf16[128,2,3584]{2,1,0:T(2,128)(2,1)} %reshape.311), channel_id=1, replica_groups=mesh['gx'=8,'yz'=16] {'gx','yz'}, dimensions={0} | all-to-all | bytes 3670016 | tf_op jit(solution)/shard_map/all_to_all | solution.py:67
  167.1 2.2 reduce.4
  169.2 0.3 fusion.40
  169.5 2.3 broadcast_in_dim.120
  171.8 5.1 %all-to-all-start.6 = ((bf16[128,2,3584]{2,1,0:T(2,128)(2,1)}), bf16[128,2,3584]{2,1,0:T(2,128)(2,1)S(1)}, u32[]{:S(2)}, u32[]{:S(2)}) async-start(bf16[128,2,3584]{2,1,0:T(2,128)(2,1)} %bitcast.39), calls=%async_computation.6 | async-start | bytes 3670016 | tf_op jit(solution)/shard_map/all_to_all | solution.py:58
  177.6 0.2 fusion.32
  177.8 25.9 %all-to-all-done.6 = bf16[128,2,3584]{2,1,0:T(2,128)(2,1)S(1)} async-done(((bf16[128,2,3584]{2,1,0:T(2,128)(2,1)}), bf16[128,2,3584]{2,1,0:T(2,128)(2,1)S(1)}, u32[]{:S(2)}, u32[]{:S(2)}) %all-to-all-start.6) | async-done | bytes 1835040 | tf_op jit(solution)/shard_map/all_to_all | solution.py:58
  203.7 3.1 %fusion = f32[128,2,512]{2,0,1:T(8,128)S(1)} fusion(bf16[3584,512]{1,0:T(8,128)(2,1)} %param.27, bf16[128,2,3584]{2,1,0:T(2,128)(2,1)S(1)} %all-to-all-done.6), kind=kOutput, calls=%fused_computation.1 | convolution fusion | flops 939524096 | bytes 6029312 | tf_op jit(solution)/shard_map/dot_general | solution.py:77
  206.9 1.3 copy.63
  208.1 4.9 %all-to-all-start.7 = ((f32[128,2,512]{2,1,0:T(2,128)}), f32[128,2,512]{2,1,0:T(2,128)S(1)}, u32[]{:S(2)}, u32[]{:S(2)}) async-start(f32[128,2,512]{2,1,0:T(2,128)} %copy.63), calls=%async_computation.7 | async-start | bytes 1048576 | tf_op jit(solution)/shard_map/all_to_all | solution.py:67
  213.1 0.4 fusion.26
  213.5 13.8 %all-to-all-done.7 = f32[128,2,512]{2,1,0:T(2,128)S(1)} async-done(((f32[128,2,512]{2,1,0:T(2,128)}), f32[128,2,512]{2,1,0:T(2,128)S(1)}, u32[]{:S(2)}, u32[]{:S(2)}) %all-to-all-start.7) | async-done | bytes 524320 | tf_op jit(solution)/shard_map/all_to_all | solution.py:67
  227.3 0.2 reduce_sum.106
  227.5 0.2 fusion.46
  227.7 0.7 add_convert_fusion
  228.3 4.6 %fusion.54 = f32[2,512]{1,0:T(2,128)S(1)} fusion(bf16[8192,512]{1,0:T(8,128)(2,1)} %all-gather.2.cloned.1.call-done, bf16[2,8192]{1,0:T(2,128)(2,1)S(1)} %get-tuple-element.7, f32[2]{0:T(128)S(1)} %add_rsqrt_fusion, f32[8192]{0:T(1024)S(1)} %copy-done.5), kind=kOutput, calls=%fused_computation.69 | convolution fusion | flops 16842752 | bytes 8458248 | tf_op jit(solution)/shard_map/dot_general | solution.py:82
  233.0 0.7 fusion.67
  233.7 2.0 fusion.68
  236.9 1.3 fusion.69
  238.3 0.6 pad_maximum_fusion.1
  (40 shorter events, 0.4 us)
Async XLA Ops:
  7.2 29.5 %copy-start = (bf16[1024,640]{1,0:T(8,128)(2,1)S(1)}, bf16[1024,640]{1,0:T(8,128)(2,1)}, u32[]{:S(2)}) copy-start(bf16[1024,640]{1,0:T(8,128)(2,1)} %param.23) | copy-start | bytes 3932164
  11.0 25.7 %all-to-all-start = ((bf16[128,2,1024]{2,1,0:T(2,128)(2,1)}), bf16[128,2,1024]{2,1,0:T(2,128)(2,1)}, u32[]{:S(2)}, u32[]{:S(2)}) async-start(bf16[128,2,1024]{2,1,0:T(2,128)(2,1)} %bitcast.3), calls=%async_computation | async-start | bytes 1048576 | tf_op jit(solution)/shard_map/all_to_all | solution.py:58
  22.9 205.4 %all-gather.2.cloned.1.call-start = ((), (), s32[]{:S(2)}) async-start(), calls=%async_computation.8 | async-start | bytes 8454144 | tf_op jit(solution)/shard_map/all_gather | solution.py:165
  24.3 2.4 copy-start.1
  39.6 20.4 %all-to-all-start.1 = ((f32[128,2,640]{2,1,0:T(2,128)}), f32[128,2,640]{2,1,0:T(2,128)}, u32[]{:S(2)}, u32[]{:S(2)}) async-start(f32[128,2,640]{2,1,0:T(2,128)} %copy.53), calls=%async_computation.1 | async-start | bytes 1310720 | tf_op jit(solution)/shard_map/all_to_all | solution.py:67
  61.4 0.6 copy-start.6
  62.2 1.6 copy-start.2
  64.5 19.4 %copy-start.3 = (bf16[1024,512]{1,0:T(8,128)(2,1)S(1)}, bf16[1024,512]{1,0:T(8,128)(2,1)}, u32[]{:S(2)}) copy-start(bf16[1024,512]{1,0:T(8,128)(2,1)} %param.24) | copy-start | bytes 3145732
  83.9 5.8 %copy-start.7 = (f32[8192]{0:T(1024)S(1)}, f32[8192]{0:T(1024)}, u32[]{:S(2)}) copy-start(f32[8192]{0:T(1024)} %param.25) | copy-start | bytes 98308
  84.3 24.5 %copy-start.4 = (bf16[2,1,8192]{2,0,1:T(2,128)(2,1)S(1)}, bf16[2,1,8192]{2,0,1:T(2,128)(2,1)}, u32[]{:S(2)}) copy-start(bf16[2,1,8192]{2,0,1:T(2,128)(2,1)} %param.15) | copy-start | bytes 98308
  85.6 22.9 %all-to-all-start.3 = ((f32[128,2,512]{2,1,0:T(2,128)}), f32[128,2,512]{2,1,0:T(2,128)S(1)}, u32[]{:S(2)}, u32[]{:S(2)}) async-start(f32[128,2,512]{2,1,0:T(2,128)} %copy.59), calls=%async_computation.3 | async-start | bytes 1048576 | tf_op jit(solution)/shard_map/all_to_all | solution.py:67
  171.8 5.8 %copy-start.8 = (s32[512]{0:T(512)S(1)}, s32[512]{0:T(512)}, u32[]{:S(2)}) copy-start(s32[512]{0:T(512)} %param.20) | copy-start | bytes 6148
  171.8 5.8 %copy-start.9 = (s32[1,16]{1,0:T(1,128)S(1)}, s32[1,16]{1,0:T(1,128)}, u32[]{:S(2)}) copy-start(s32[1,16]{1,0:T(1,128)} %param.19) | copy-start | bytes 196
  171.8 31.9 %all-to-all-start.6 = ((bf16[128,2,3584]{2,1,0:T(2,128)(2,1)}), bf16[128,2,3584]{2,1,0:T(2,128)(2,1)S(1)}, u32[]{:S(2)}, u32[]{:S(2)}) async-start(bf16[128,2,3584]{2,1,0:T(2,128)(2,1)} %bitcast.39), calls=%async_computation.6 | async-start | bytes 3670016 | tf_op jit(solution)/shard_map/all_to_all | solution.py:58
  206.8 21.5 %copy-start.5 = (f32[8192]{0:T(1024)S(1)}, f32[8192]{0:T(1024)}, u32[]{:S(2)}) copy-start(f32[8192]{0:T(1024)} %param.28) | copy-start | bytes 98308
  208.1 19.1 %all-to-all-start.7 = ((f32[128,2,512]{2,1,0:T(2,128)}), f32[128,2,512]{2,1,0:T(2,128)S(1)}, u32[]{:S(2)}, u32[]{:S(2)}) async-start(f32[128,2,512]{2,1,0:T(2,128)} %copy.63), calls=%async_computation.7 | async-start | bytes 1048576 | tf_op jit(solution)/shard_map/all_to_all | solution.py:67
Sparse Core Ops, SparseCore 0:
  26.9 82.4 all-gather.1

commit v4 on v3

--- a/solution.py
+++ b/solution.py
@@ -55,26 +55,22 @@
     send = jnp.broadcast_to(
         blocks[:, None], (groups, devices // groups, rows_here, block)
     ).reshape(devices, rows_here, block)
-    got = lax.all_to_all(send, ALL, 0, 0, tiled=True)
-    return got.reshape(devices * rows_here, block)
-
-
-def gather_rows(partial, groups, link_type=jnp.float32):
-    rows, width = partial.shape
-    partial = partial.astype(link_type)
-    devices = lax.psum(1, ALL)
-    rows_here = rows // devices
-    got = lax.all_to_all(partial.reshape(devices, rows_here, width), ALL, 0, 0, tiled=True)
+    return lax.all_to_all(send, ALL, 0, 0, tiled=True)
+
+
+def gather_rows(partial, groups, link_type):
+    devices, rows_here, width = partial.shape
+    got = lax.all_to_all(partial.astype(link_type), ALL, 0, 0, tiled=True)
     summed = jnp.sum(
         got.reshape(groups, devices // groups, rows_here, width).astype(jnp.float32), axis=0
     )
     return summed.transpose(1, 0, 2).reshape(rows_here, (devices // groups) * width)
 
 
-def project(inputs, weight, link_type=jnp.float32):
+def project(inputs, weight, link_type=jnp.bfloat16):
     groups = lax.psum(1, "gx")
     spread = spread_rows(inputs, groups)
-    partial = jnp.dot(spread, weight, preferred_element_type=jnp.float32)
+    partial = jnp.einsum("dsk,kn->dsn", spread, weight, preferred_element_type=jnp.float32)
     return gather_rows(partial, groups, link_type).astype(jnp.bfloat16)
 
 
@@ -174,7 +170,7 @@
     attended = attend(queries, k_cache[0], v_cache[0], lengths, keys_now, values_now)
     projected = project(attended, o_weight)
     residual = (layer_in.astype(jnp.float32) + projected.astype(jnp.float32)).astype(jnp.bfloat16)
-    gate_up = project(norm_rows(residual, ffn_gain), gate_up_weight, jnp.bfloat16)
+    gate_up = project(norm_rows(residual, ffn_gain), gate_up_weight)
     hidden_units = (
         jax.nn.silu(gate_up[:, :FF].astype(jnp.float32)) * gate_up[:, FF:].astype(jnp.float32)
     ).astype(jnp.bfloat16)

time: 247 us -> 233 us (0.943)
  waiting for transfers between devices: 82.3 us -> 71.8 us
    all_to_all x5, waiting for transfers between devices: 81.7 us -> 71.1 us  [the longest x3 37.8 us: gather_rows(): got = lax.all_to_all(partial.astype(link_type), ALL, 0, 0, tiled=True)]
    convert_element_type x0 -> x4, local copies, waits for them, and re-layouts: none -> 4.92 us  [gather_rows(): got = lax.all_to_all(partial.astype(link_type), ALL, 0, 0, tiled=True)]
    dot_general x3 -> x0, local copies, waits for them, and re-layouts: 3.85 us -> none  [project(): partial = jnp.dot(spread, weight, preferred_element_type=jnp.float32)]
    reshape x2 -> x0, local copies, waits for them, and re-layouts: 2.72 us -> none  [the longest x1 1.67 us: gather_rows(): partial.reshape(devices, rows_here, width)]
where the time goes in v4:
time: 233 us; the launch traced here: 232 us
  waiting for transfers between devices  71.8 us (31%)
  blocking collectives  66.7 us (29%)
  starting transfers between devices  31 us (13%)
  matrix products  18.3 us (8%)
  between operations  17 us (7%)
  local copies, waits for them, and re-layouts  14.8 us (6%)
  other arithmetic  12.7 us (5%)
    all_to_all x3, waiting for transfers between devices, gather_rows(): got = lax.all_to_all(partial.astype(link_type), ALL, 0, 0, tiled=True)  37.8 us
    all_to_all x2, blocking collectives, spread_rows(): return lax.all_to_all(send, ALL, 0, 0, tiled=True)  36.3 us
    all_to_all x2, waiting for transfers between devices, spread_rows(): return lax.all_to_all(send, ALL, 0, 0, tiled=True)  33.4 us
    all_to_all x1, blocking collectives, gather_rows(): got = lax.all_to_all(partial.astype(link_type), ALL, 0, 0, tiled=True)  30.4 us
    all_to_all x2, starting transfers between devices, spread_rows(): return lax.all_to_all(send, ALL, 0, 0, tiled=True)  17.1 us
    all_to_all x3, starting transfers between devices, gather_rows(): got = lax.all_to_all(partial.astype(link_type), ALL, 0, 0, tiled=True)  13.9 us
    dot_general x4, matrix products, project(): jnp.einsum('dsk,kn->dsn', spread, weight, preferred_element_type=jnp.floa...  10.3 us
    unnamed x23, local copies, waits for them, and re-layouts  5.05 us
  transfers between devices with their start and end apart: 6, of which 5 were waited for; matrix products, arithmetic and copies ran while one was open for 14% of the time, Pallas kernels for 0%

profile of v4, /device:TPU:1, one launch (start us, length us, event | category | flops | bytes accessed | tf_op | source)
XLA Modules:
  0.0 232.3 jit_solution(414969979009615732)
XLA Ops:
  7.2 0.0 copy-start
  7.2 1.0 fusion.65
  8.2 0.8 convert.50
  9.0 0.8 mul.177
  9.8 0.1 fusion.72
  9.9 1.1 broadcast_in_dim.61
  11.0 11.9 %all-to-all-start = ((bf16[128,2,1024]{2,1,0:T(2,128)(2,1)}), bf16[128,2,1024]{2,1,0:T(2,128)(2,1)}, u32[]{:S(2)}, u32[]{:S(2)}) async-start(bf16[128,2,1024]{2,1,0:T(2,128)(2,1)} %bitcast.3), calls=%async_computation | async-start | bytes 1048576 | tf_op jit(solution)/shard_map/all_to_all | solution.py:58
  22.9 0.0 all-gather.2.cloned.1.call-start
  23.0 0.7 all-gather.2.cloned.1.call-update
  24.3 0.0 copy-start.1
  24.3 2.4 %copy.79 = bf16[128,8,8,128]{3,2,1,0:T(8,128)(2,1)S(1)} copy(bf16[128,8,8,128]{3,1,2,0:T(8,128)(2,1)} %bitcast.161) | data formatting | bytes 4194304
  26.7 0.0 copy-done.1
  26.7 2.0 copy.80
  28.8 7.9 %all-to-all-done = bf16[128,2,1024]{2,1,0:T(2,128)(2,1)} async-done(((bf16[128,2,1024]{2,1,0:T(2,128)(2,1)}), bf16[128,2,1024]{2,1,0:T(2,128)(2,1)}, u32[]{:S(2)}, u32[]{:S(2)}) %all-to-all-start) | async-done | bytes 524320 | tf_op jit(solution)/shard_map/all_to_all | solution.py:58
  36.6 1.6 fusion.23
  38.3 1.1 copy.55
  39.3 5.0 %all-to-all-start.1 = ((bf16[128,2,640]{2,1,0:T(2,128)(2,1)}), bf16[128,2,640]{2,1,0:T(2,128)(2,1)}, u32[]{:S(2)}, u32[]{:S(2)}) async-start(bf16[128,2,640]{2,1,0:T(2,128)(2,1)} %copy.55), calls=%async_computation.1 | async-start | bytes 655360 | tf_op jit(solution)/shard_map/all_to_all | solution.py:63
  44.3 0.1 multiply_cosine_fusion
  44.4 11.9 %all-to-all-done.1 = bf16[128,2,640]{2,1,0:T(2,128)(2,1)} async-done(((bf16[128,2,640]{2,1,0:T(2,128)(2,1)}), bf16[128,2,640]{2,1,0:T(2,128)(2,1)}, u32[]{:S(2)}, u32[]{:S(2)}) %all-to-all-start.1) | async-done | bytes 327712 | tf_op jit(solution)/shard_map/all_to_all | solution.py:63
  56.4 1.3 reduce.4
  57.7 0.6 copy-done.5
  58.3 0.1 fusion.69
  58.4 0.1 subtract_convert_fusion.1
  58.5 0.8 fusion.95
  59.3 0.4 fusion.96
  59.6 0.2 fusion.44
  59.9 0.1 fusion.89
  60.0 0.1 copy-done.2
  60.1 0.7 fusion.32
  60.8 0.9 fusion.35
  61.7 0.3 broadcast_in_dim.67
  62.0 0.0 copy-start.6
  62.0 18.5 %all_to_all.40 = bf16[128,2,1024]{2,1,0:T(2,128)(2,1)S(1)} all-to-all(bf16[128,2,1024]{2,1,0:T(2,128)(2,1)S(1)} %bitcast.164), channel_id=1, replica_groups=mesh['gx'=8,'yz'=16] {'gx','yz'}, dimensions={0} | all-to-all | bytes 1048576 | tf_op jit(solution)/shard_map/all_to_all | solution.py:58
  80.5 0.4 convolution_convert_fusion
  80.9 1.0 copy.61
  81.9 4.0 %all-to-all-start.3 = ((bf16[128,2,512]{2,1,0:T(2,128)(2,1)}), bf16[128,2,512]{2,1,0:T(2,128)(2,1)S(1)}, u32[]{:S(2)}, u32[]{:S(2)}) async-start(bf16[128,2,512]{2,1,0:T(2,128)(2,1)} %copy.61), calls=%async_computation.3 | async-start | bytes 524288 | tf_op jit(solution)/shard_map/all_to_all | solution.py:63
  86.0 14.3 %all-to-all-done.3 = bf16[128,2,512]{2,1,0:T(2,128)(2,1)S(1)} async-done(((bf16[128,2,512]{2,1,0:T(2,128)(2,1)}), bf16[128,2,512]{2,1,0:T(2,128)(2,1)S(1)}, u32[]{:S(2)}, u32[]{:S(2)}) %all-to-all-start.3) | async-done | bytes 262176 | tf_op jit(solution)/shard_map/all_to_all | solution.py:63
  100.3 0.2 reduce.5
  100.6 0.2 fusion.57
  100.8 0.1 fusion.71
  100.9 0.3 broadcast_in_dim.68
  101.2 17.8 %all_to_all.41 = bf16[128,2,1024]{2,1,0:T(2,128)(2,1)S(1)} all-to-all(bf16[128,2,1024]{2,1,0:T(2,128)(2,1)S(1)} %bitcast.165), channel_id=1, replica_groups=mesh['gx'=8,'yz'=16] {'gx','yz'}, dimensions={0} | all-to-all | bytes 1048576 | tf_op jit(solution)/shard_map/all_to_all | solution.py:58
  119.0 5.1 %fusion.2 = bf16[128,2,3584]{2,0,1:T(8,128)(2,1)S(1)} fusion(bf16[1024,3584]{1,0:T(8,128)(2,1)} %param.26, bf16[128,2,1024]{2,1,0:T(2,128)(2,1)S(1)} %all_to_all.41), kind=kOutput, calls=%fused_computation.2 | convolution fusion | flops 1879965696 | bytes 9699328 | tf_op jit(solution)/shard_map/dsk,kn->dsn/dot_general | solution.py:73
  124.2 1.9 copy.65
  126.1 30.4 %all_to_all.42 = bf16[128,2,3584]{2,1,0:T(2,128)(2,1)S(1)} all-to-all(bf16[128,2,3584]{2,1,0:T(2,128)(2,1)S(1)} %copy.65), channel_id=1, replica_groups=mesh['gx'=8,'yz'=16] {'gx','yz'}, dimensions={0} | all-to-all | bytes 3670016 | tf_op jit(solution)/shard_map/all_to_all | solution.py:63
  156.5 2.2 reduce.6
  158.7 0.3 fusion.53
  159.0 2.3 broadcast_in_dim.120
  161.2 5.1 %all-to-all-start.6 = ((bf16[128,2,3584]{2,1,0:T(2,128)(2,1)}), bf16[128,2,3584]{2,1,0:T(2,128)(2,1)S(1)}, u32[]{:S(2)}, u32[]{:S(2)}) async-start(bf16[128,2,3584]{2,1,0:T(2,128)(2,1)} %bitcast.40), calls=%async_computation.6 | async-start | bytes 3670016 | tf_op jit(solution)/shard_map/all_to_all | solution.py:58
  167.0 0.2 fusion.45
  167.3 0.4 fusion.39
  167.7 25.5 %all-to-all-done.6 = bf16[128,2,3584]{2,1,0:T(2,128)(2,1)S(1)} async-done(((bf16[128,2,3584]{2,1,0:T(2,128)(2,1)}), bf16[128,2,3584]{2,1,0:T(2,128)(2,1)S(1)}, u32[]{:S(2)}, u32[]{:S(2)}) %all-to-all-start.6) | async-done | bytes 1835040 | tf_op jit(solution)/shard_map/all_to_all | solution.py:58
  193.1 3.1 %fusion.26 = bf16[128,2,512]{2,0,1:T(8,128)(2,1)S(1)} fusion(bf16[3584,512]{1,0:T(8,128)(2,1)} %param.27, bf16[128,2,3584]{2,1,0:T(2,128)(2,1)S(1)} %all-to-all-done.6), kind=kOutput, calls=%fused_computation.16 | convolution fusion | flops 939655168 | bytes 5767168 | tf_op jit(solution)/shard_map/dsk,kn->dsn/dot_general | solution.py:73
  196.3 1.0 copy.67
  197.3 4.9 %all-to-all-start.7 = ((bf16[128,2,512]{2,1,0:T(2,128)(2,1)}), bf16[128,2,512]{2,1,0:T(2,128)(2,1)S(1)}, u32[]{:S(2)}, u32[]{:S(2)}) async-start(bf16[128,2,512]{2,1,0:T(2,128)(2,1)} %copy.67), calls=%async_computation.7 | async-start | bytes 524288 | tf_op jit(solution)/shard_map/all_to_all | solution.py:63
  202.2 11.5 %all-to-all-done.7 = bf16[128,2,512]{2,1,0:T(2,128)(2,1)S(1)} async-done(((bf16[128,2,512]{2,1,0:T(2,128)(2,1)}), bf16[128,2,512]{2,1,0:T(2,128)(2,1)S(1)}, u32[]{:S(2)}, u32[]{:S(2)}) %all-to-all-start.7) | async-done | bytes 262176 | tf_op jit(solution)/shard_map/all_to_all | solution.py:63
  213.8 0.2 reduce.7
  214.0 0.2 fusion.59
  214.2 0.7 add_convert_fusion
  214.9 4.6 %fusion.67 = f32[2,512]{1,0:T(2,128)S(1)} fusion(bf16[8192,512]{1,0:T(8,128)(2,1)} %all-gather.2.cloned.1.call-done, bf16[2,8192]{1,0:T(2,128)(2,1)S(1)} %get-tuple-element.7, f32[2]{0:T(128)S(1)} %add_rsqrt_fusion, f32[8192]{0:T(1024)S(1)} %copy-done.4), kind=kOutput, calls=%fused_computation.74 | convolution fusion | flops 16842752 | bytes 8458248 | tf_op jit(solution)/shard_map/dot_general | solution.py:78
  219.5 0.7 fusion.80
  220.2 2.0 fusion.81
  223.5 1.3 fusion.82
  224.8 0.6 pad_maximum_fusion.1
  (39 shorter events, 0.4 us)
Async XLA Ops:
  7.2 29.5 %copy-start = (bf16[1024,640]{1,0:T(8,128)(2,1)S(1)}, bf16[1024,640]{1,0:T(8,128)(2,1)}, u32[]{:S(2)}) copy-start(bf16[1024,640]{1,0:T(8,128)(2,1)} %param.23) | copy-start | bytes 3932164
  11.0 25.7 %all-to-all-start = ((bf16[128,2,1024]{2,1,0:T(2,128)(2,1)}), bf16[128,2,1024]{2,1,0:T(2,128)(2,1)}, u32[]{:S(2)}, u32[]{:S(2)}) async-start(bf16[128,2,1024]{2,1,0:T(2,128)(2,1)} %bitcast.3), calls=%async_computation | async-start | bytes 1048576 | tf_op jit(solution)/shard_map/all_to_all | solution.py:58
  22.9 192.0 %all-gather.2.cloned.1.call-start = ((), (), s32[]{:S(2)}) async-start(), calls=%async_computation.8 | async-start | bytes 8454144 | tf_op jit(solution)/shard_map/all_gather | solution.py:161
  24.3 2.4 %copy-start.1 = (bf16[1,1024,1024]{2,1,0:T(8,128)(2,1)S(1)}, bf16[1,1024,1024]{2,1,0:T(8,128)(2,1)}, u32[]{:S(2)}) copy-start(bf16[1,1024,1024]{2,1,0:T(8,128)(2,1)} %param.17) | copy-start | bytes 6291460
  39.3 17.0 %all-to-all-start.1 = ((bf16[128,2,640]{2,1,0:T(2,128)(2,1)}), bf16[128,2,640]{2,1,0:T(2,128)(2,1)}, u32[]{:S(2)}, u32[]{:S(2)}) async-start(bf16[128,2,640]{2,1,0:T(2,128)(2,1)} %copy.55), calls=%async_computation.1 | async-start | bytes 655360 | tf_op jit(solution)/shard_map/all_to_all | solution.py:63
  57.7 0.6 copy-start.5
  58.5 1.6 copy-start.2
  60.1 20.4 %copy-start.8 = (bf16[1024,512]{1,0:T(8,128)(2,1)S(1)}, bf16[1024,512]{1,0:T(8,128)(2,1)}, u32[]{:S(2)}) copy-start(bf16[1024,512]{1,0:T(8,128)(2,1)} %param.24) | copy-start | bytes 3145732
  62.0 23.9 %copy-start.6 = (f32[8192]{0:T(1024)S(1)}, f32[8192]{0:T(1024)}, u32[]{:S(2)}) copy-start(f32[8192]{0:T(1024)} %param.25) | copy-start | bytes 98308
  80.5 20.1 %copy-start.3 = (bf16[2,1,8192]{2,0,1:T(2,128)(2,1)S(1)}, bf16[2,1,8192]{2,0,1:T(2,128)(2,1)}, u32[]{:S(2)}) copy-start(bf16[2,1,8192]{2,0,1:T(2,128)(2,1)} %param.15) | copy-start | bytes 98308
  81.9 18.3 %all-to-all-start.3 = ((bf16[128,2,512]{2,1,0:T(2,128)(2,1)}), bf16[128,2,512]{2,1,0:T(2,128)(2,1)S(1)}, u32[]{:S(2)}, u32[]{:S(2)}) async-start(bf16[128,2,512]{2,1,0:T(2,128)(2,1)} %copy.61), calls=%async_computation.3 | async-start | bytes 524288 | tf_op jit(solution)/shard_map/all_to_all | solution.py:63
  161.2 5.8 %copy-start.7 = (s32[512]{0:T(512)S(1)}, s32[512]{0:T(512)}, u32[]{:S(2)}) copy-start(s32[512]{0:T(512)} %param.20) | copy-start | bytes 6148
  161.2 5.8 %copy-start.9 = (s32[1,16]{1,0:T(1,128)S(1)}, s32[1,16]{1,0:T(1,128)}, u32[]{:S(2)}) copy-start(s32[1,16]{1,0:T(1,128)} %param.19) | copy-start | bytes 196
  161.2 31.9 %all-to-all-start.6 = ((bf16[128,2,3584]{2,1,0:T(2,128)(2,1)}), bf16[128,2,3584]{2,1,0:T(2,128)(2,1)S(1)}, u32[]{:S(2)}, u32[]{:S(2)}) async-start(bf16[128,2,3584]{2,1,0:T(2,128)(2,1)} %bitcast.40), calls=%async_computation.6 | async-start | bytes 3670016 | tf_op jit(solution)/shard_map/all_to_all | solution.py:58
  167.6 47.3 %copy-start.4 = (f32[8192]{0:T(1024)S(1)}, f32[8192]{0:T(1024)}, u32[]{:S(2)}) copy-start(f32[8192]{0:T(1024)} %param.28) | copy-start | bytes 98308
  197.3 16.5 %all-to-all-start.7 = ((bf16[128,2,512]{2,1,0:T(2,128)(2,1)}), bf16[128,2,512]{2,1,0:T(2,128)(2,1)S(1)}, u32[]{:S(2)}, u32[]{:S(2)}) async-start(bf16[128,2,512]{2,1,0:T(2,128)(2,1)} %copy.67), calls=%async_computation.7 | async-start | bytes 524288 | tf_op jit(solution)/shard_map/all_to_all | solution.py:63
Sparse Core Ops, SparseCore 0:
  26.9 77.1 all-gather.1

commit v5 on v4

--- a/solution.py
+++ b/solution.py
@@ -74,8 +74,32 @@
     return gather_rows(partial, groups, link_type).astype(jnp.bfloat16)
 
 
-def head_logits(normed, lm_full):
-    return jnp.dot(normed, lm_full, preferred_element_type=jnp.float32)
+SHIFT_ORDER = (2, 8, 64, 32, 4, 1, 16)
+
+
+def gather_weight(shard):
+    devices = lax.psum(1, ALL)
+    held = shard
+    for step in SHIFT_ORDER:
+        pairs = [(i, i ^ step) for i in range(devices)]
+        held = jnp.concatenate([held, lax.ppermute(held, ALL, pairs)], axis=0)
+    return held
+
+
+def held_order():
+    return [
+        sum(step for bit, step in enumerate(SHIFT_ORDER) if (place >> bit) & 1)
+        for place in range(2 ** len(SHIFT_ORDER))
+    ]
+
+
+def head_logits(normed, lm_held):
+    devices = lax.psum(1, ALL)
+    me = lax.axis_index(ALL)
+    rows_here, width = normed.shape
+    order = jnp.bitwise_xor(me, jnp.array(held_order(), dtype=jnp.int32))
+    matched = jnp.take(normed.reshape(rows_here, devices, width // devices), order, axis=1)
+    return jnp.dot(matched.reshape(rows_here, width), lm_held, preferred_element_type=jnp.float32)
 
 
 def attend(queries, k_cache, v_cache, lengths, keys_new, values_new):
@@ -158,7 +182,7 @@
     q_width = HEADS * HEAD
     kv_width = KV_HEADS * HEAD
     steps = hidden_in.shape[0]
-    lm_full = lax.all_gather(lm_weight, ALL, axis=0, tiled=True)
+    lm_full = gather_weight(lm_weight)
     layer_in = hidden_in[:, 0, :]
     positions = lengths[0] + jnp.arange(steps, dtype=jnp.int32)
     mixed = project(norm_rows(layer_in, attn_gain), qkv_weight)

time: 233 us -> 293 us (1.26)
  waiting for transfers between devices: 71.8 us -> 129 us
  blocking collectives: 66.7 us -> 17.8 us
  starting transfers between devices: 31 us -> 66.4 us
  local copies, waits for them, and re-layouts: 14.8 us -> 36.5 us
  between operations: 17 us -> 3.91 us
  other arithmetic: 12.7 us -> 18.4 us
    ppermute x0 -> x7, waiting for transfers between devices: none -> 95.8 us  [gather_weight(): held = jnp.concatenate([held, lax.ppermute(held, ALL, pairs)], axis=0)]
    all_to_all x1 -> x0, blocking collectives: 30.4 us -> none  [gather_rows(): got = lax.all_to_all(partial.astype(link_type), ALL, 0, 0, tiled=True)]
    all_to_all x2 -> x3, waiting for transfers between devices: 33.4 us -> 9.84 us  [spread_rows(): return lax.all_to_all(send, ALL, 0, 0, tiled=True)]
    all_to_all x2 -> x1, blocking collectives: 36.3 us -> 17.8 us  [spread_rows(): return lax.all_to_all(send, ALL, 0, 0, tiled=True)]
    ppermute x0 -> x7, starting transfers between devices: none -> 14.7 us  [gather_weight(): held = jnp.concatenate([held, lax.ppermute(held, ALL, pairs)], axis=0)]
    all_to_all x3 -> x4, waiting for transfers between devices: 37.8 us -> 23.6 us  [gather_rows(): got = lax.all_to_all(partial.astype(link_type), ALL, 0, 0, tiled=True)]
    all_to_all x3 -> x4, starting transfers between devices: 13.9 us -> 24.8 us  [gather_rows(): got = lax.all_to_all(partial.astype(link_type), ALL, 0, 0, tiled=True)]
    all_to_all x2 -> x3, starting transfers between devices: 17.1 us -> 26.8 us  [spread_rows(): return lax.all_to_all(send, ALL, 0, 0, tiled=True)]
  transfers between devices with their start and end apart: 6 -> 14, of which waited for: 5 -> 9; matrix products, arithmetic and copies ran while one was open for 14% -> 14% of each run, Pallas kernels for 0% -> 0%
where the time goes in v5:
time: 293 us; the launch traced here: 292 us
  waiting for transfers between devices  129 us (44%)
  starting transfers between devices  66.4 us (23%)
  local copies, waits for them, and re-layouts  36.5 us (12%)
  matrix products  19.6 us (7%)
  other arithmetic  18.4 us (6%)
  blocking collectives  17.8 us (6%)
  between operations  3.91 us (1%)
    ppermute x7, waiting for transfers between devices, gather_weight(): held = jnp.concatenate([held, lax.ppermute(held, ALL, pairs)], axis=0)  95.8 us
    all_to_all x3, starting transfers between devices, spread_rows(): return lax.all_to_all(send, ALL, 0, 0, tiled=True)  26.8 us
    all_to_all x4, starting transfers between devices, gather_rows(): got = lax.all_to_all(partial.astype(link_type), ALL, 0, 0, tiled=True)  24.8 us
    all_to_all x4, waiting for transfers between devices, gather_rows(): got = lax.all_to_all(partial.astype(link_type), ALL, 0, 0, tiled=True)  23.6 us
    all_to_all x1, blocking collectives, spread_rows(): return lax.all_to_all(send, ALL, 0, 0, tiled=True)  17.8 us
    ppermute x7, starting transfers between devices, gather_weight(): held = jnp.concatenate([held, lax.ppermute(held, ALL, pairs)], axis=0)  14.7 us
    unnamed x43, local copies, waits for them, and re-layouts  14.6 us
    dot_general x4, matrix products, project(): jnp.einsum('dsk,kn->dsn', spread, weight, preferred_element_type=jnp.floa...  11.6 us
  transfers between devices with their start and end apart: 14, of which 9 were waited for; matrix products, arithmetic and copies ran while one was open for 14% of the time, Pallas kernels for 0%

profile of v5, /device:TPU:1, one launch (start us, length us, event | category | flops | bytes accessed | tf_op | source)
XLA Modules:
  0.0 291.9 jit_solution(10322795673495491694)
XLA Ops:
  0.6 0.9 convert_element_type.283
  1.5 1.0 fusion.62
  2.5 0.8 mul.184
  3.4 1.1 broadcast_in_dim.128
  4.5 11.9 %all-to-all-start = ((bf16[128,2,1024]{2,1,0:T(2,128)(2,1)}), bf16[128,2,1024]{2,1,0:T(2,128)(2,1)}, u32[]{:S(2)}, u32[]{:S(2)}) async-start(bf16[128,2,1024]{2,1,0:T(2,128)(2,1)} %bitcast.3), calls=%async_computation | async-start | bytes 1048576 | tf_op jit(solution)/shard_map/all_to_all | solution.py:58
  17.3 2.2 copy.123
  19.5 2.0 copy.124
  22.0 8.2 %all-to-all-done = bf16[128,2,1024]{2,1,0:T(2,128)(2,1)} async-done(((bf16[128,2,1024]{2,1,0:T(2,128)(2,1)}), bf16[128,2,1024]{2,1,0:T(2,128)(2,1)}, u32[]{:S(2)}, u32[]{:S(2)}) %all-to-all-start) | async-done | bytes 524320 | tf_op jit(solution)/shard_map/all_to_all | solution.py:58
  30.1 1.6 fusion.23
  31.8 1.1 copy.91
  32.8 5.0 %all-to-all-start.1 = ((bf16[128,2,640]{2,1,0:T(2,128)(2,1)}), bf16[128,2,640]{2,1,0:T(2,128)(2,1)}, u32[]{:S(2)}, u32[]{:S(2)}) async-start(bf16[128,2,640]{2,1,0:T(2,128)(2,1)} %copy.91), calls=%async_computation.1 | async-start | bytes 655360 | tf_op jit(solution)/shard_map/all_to_all | solution.py:63
  37.8 0.7 multiply_cosine_fusion
  38.5 11.2 %all-to-all-done.1 = bf16[128,2,640]{2,1,0:T(2,128)(2,1)} async-done(((bf16[128,2,640]{2,1,0:T(2,128)(2,1)}), bf16[128,2,640]{2,1,0:T(2,128)(2,1)}, u32[]{:S(2)}, u32[]{:S(2)}) %all-to-all-start.1) | async-done | bytes 327712 | tf_op jit(solution)/shard_map/all_to_all | solution.py:63
  49.7 1.3 reduce.4
  51.1 0.9 fusion.65
  52.0 0.8 subtract_convert_fusion.1
  52.8 0.8 fusion.91
  53.6 1.1 fusion.92
  54.7 0.8 fusion.85
  55.7 0.7 fusion.32
  57.0 17.8 %all_to_all.40 = bf16[128,2,1024]{2,1,0:T(2,128)(2,1)S(1)} all-to-all(bf16[128,2,1024]{2,1,0:T(2,128)(2,1)S(1)} %bitcast.166), channel_id=1, replica_groups=mesh['gx'=8,'yz'=16] {'gx','yz'}, dimensions={0} | all-to-all | bytes 1048576 | tf_op jit(solution)/shard_map/all_to_all | solution.py:58
  74.9 1.7 convolution_convert_fusion
  76.5 1.0 copy.97
  77.5 4.0 %all-to-all-start.3 = ((bf16[128,2,512]{2,1,0:T(2,128)(2,1)}), bf16[128,2,512]{2,1,0:T(2,128)(2,1)S(1)}, u32[]{:S(2)}, u32[]{:S(2)}) async-start(bf16[128,2,512]{2,1,0:T(2,128)(2,1)} %copy.97), calls=%async_computation.3 | async-start | bytes 524288 | tf_op jit(solution)/shard_map/all_to_all | solution.py:63
  81.5 3.1 %collective-permute-start = (bf16[64,512]{1,0:T(8,128)(2,1)S(1)}, bf16[64,512]{1,0:T(8,128)(2,1)S(1)}, u32[]{:S(2)}, u32[]{:S(2)}) collective-permute-start(bf16[64,512]{1,0:T(8,128)(2,1)S(1)} %copy-done.5), channel_id=1, source_target_pairs={{0,2},{1,3},{2,0},{3,1},{4,6},{5,7},{6,4},{7,5},{8,10},{9,11},{10,... | collective-permute-start | bytes 196616 | tf_op jit(solution)/shard_map/ppermute | solution.py:85
  84.6 2.5 collective-permute-done
  87.1 4.2 %collective-permute-start.1 = (bf16[128,512]{1,0:T(8,128)(2,1)S(1)}, bf16[128,512]{1,0:T(8,128)(2,1)S(1)}, u32[]{:S(2)}, u32[]{:S(2)}) collective-permute-start(bf16[128,512]{1,0:T(8,128)(2,1)S(1)} %pad_maximum_fusion.2), channel_id=1, source_target_pairs={{0,8},{1,9},{2,10},{3,11},{4,12},{5,13},{6,14},{7,15},{8,0},{9,1},... | collective-permute-start | bytes 393224 | tf_op jit(solution)/shard_map/ppermute | solution.py:85
  91.4 1.7 all-to-all-done.3
  93.7 1.1 broadcast_in_dim.135
  94.8 5.2 %all-to-all-start.4 = ((bf16[128,2,1024]{2,1,0:T(2,128)(2,1)}), bf16[128,2,1024]{2,1,0:T(2,128)(2,1)S(1)}, u32[]{:S(2)}, u32[]{:S(2)}) async-start(bf16[128,2,1024]{2,1,0:T(2,128)(2,1)} %bitcast.32), calls=%async_computation.4 | async-start | bytes 1048576 | tf_op jit(solution)/shard_map/all_to_all | solution.py:58
  100.1 2.9 %collective-permute-start.2 = (bf16[256,512]{1,0:T(8,128)(2,1)S(1)}, bf16[256,512]{1,0:T(8,128)(2,1)S(1)}, u32[]{:S(2)}, u32[]{:S(2)}) collective-permute-start(bf16[256,512]{1,0:T(8,128)(2,1)S(1)} %pad_maximum_fusion.1), channel_id=1, source_target_pairs={{0,64},{1,65},{2,66},{3,67},{4,68},{5,69},{6,70},{7,71},{8,72},{9,... | collective-permute-start | bytes 786440 | tf_op jit(solution)/shard_map/ppermute | solution.py:85
  103.0 11.1 %collective-permute-done.2 = bf16[256,512]{1,0:T(8,128)(2,1)S(1)} collective-permute-done((bf16[256,512]{1,0:T(8,128)(2,1)S(1)}, bf16[256,512]{1,0:T(8,128)(2,1)S(1)}, u32[]{:S(2)}, u32[]{:S(2)}) %collective-permute-start.2) | collective-permute-done | bytes 262176 | tf_op jit(solution)/shard_map/ppermute | solution.py:85
  114.1 0.7 copy-done.4
  114.8 0.9 pad_maximum_fusion
  116.0 5.1 %fusion.2 = bf16[128,2,3584]{2,0,1:T(8,128)(2,1)S(1)} fusion(bf16[1024,3584]{1,0:T(8,128)(2,1)} %param.27, bf16[128,2,1024]{2,1,0:T(2,128)(2,1)S(1)} %all-to-all-done.4), kind=kOutput, calls=%fused_computation.3 | convolution fusion | flops 1879965696 | bytes 9699328 | tf_op jit(solution)/shard_map/dsk,kn->dsn/dot_general | solution.py:73
  121.1 3.1 %copy.101 = bf16[128,2,3584]{2,1,0:T(2,128)(2,1)} copy(bf16[128,2,3584]{2,0,1:T(8,128)(2,1)S(1)} %fusion.2) | data formatting | bytes 3670016 | tf_op jit(solution)/shard_map/convert_element_type | solution.py:63
  124.3 9.5 %all-to-all-start.5 = ((bf16[128,2,3584]{2,1,0:T(2,128)(2,1)}), bf16[128,2,3584]{2,1,0:T(2,128)(2,1)S(1)}, u32[]{:S(2)}, u32[]{:S(2)}) async-start(bf16[128,2,3584]{2,1,0:T(2,128)(2,1)} %copy.101), calls=%async_computation.5 | async-start | bytes 3670016 | tf_op jit(solution)/shard_map/all_to_all | solution.py:63
  133.8 0.7 constant_dynamic-update-slice_fusion.17
  134.5 0.7 constant_dynamic-update-slice_fusion.16
  135.2 0.8 constant_dynamic-update-slice_fusion.15
  135.9 1.8 constant_dynamic-update-slice_fusion.14
  137.8 2.2 constant_dynamic-update-slice_fusion.13
  140.0 1.5 collective-permute-start.4
  141.4 37.4 %collective-permute-done.4 = bf16[1024,512]{1,0:T(8,128)(2,1)S(1)} collective-permute-done((bf16[1024,512]{1,0:T(8,128)(2,1)S(1)}, bf16[1024,512]{1,0:T(8,128)(2,1)S(1)}, u32[]{:S(2)}, u32[]{:S(2)}) %collective-permute-start.4) | collective-permute-done | bytes 1048608 | tf_op jit(solution)/shard_map/ppermute | solution.py:85
  178.9 1.6 constant_dynamic-update-slice_fusion.12
  180.4 2.0 copy-done.13
  182.6 2.9 reduce.6
  185.4 1.2 fusion.53
  186.7 2.2 broadcast_in_dim.136
  188.9 9.7 %all-to-all-start.6 = ((bf16[128,2,3584]{2,1,0:T(2,128)(2,1)}), bf16[128,2,3584]{2,1,0:T(2,128)(2,1)S(1)}, u32[]{:S(2)}, u32[]{:S(2)}) async-start(bf16[128,2,3584]{2,1,0:T(2,128)(2,1)} %bitcast.40), calls=%async_computation.6 | async-start | bytes 3670016 | tf_op jit(solution)/shard_map/all_to_all | solution.py:58
  199.2 44.8 %collective-permute-done.5 = bf16[2048,512]{1,0:T(8,128)(2,1)} collective-permute-done((bf16[2048,512]{1,0:T(8,128)(2,1)}, bf16[2048,512]{1,0:T(8,128)(2,1)}, u32[]{:S(2)}, u32[]{:S(2)}) %collective-permute-start.5) | collective-permute-done | bytes 2097184 | tf_op jit(solution)/shard_map/ppermute | solution.py:85
  244.0 3.9 %constant_dynamic-update-slice_fusion.11 = (bf16[4096,512]{1,0:T(8,128)(2,1)}, bf16[8192,512]{1,0:T(8,128)(2,1)}) fusion(bf16[4096,512]{1,0:T(8,128)(2,1)} %copy-done.13, bf16[2048,512]{1,0:T(8,128)(2,1)} %collective-permute-done.5, bf16[8192,512]{1,0:T(8,128)(2,1)} %get-tuple-element.13), kind=kLoop, calls=%fused_computation.89 | loop fusion | bytes 6291456 | tf_op jit(solution)/shard_map/concatenate | solution.py:85
  247.9 2.6 collective-permute-start.6
  251.1 1.7 all-to-all-done.6
  252.8 3.1 %fusion.26 = bf16[128,2,512]{2,0,1:T(8,128)(2,1)S(1)} fusion(bf16[3584,512]{1,0:T(8,128)(2,1)} %param.28, bf16[128,2,3584]{2,1,0:T(2,128)(2,1)S(1)} %all-to-all-done.6), kind=kOutput, calls=%fused_computation.17 | convolution fusion | flops 939655168 | bytes 5767168 | tf_op jit(solution)/shard_map/dsk,kn->dsn/dot_general | solution.py:73
  255.9 1.0 copy.103
  256.9 6.4 %all-to-all-start.7 = ((bf16[128,2,512]{2,1,0:T(2,128)(2,1)}), bf16[128,2,512]{2,1,0:T(2,128)(2,1)S(1)}, u32[]{:S(2)}, u32[]{:S(2)}) async-start(bf16[128,2,512]{2,1,0:T(2,128)(2,1)} %copy.103), calls=%async_computation.7 | async-start | bytes 524288 | tf_op jit(solution)/shard_map/all_to_all | solution.py:63
  264.1 10.7 %all-to-all-done.7 = bf16[128,2,512]{2,1,0:T(2,128)(2,1)S(1)} async-done(((bf16[128,2,512]{2,1,0:T(2,128)(2,1)}), bf16[128,2,512]{2,1,0:T(2,128)(2,1)S(1)}, u32[]{:S(2)}, u32[]{:S(2)}) %all-to-all-start.7) | async-done | bytes 262176 | tf_op jit(solution)/shard_map/all_to_all | solution.py:63
  275.6 0.7 gather_fusion
  276.5 0.7 add_convert_fusion.2
  277.2 4.4 %constant_dynamic-update-slice_fusion.18 = bf16[8192,512]{1,0:T(8,128)(2,1)} fusion(bf16[8192,512]{1,0:T(8,128)(2,1)} %get-tuple-element.11, bf16[4096,512]{1,0:T(8,128)(2,1)} %collective-permute-done.6), kind=kLoop, calls=%fused_computation.96 | loop fusion | bytes 8388608 | tf_op jit(solution)/shard_map/concatenate | solution.py:85
  281.6 4.6 %fusion.64 = f32[2,512]{1,0:T(2,128)S(1)} fusion(bf16[8192,512]{1,0:T(8,128)(2,1)} %constant_dynamic-update-slice_fusion.18, bf16[2,8192]{1,0:T(2,128)(2,1)S(1)} %gather.7, pred[8192]{0:T(1024)(128)(4,1)S(1)} %broadcast_in_dim.138), kind=kOutput, calls=%fused_computation.104 | convolution fusion | flops 16793600 | bytes 8433664 | tf_op jit(solution)/shard_map/dot_general | solution.py:102
  286.8 1.9 fusion.77
  290.0 1.3 fusion.78
  (95 shorter events, 6.3 us)
Async XLA Ops:
  0.6 29.5 %copy-start = (bf16[1024,640]{1,0:T(8,128)(2,1)S(1)}, bf16[1024,640]{1,0:T(8,128)(2,1)}, u32[]{:S(2)}) copy-start(bf16[1024,640]{1,0:T(8,128)(2,1)} %param.24) | copy-start | bytes 3932164
  1.5 19.9 %copy-start.8 = (f32[2,1,8192]{2,0,1:T(2,128)}, f32[2,1,8192]{2,0,1:T(2,128)S(1)}, u32[]{:S(2)}) copy-start(f32[2,1,8192]{2,0,1:T(2,128)S(1)} %convert_element_type.283) | copy-start | bytes 196612
  4.5 25.7 %all-to-all-start = ((bf16[128,2,1024]{2,1,0:T(2,128)(2,1)}), bf16[128,2,1024]{2,1,0:T(2,128)(2,1)}, u32[]{:S(2)}, u32[]{:S(2)}) async-start(bf16[128,2,1024]{2,1,0:T(2,128)(2,1)} %bitcast.3), calls=%async_computation | async-start | bytes 1048576 | tf_op jit(solution)/shard_map/all_to_all | solution.py:58
  16.4 3.0 %copy-start.1 = (bf16[1,1024,1024]{2,1,0:T(8,128)(2,1)S(1)}, bf16[1,1024,1024]{2,1,0:T(8,128)(2,1)}, u32[]{:S(2)}) copy-start(bf16[1,1024,1024]{2,1,0:T(8,128)(2,1)} %param.18) | copy-start | bytes 6291460
  32.8 16.9 %all-to-all-start.1 = ((bf16[128,2,640]{2,1,0:T(2,128)(2,1)}), bf16[128,2,640]{2,1,0:T(2,128)(2,1)}, u32[]{:S(2)}, u32[]{:S(2)}) async-start(bf16[128,2,640]{2,1,0:T(2,128)(2,1)} %copy.91), calls=%async_computation.1 | async-start | bytes 655360 | tf_op jit(solution)/shard_map/all_to_all | solution.py:63
  51.0 4.7 %copy-start.2 = (bf16[128,8,8,128]{3,2,1,0:T(8,128)(2,1)S(1)}, bf16[128,8,8,128]{3,2,1,0:T(8,128)(2,1)}, u32[]{:S(2)}) copy-start(bf16[128,8,8,128]{3,2,1,0:T(8,128)(2,1)} %copy.124) | copy-start | bytes 6291460
  53.6 2.8 copy-start.14
  55.7 25.8 %copy-start.5 = (bf16[64,512]{1,0:T(8,128)(2,1)S(1)}, bf16[64,512]{1,0:T(8,128)(2,1)}, u32[]{:S(2)}) copy-start(bf16[64,512]{1,0:T(8,128)(2,1)} %param.30) | copy-start | bytes 196612
  55.7 28.9 %copy-start.11 = (f32[8192]{0:T(1024)S(1)}, f32[8192]{0:T(1024)}, u32[]{:S(2)}) copy-start(f32[8192]{0:T(1024)} %param.26) | copy-start | bytes 98308
  56.4 37.0 %copy-start.3 = (bf16[2,1,8192]{2,0,1:T(2,128)(2,1)S(1)}, bf16[2,1,8192]{2,0,1:T(2,128)(2,1)}, u32[]{:S(2)}) copy-start(bf16[2,1,8192]{2,0,1:T(2,128)(2,1)} %param.16) | copy-start | bytes 98308
  56.4 37.2 %copy-start.9 = (f32[2,1,8192]{2,0,1:T(2,128)S(1)}, f32[2,1,8192]{2,0,1:T(2,128)}, u32[]{:S(2)}) copy-start(f32[2,1,8192]{2,0,1:T(2,128)} %copy-done.8) | copy-start | bytes 196612
  77.5 15.5 %all-to-all-start.3 = ((bf16[128,2,512]{2,1,0:T(2,128)(2,1)}), bf16[128,2,512]{2,1,0:T(2,128)(2,1)S(1)}, u32[]{:S(2)}, u32[]{:S(2)}) async-start(bf16[128,2,512]{2,1,0:T(2,128)(2,1)} %copy.97), calls=%async_computation.3 | async-start | bytes 524288 | tf_op jit(solution)/shard_map/all_to_all | solution.py:63
  81.5 5.6 %collective-permute-start = (bf16[64,512]{1,0:T(8,128)(2,1)S(1)}, bf16[64,512]{1,0:T(8,128)(2,1)S(1)}, u32[]{:S(2)}, u32[]{:S(2)}) collective-permute-start(bf16[64,512]{1,0:T(8,128)(2,1)S(1)} %copy-done.5), channel_id=1, source_target_pairs={{0,2},{1,3},{2,0},{3,1},{4,6},{5,7},{6,4},{7,5},{8,10},{9,11},{10,... | collective-permute-start | bytes 196616 | tf_op jit(solution)/shard_map/ppermute | solution.py:85
  87.1 12.9 %collective-permute-start.1 = (bf16[128,512]{1,0:T(8,128)(2,1)S(1)}, bf16[128,512]{1,0:T(8,128)(2,1)S(1)}, u32[]{:S(2)}, u32[]{:S(2)}) collective-permute-start(bf16[128,512]{1,0:T(8,128)(2,1)S(1)} %pad_maximum_fusion.2), channel_id=1, source_target_pairs={{0,8},{1,9},{2,10},{3,11},{4,12},{5,13},{6,14},{7,15},{8,0},{9,1},... | collective-permute-start | bytes 393224 | tf_op jit(solution)/shard_map/ppermute | solution.py:85
  93.4 27.8 %copy-start.6 = (f32[2,16,512]{2,1,0:T(8,128)}, f32[2,16,512]{2,1,0:T(8,128)S(1)}, u32[]{:S(2)}) copy-start(f32[2,16,512]{2,1,0:T(8,128)S(1)} %copy.98) | copy-start | bytes 196612
  94.8 21.2 %all-to-all-start.4 = ((bf16[128,2,1024]{2,1,0:T(2,128)(2,1)}), bf16[128,2,1024]{2,1,0:T(2,128)(2,1)S(1)}, u32[]{:S(2)}, u32[]{:S(2)}) async-start(bf16[128,2,1024]{2,1,0:T(2,128)(2,1)} %bitcast.32), calls=%async_computation.4 | async-start | bytes 1048576 | tf_op jit(solution)/shard_map/all_to_all | solution.py:58
  100.1 14.1 %collective-permute-start.2 = (bf16[256,512]{1,0:T(8,128)(2,1)S(1)}, bf16[256,512]{1,0:T(8,128)(2,1)S(1)}, u32[]{:S(2)}, u32[]{:S(2)}) collective-permute-start(bf16[256,512]{1,0:T(8,128)(2,1)S(1)} %pad_maximum_fusion.1), channel_id=1, source_target_pairs={{0,64},{1,65},{2,66},{3,67},{4,68},{5,69},{6,70},{7,71},{8,72},{9,... | collective-permute-start | bytes 786440 | tf_op jit(solution)/shard_map/ppermute | solution.py:85
  114.1 0.7 copy-start.4
  115.7 22.1 %collective-permute-start.3 = (bf16[512,512]{1,0:T(8,128)(2,1)}, bf16[512,512]{1,0:T(8,128)(2,1)}, u32[]{:S(2)}, u32[]{:S(2)}) collective-permute-start(bf16[512,512]{1,0:T(8,128)(2,1)} %pad_maximum_fusion), channel_id=1, source_target_pairs={{0,32},{1,33},{2,34},{3,35},{4,36},{5,37},{6,38},{7,39},{8,40},{9,... | collective-permute-start | bytes 1572872 | tf_op jit(solution)/shard_map/ppermute | solution.py:85
  124.3 58.3 %all-to-all-start.5 = ((bf16[128,2,3584]{2,1,0:T(2,128)(2,1)}), bf16[128,2,3584]{2,1,0:T(2,128)(2,1)S(1)}, u32[]{:S(2)}, u32[]{:S(2)}) async-start(bf16[128,2,3584]{2,1,0:T(2,128)(2,1)} %copy.101), calls=%async_computation.5 | async-start | bytes 3670016 | tf_op jit(solution)/shard_map/all_to_all | solution.py:63
  140.0 38.9 %collective-permute-start.4 = (bf16[1024,512]{1,0:T(8,128)(2,1)S(1)}, bf16[1024,512]{1,0:T(8,128)(2,1)S(1)}, u32[]{:S(2)}, u32[]{:S(2)}) collective-permute-start(bf16[1024,512]{1,0:T(8,128)(2,1)S(1)} %get-tuple-element.18), channel_id=1, source_target_pairs={{0,4},{1,5},{2,6},{3,7},{4,0},{5,1},{6,2},{7,3},{8,12},{9,13},{10,... | collective-permute-start | bytes 3145736 | tf_op jit(solution)/shard_map/ppermute | solution.py:85
  180.4 2.0 copy-start.13
  182.4 61.6 %collective-permute-start.5 = (bf16[2048,512]{1,0:T(8,128)(2,1)}, bf16[2048,512]{1,0:T(8,128)(2,1)}, u32[]{:S(2)}, u32[]{:S(2)}) collective-permute-start(bf16[2048,512]{1,0:T(8,128)(2,1)} %get-tuple-element.14), channel_id=1, source_target_pairs={{0,1},{1,0},{2,3},{3,2},{4,5},{5,4},{6,7},{7,6},{8,9},{9,8},{10,11... | collective-permute-start | bytes 6291464 | tf_op jit(solution)/shard_map/ppermute | solution.py:85
  188.9 61.6 %copy-start.15 = (s32[128]{0:T(128)S(1)}, s32[128]{0:T(128)}, u32[]{:S(2)}) copy-start(s32[128]{0:T(128)} %constant.56.clone) | copy-start | bytes 1540
  188.9 61.6 %copy-start.12 = (s32[512]{0:T(512)S(1)}, s32[512]{0:T(512)}, u32[]{:S(2)}) copy-start(s32[512]{0:T(512)} %param.21) | copy-start | bytes 6148
  188.9 61.6 %copy-start.16 = (s32[1,16]{1,0:T(1,128)S(1)}, s32[1,16]{1,0:T(1,128)}, u32[]{:S(2)}) copy-start(s32[1,16]{1,0:T(1,128)} %param.20) | copy-start | bytes 196
  188.9 63.9 %all-to-all-start.6 = ((bf16[128,2,3584]{2,1,0:T(2,128)(2,1)}), bf16[128,2,3584]{2,1,0:T(2,128)(2,1)S(1)}, u32[]{:S(2)}, u32[]{:S(2)}) async-start(bf16[128,2,3584]{2,1,0:T(2,128)(2,1)} %bitcast.40), calls=%async_computation.6 | async-start | bytes 3670016 | tf_op jit(solution)/shard_map/all_to_all | solution.py:58
  247.9 29.3 %collective-permute-start.6 = (bf16[4096,512]{1,0:T(8,128)(2,1)}, bf16[4096,512]{1,0:T(8,128)(2,1)}, u32[]{:S(2)}, u32[]{:S(2)}) collective-permute-start(bf16[4096,512]{1,0:T(8,128)(2,1)} %get-tuple-element.10), channel_id=1, source_target_pairs={{0,16},{1,17},{2,18},{3,19},{4,20},{5,21},{6,22},{7,23},{8,24},{9,... | collective-permute-start | bytes 12582920 | tf_op jit(solution)/shard_map/ppermute | solution.py:85
  251.1 12.4 %copy-start.10 = (f32[8192]{0:T(1024)S(1)}, f32[8192]{0:T(1024)}, u32[]{:S(2)}) copy-start(f32[8192]{0:T(1024)} %param.29) | copy-start | bytes 98308
  251.1 12.8 %copy-start.7 = (f32[2,16,512]{2,1,0:T(8,128)S(1)}, f32[2,16,512]{2,1,0:T(8,128)}, u32[]{:S(2)}) copy-start(f32[2,16,512]{2,1,0:T(8,128)} %copy-done.6) | copy-start | bytes 196612
  256.9 17.8 %all-to-all-start.7 = ((bf16[128,2,512]{2,1,0:T(2,128)(2,1)}), bf16[128,2,512]{2,1,0:T(2,128)(2,1)S(1)}, u32[]{:S(2)}, u32[]{:S(2)}) async-start(bf16[128,2,512]{2,1,0:T(2,128)(2,1)} %copy.103), calls=%async_computation.7 | async-start | bytes 524288 | tf_op jit(solution)/shard_map/all_to_all | solution.py:63

commit v6 on v5

--- a/solution.py
+++ b/solution.py
@@ -67,23 +67,36 @@
     return summed.transpose(1, 0, 2).reshape(rows_here, (devices // groups) * width)
 
 
-def project(inputs, weight, link_type=jnp.bfloat16):
+def project(inputs, weight, tie_in, tie_out, link_type=jnp.bfloat16):
     groups = lax.psum(1, "gx")
-    spread = spread_rows(inputs, groups)
+    spread = spread_rows(tie_in(inputs), groups)
     partial = jnp.einsum("dsk,kn->dsn", spread, weight, preferred_element_type=jnp.float32)
-    return gather_rows(partial, groups, link_type).astype(jnp.bfloat16)
+    return gather_rows(tie_out(partial), groups, link_type).astype(jnp.bfloat16)
 
 
 SHIFT_ORDER = (2, 8, 64, 32, 4, 1, 16)
 
 
-def gather_weight(shard):
-    devices = lax.psum(1, ALL)
-    held = shard
-    for step in SHIFT_ORDER:
+class WeightGather:
+    def __init__(self, shard):
+        self.held = shard
+        self.done = 0
+
+    def tie(self, value):
+        if self.done == len(SHIFT_ORDER):
+            return value
+        devices = lax.psum(1, ALL)
+        step = SHIFT_ORDER[self.done]
         pairs = [(i, i ^ step) for i in range(devices)]
-        held = jnp.concatenate([held, lax.ppermute(held, ALL, pairs)], axis=0)
-    return held
+        grown = jnp.concatenate([self.held, lax.ppermute(self.held, ALL, pairs)], axis=0)
+        self.held, value = lax.optimization_barrier((grown, value))
+        self.done += 1
+        return value
+
+    def result(self):
+        while self.done < len(SHIFT_ORDER):
+            self.tie(jnp.zeros((), jnp.float32))
+        return self.held
 
 
 def held_order():
@@ -182,25 +195,30 @@
     q_width = HEADS * HEAD
     kv_width = KV_HEADS * HEAD
     steps = hidden_in.shape[0]
-    lm_full = gather_weight(lm_weight)
+    lm_gather = WeightGather(lm_weight)
+    tie = lm_gather.tie
+
+    def keep(value):
+        return value
+
     layer_in = hidden_in[:, 0, :]
     positions = lengths[0] + jnp.arange(steps, dtype=jnp.int32)
-    mixed = project(norm_rows(layer_in, attn_gain), qkv_weight)
+    mixed = project(norm_rows(layer_in, attn_gain), qkv_weight, keep, tie)
     queries = rotate(mixed[:, :q_width].reshape(-1, HEADS, HEAD), positions).reshape(-1, q_width)
     keys_now = rotate(
         mixed[:, q_width : q_width + kv_width].reshape(-1, KV_HEADS, HEAD), positions
     ).reshape(-1, kv_width)
     values_now = mixed[:, q_width + kv_width :]
     attended = attend(queries, k_cache[0], v_cache[0], lengths, keys_now, values_now)
-    projected = project(attended, o_weight)
+    projected = project(attended, o_weight, tie, tie)
     residual = (layer_in.astype(jnp.float32) + projected.astype(jnp.float32)).astype(jnp.bfloat16)
-    gate_up = project(norm_rows(residual, ffn_gain), gate_up_weight)
+    gate_up = project(norm_rows(residual, ffn_gain), gate_up_weight, tie, tie)
     hidden_units = (
         jax.nn.silu(gate_up[:, :FF].astype(jnp.float32)) * gate_up[:, FF:].astype(jnp.float32)
     ).astype(jnp.bfloat16)
-    lowered = project(hidden_units, down_weight)
+    lowered = project(hidden_units, down_weight, tie, tie)
     result = (residual.astype(jnp.float32) + lowered.astype(jnp.float32)).astype(jnp.bfloat16)
-    logits = head_logits(norm_rows(result, final_gain), lm_full)
+    logits = head_logits(norm_rows(result, final_gain), lm_gather.result())
     remaining = counts.astype(jnp.float32)
     first_log = masked_log_probs(logits[0:1], remaining, token_elem)
     remaining = remaining - used_elements(tokens, token_elem)

time: 293 us -> 307 us (1.048)
  waiting for transfers between devices: 129 us -> 155 us
  blocking collectives: 17.8 us -> 0 us
  local copies, waits for them, and re-layouts: 36.5 us -> 18.8 us
  starting transfers between devices: 66.4 us -> 79.9 us
  other arithmetic: 18.4 us -> 30.9 us
    all_to_all x3 -> x4, waiting for transfers between devices: 9.84 us -> 42.9 us  [spread_rows(): return lax.all_to_all(send, ALL, 0, 0, tiled=True)]
    ppermute x7, waiting for transfers between devices: 95.8 us -> 63.9 us  [tie(): lax.ppermute(self.held, ALL, pairs)]
    all_to_all x4, waiting for transfers between devices: 23.6 us -> 47.8 us  [gather_rows(): got = lax.all_to_all(partial.astype(link_type), ALL, 0, 0, tiled=True)]
    all_to_all x1 -> x0, blocking collectives: 17.8 us -> none  [spread_rows(): return lax.all_to_all(send, ALL, 0, 0, tiled=True)]
    concatenate x3 -> x7, other arithmetic: 0.89 us -> 14.4 us  [tie(): jnp.concatenate([self.held, lax.ppermute(self.held, ALL, pairs)], axis=0)]
    unnamed x43 -> x32, local copies, waits for them, and re-layouts: 14.6 us -> 4.49 us
    all_to_all x3 -> x4, starting transfers between devices: 26.8 us -> 36.5 us  [spread_rows(): return lax.all_to_all(send, ALL, 0, 0, tiled=True)]
    concatenate x2 -> x0, local copies, waits for them, and re-layouts: 8.31 us -> none  [gather_weight(): held = jnp.concatenate([held, lax.ppermute(held, ALL, pairs)], axis=0)]
  transfers between devices with their start and end apart: 14 -> 15, of which waited for: 9 -> 14; matrix products, arithmetic and copies ran while one was open for 14% -> 8% of each run, Pallas kernels for 0% -> 0%
where the time goes in v6:
time: 307 us; the launch traced here: 306 us
  waiting for transfers between devices  155 us (50%)
  starting transfers between devices  79.9 us (26%)
  other arithmetic  30.9 us (10%)
  local copies, waits for them, and re-layouts  18.8 us (6%)
  matrix products  17.8 us (6%)
  between operations  3.75 us (1%)
    ppermute x7, waiting for transfers between devices, tie(): lax.ppermute(self.held, ALL, pairs)  63.9 us
    all_to_all x4, waiting for transfers between devices, gather_rows(): got = lax.all_to_all(partial.astype(link_type), ALL, 0, 0, tiled=True)  47.8 us
    all_to_all x4, waiting for transfers between devices, spread_rows(): return lax.all_to_all(send, ALL, 0, 0, tiled=True)  42.9 us
    all_to_all x4, starting transfers between devices, spread_rows(): return lax.all_to_all(send, ALL, 0, 0, tiled=True)  36.5 us
    all_to_all x4, starting transfers between devices, gather_rows(): got = lax.all_to_all(partial.astype(link_type), ALL, 0, 0, tiled=True)  28.7 us
    ppermute x7, starting transfers between devices, tie(): lax.ppermute(self.held, ALL, pairs)  14.8 us
    concatenate x7, other arithmetic, tie(): jnp.concatenate([self.held, lax.ppermute(self.held, ALL, pairs)], axis=0)  14.4 us
    dot_general x4, matrix products, project(): jnp.einsum('dsk,kn->dsn', spread, weight, preferred_element_type=jnp.floa...  10.5 us
  transfers between devices with their start and end apart: 15, of which 14 were waited for; matrix products, arithmetic and copies ran while one was open for 8% of the time, Pallas kernels for 0%

profile of v6, /device:TPU:1, one launch (start us, length us, event | category | flops | bytes accessed | tf_op | source)
XLA Modules:
  0.0 305.8 jit_solution(6203763890450995450)
XLA Ops:
  0.6 0.9 convert_element_type.264
  1.5 0.9 fusion.53
  2.5 0.8 mul.180
  3.4 1.1 broadcast_in_dim.126
  4.4 11.5 %all-to-all-start = ((bf16[128,2,1024]{2,1,0:T(2,128)(2,1)}), bf16[128,2,1024]{2,1,0:T(2,128)(2,1)S(1)}, u32[]{:S(2)}, u32[]{:S(2)}) async-start(bf16[128,2,1024]{2,1,0:T(2,128)(2,1)} %bitcast.2), calls=%async_computation | async-start | bytes 1048576 | tf_op jit(solution)/shard_map/all_to_all | solution.py:58
  15.9 2.9 collective-permute-start
  19.7 3.9 %collective-permute-done = bf16[64,512]{1,0:T(8,128)(2,1)S(1)} collective-permute-done((bf16[64,512]{1,0:T(8,128)(2,1)}, bf16[64,512]{1,0:T(8,128)(2,1)S(1)}, u32[]{:S(2)}, u32[]{:S(2)}) %collective-permute-start) | collective-permute-done | bytes 65568 | tf_op jit(solution)/shard_map/ppermute | solution.py:91
  23.5 0.8 pad_maximum_fusion.6
  24.4 5.6 %all-to-all-done = bf16[128,2,1024]{2,1,0:T(2,128)(2,1)S(1)} async-done(((bf16[128,2,1024]{2,1,0:T(2,128)(2,1)}), bf16[128,2,1024]{2,1,0:T(2,128)(2,1)S(1)}, u32[]{:S(2)}, u32[]{:S(2)}) %all-to-all-start) | async-done | bytes 524320 | tf_op jit(solution)/shard_map/all_to_all | solution.py:58
  30.0 0.6 fusion.9
  30.6 1.1 copy.73
  31.6 5.4 %all-to-all-start.1 = ((bf16[128,2,640]{2,1,0:T(2,128)(2,1)}), bf16[128,2,640]{2,1,0:T(2,128)(2,1)}, u32[]{:S(2)}, u32[]{:S(2)}) async-start(bf16[128,2,640]{2,1,0:T(2,128)(2,1)} %copy.73), calls=%async_computation.1 | async-start | bytes 655360 | tf_op jit(solution)/shard_map/all_to_all | solution.py:63
  37.0 3.3 %collective-permute-start.1 = (bf16[128,512]{1,0:T(8,128)(2,1)S(1)}, bf16[128,512]{1,0:T(8,128)(2,1)S(1)}, u32[]{:S(2)}, u32[]{:S(2)}) collective-permute-start(bf16[128,512]{1,0:T(8,128)(2,1)S(1)} %pad_maximum_fusion.6), channel_id=1, source_target_pairs={{0,8},{1,9},{2,10},{3,11},{4,12},{5,13},{6,14},{7,15},{8,0},{9,1},... | collective-permute-start | bytes 393224 | tf_op jit(solution)/shard_map/ppermute | solution.py:91
  40.4 2.4 copy.106
  42.7 2.0 copy.107
  44.7 1.7 collective-permute-done.1
  46.4 0.7 pad_maximum_fusion.5
  47.1 1.7 all-to-all-done.1
  48.8 1.3 reduce.4
  50.4 0.8 fusion.81
  51.9 0.7 fusion.21
  53.0 1.1 broadcast_in_dim.134
  54.1 6.1 %all-to-all-start.2 = ((bf16[128,2,1024]{2,1,0:T(2,128)(2,1)}), bf16[128,2,1024]{2,1,0:T(2,128)(2,1)S(1)}, u32[]{:S(2)}, u32[]{:S(2)}) async-start(bf16[128,2,1024]{2,1,0:T(2,128)(2,1)} %bitcast.25), calls=%async_computation.2 | async-start | bytes 1048576 | tf_op jit(solution)/shard_map/all_to_all | solution.py:58
  60.2 2.9 collective-permute-start.2
  63.1 11.1 %collective-permute-done.2 = bf16[256,512]{1,0:T(8,128)(2,1)S(1)} collective-permute-done((bf16[256,512]{1,0:T(8,128)(2,1)S(1)}, bf16[256,512]{1,0:T(8,128)(2,1)S(1)}, u32[]{:S(2)}, u32[]{:S(2)}) %collective-permute-start.2) | collective-permute-done | bytes 262176 | tf_op jit(solution)/shard_map/ppermute | solution.py:91
  74.4 1.7 fusion.29
  76.1 1.0 copy.81
  77.1 8.3 %all-to-all-start.3 = ((bf16[128,2,512]{2,1,0:T(2,128)(2,1)}), bf16[128,2,512]{2,1,0:T(2,128)(2,1)S(1)}, u32[]{:S(2)}, u32[]{:S(2)}) async-start(bf16[128,2,512]{2,1,0:T(2,128)(2,1)} %copy.81), calls=%async_computation.3 | async-start | bytes 524288 | tf_op jit(solution)/shard_map/all_to_all | solution.py:63
  85.3 1.4 collective-permute-start.3
  86.8 10.4 %all-to-all-done.3 = bf16[128,2,512]{2,1,0:T(2,128)(2,1)S(1)} async-done(((bf16[128,2,512]{2,1,0:T(2,128)(2,1)}), bf16[128,2,512]{2,1,0:T(2,128)(2,1)S(1)}, u32[]{:S(2)}, u32[]{:S(2)}) %all-to-all-start.3) | async-done | bytes 262176 | tf_op jit(solution)/shard_map/all_to_all | solution.py:63
  97.4 0.7 convert_bitcast_fusion.2
  98.4 2.4 collective-permute-done.3
  100.9 1.1 broadcast_in_dim.135
  102.0 9.9 %all-to-all-start.4 = ((bf16[128,2,1024]{2,1,0:T(2,128)(2,1)}), bf16[128,2,1024]{2,1,0:T(2,128)(2,1)S(1)}, u32[]{:S(2)}, u32[]{:S(2)}) async-start(bf16[128,2,1024]{2,1,0:T(2,128)(2,1)} %bitcast.32), calls=%async_computation.4 | async-start | bytes 1048576 | tf_op jit(solution)/shard_map/all_to_all | solution.py:58
  111.9 1.7 collective-permute-start.4
  113.6 12.3 %all-to-all-done.4 = bf16[128,2,1024]{2,1,0:T(2,128)(2,1)S(1)} async-done(((bf16[128,2,1024]{2,1,0:T(2,128)(2,1)}), bf16[128,2,1024]{2,1,0:T(2,128)(2,1)S(1)}, u32[]{:S(2)}, u32[]{:S(2)}) %all-to-all-start.4) | async-done | bytes 524320 | tf_op jit(solution)/shard_map/all_to_all | solution.py:58
  125.9 5.1 %fusion = bf16[128,2,3584]{2,0,1:T(8,128)(2,1)S(1)} fusion(bf16[1024,3584]{1,0:T(8,128)(2,1)} %param.27, bf16[128,2,1024]{2,1,0:T(2,128)(2,1)S(1)} %all-to-all-done.4), kind=kOutput, calls=%fused_computation.2 | convolution fusion | flops 1879048192 | bytes 9699328 | tf_op jit(solution)/shard_map/dsk,kn->dsn/dot_general | solution.py:73
  131.1 10.8 %collective-permute-done.4 = bf16[1024,512]{1,0:T(8,128)(2,1)} collective-permute-done((bf16[1024,512]{1,0:T(8,128)(2,1)S(1)}, bf16[1024,512]{1,0:T(8,128)(2,1)}, u32[]{:S(2)}, u32[]{:S(2)}) %collective-permute-start.4) | collective-permute-done | bytes 1048608 | tf_op jit(solution)/shard_map/ppermute | solution.py:91
  141.9 1.7 pad_maximum_fusion.2
  143.5 3.2 %copy.84 = bf16[128,2,3584]{2,1,0:T(2,128)(2,1)} copy(bf16[128,2,3584]{2,0,1:T(8,128)(2,1)S(1)} %fusion) | data formatting | bytes 3670016 | tf_op jit(solution)/shard_map/convert_element_type | solution.py:63
  146.7 10.1 %all-to-all-start.5 = ((bf16[128,2,3584]{2,1,0:T(2,128)(2,1)}), bf16[128,2,3584]{2,1,0:T(2,128)(2,1)}, u32[]{:S(2)}, u32[]{:S(2)}) async-start(bf16[128,2,3584]{2,1,0:T(2,128)(2,1)} %copy.84), calls=%async_computation.5 | async-start | bytes 3670016 | tf_op jit(solution)/shard_map/all_to_all | solution.py:63
  156.8 1.4 collective-permute-start.5
  158.2 24.9 %all-to-all-done.5 = bf16[128,2,3584]{2,1,0:T(2,128)(2,1)} async-done(((bf16[128,2,3584]{2,1,0:T(2,128)(2,1)}), bf16[128,2,3584]{2,1,0:T(2,128)(2,1)}, u32[]{:S(2)}, u32[]{:S(2)}) %all-to-all-start.5) | async-done | bytes 1835040 | tf_op jit(solution)/shard_map/all_to_all | solution.py:63
  183.1 4.0 %reduce.6 = bf16[16,2,3584]{2,1,0:T(2,128)(2,1)} reduce(bf16[8,16,2,3584]{3,2,1,0:T(2,128)(2,1)} %bitcast.34, bf16[]{:T(256)} %constant.64), dimensions={0}, to_apply=%region_8.9.clone | reduce | flops 802816 | bytes 2064386 | tf_op jit(solution)/shard_map/reduce_sum | solution.py:64
  187.1 1.2 fusion.43
  188.4 34.1 %collective-permute-done.5 = bf16[2048,512]{1,0:T(8,128)(2,1)} collective-permute-done((bf16[2048,512]{1,0:T(8,128)(2,1)S(1)}, bf16[2048,512]{1,0:T(8,128)(2,1)}, u32[]{:S(2)}, u32[]{:S(2)}) %collective-permute-start.5) | collective-permute-done | bytes 2097184 | tf_op jit(solution)/shard_map/ppermute | solution.py:91
  222.4 3.8 %pad_maximum_fusion.1 = bf16[4096,512]{1,0:T(8,128)(2,1)} fusion(bf16[2048,512]{1,0:T(8,128)(2,1)} %collective-permute-done.5, bf16[2048,512]{1,0:T(8,128)(2,1)S(1)} %pad_maximum_fusion.2), kind=kLoop, calls=%fused_computation.4 | loop fusion | flops 8388608 | bytes 8388608 | tf_op jit(solution)/shard_map/concatenate | solution.py:91
  226.2 1.0 collective-permute-start.6
  227.2 2.2 broadcast_in_dim.136
  229.4 9.1 %all-to-all-start.6 = ((bf16[128,2,3584]{2,1,0:T(2,128)(2,1)}), bf16[128,2,3584]{2,1,0:T(2,128)(2,1)S(1)}, u32[]{:S(2)}, u32[]{:S(2)}) async-start(bf16[128,2,3584]{2,1,0:T(2,128)(2,1)} %bitcast.40), calls=%async_computation.6 | async-start | bytes 3670016 | tf_op jit(solution)/shard_map/all_to_all | solution.py:58
  239.2 0.5 compare_and_fusion
  240.3 24.8 %all-to-all-done.6 = bf16[128,2,3584]{2,1,0:T(2,128)(2,1)S(1)} async-done(((bf16[128,2,3584]{2,1,0:T(2,128)(2,1)}), bf16[128,2,3584]{2,1,0:T(2,128)(2,1)S(1)}, u32[]{:S(2)}, u32[]{:S(2)}) %all-to-all-start.6) | async-done | bytes 1835040 | tf_op jit(solution)/shard_map/all_to_all | solution.py:58
  265.1 3.1 %fusion.2 = bf16[128,2,512]{2,0,1:T(8,128)(2,1)S(1)} fusion(bf16[3584,512]{1,0:T(8,128)(2,1)} %param.28, bf16[128,2,3584]{2,1,0:T(2,128)(2,1)S(1)} %all-to-all-done.6), kind=kOutput, calls=%fused_computation.5 | convolution fusion | flops 939524096 | bytes 5767168 | tf_op jit(solution)/shard_map/dsk,kn->dsn/dot_general | solution.py:73
  268.3 7.2 %pad_maximum_fusion = bf16[8192,512]{1,0:T(8,128)(2,1)} fusion(bf16[4096,512]{1,0:T(8,128)(2,1)} %collective-permute-done.6, bf16[4096,512]{1,0:T(8,128)(2,1)} %pad_maximum_fusion.1), kind=kLoop, calls=%fused_computation.1 | loop fusion | flops 16777216 | bytes 16777216 | tf_op jit(solution)/shard_map/concatenate | solution.py:91
  275.6 1.0 copy.86
  276.6 5.0 %all-to-all-start.7 = ((bf16[128,2,512]{2,1,0:T(2,128)(2,1)}), bf16[128,2,512]{2,1,0:T(2,128)(2,1)S(1)}, u32[]{:S(2)}, u32[]{:S(2)}) async-start(bf16[128,2,512]{2,1,0:T(2,128)(2,1)} %copy.86), calls=%async_computation.7 | async-start | bytes 524288 | tf_op jit(solution)/shard_map/all_to_all | solution.py:63
  282.3 10.8 %all-to-all-done.7 = bf16[128,2,512]{2,1,0:T(2,128)(2,1)S(1)} async-done(((bf16[128,2,512]{2,1,0:T(2,128)(2,1)}), bf16[128,2,512]{2,1,0:T(2,128)(2,1)S(1)}, u32[]{:S(2)}, u32[]{:S(2)}) %all-to-all-start.7) | async-done | bytes 262176 | tf_op jit(solution)/shard_map/all_to_all | solution.py:63
  294.0 0.7 gather_fusion
  294.9 4.6 %fusion.55 = f32[2,512]{1,0:T(2,128)S(1)} fusion(bf16[8192,512]{1,0:T(8,128)(2,1)} %pad_maximum_fusion, bf16[2,8192]{1,0:T(2,128)(2,1)S(1)} %gather.7, pred[8192]{0:T(1024)(128)(4,1)S(1)} %broadcast_in_dim.138), kind=kOutput, calls=%fused_computation.79 | convolution fusion | flops 16793600 | bytes 8433664 | tf_op jit(solution)/shard_map/dot_general | solution.py:115
  299.4 0.6 fusion.66
  300.1 1.9 fusion.67
  303.2 1.3 fusion.68
  304.5 0.6 pad_maximum_fusion.8
  305.1 0.7 add_convert_fusion.2
  (86 shorter events, 4.8 us)
Async XLA Ops:
  0.6 29.4 %copy-start = (bf16[1024,640]{1,0:T(8,128)(2,1)S(1)}, bf16[1024,640]{1,0:T(8,128)(2,1)}, u32[]{:S(2)}) copy-start(bf16[1024,640]{1,0:T(8,128)(2,1)} %param.24) | copy-start | bytes 3932164
  4.4 25.5 %all-to-all-start = ((bf16[128,2,1024]{2,1,0:T(2,128)(2,1)}), bf16[128,2,1024]{2,1,0:T(2,128)(2,1)S(1)}, u32[]{:S(2)}, u32[]{:S(2)}) async-start(bf16[128,2,1024]{2,1,0:T(2,128)(2,1)} %bitcast.2), calls=%async_computation | async-start | bytes 1048576 | tf_op jit(solution)/shard_map/all_to_all | solution.py:58
  15.9 7.6 %collective-permute-start = (bf16[64,512]{1,0:T(8,128)(2,1)}, bf16[64,512]{1,0:T(8,128)(2,1)S(1)}, u32[]{:S(2)}, u32[]{:S(2)}) collective-permute-start(bf16[64,512]{1,0:T(8,128)(2,1)} %param.30), channel_id=1, source_target_pairs={{0,2},{1,3},{2,0},{3,1},{4,6},{5,7},{6,4},{7,5},{8,10},{9,11},{10,... | collective-permute-start | bytes 196616 | tf_op jit(solution)/shard_map/ppermute | solution.py:91
  31.6 17.2 %all-to-all-start.1 = ((bf16[128,2,640]{2,1,0:T(2,128)(2,1)}), bf16[128,2,640]{2,1,0:T(2,128)(2,1)}, u32[]{:S(2)}, u32[]{:S(2)}) async-start(bf16[128,2,640]{2,1,0:T(2,128)(2,1)} %copy.73), calls=%async_computation.1 | async-start | bytes 655360 | tf_op jit(solution)/shard_map/all_to_all | solution.py:63
  37.0 9.4 %collective-permute-start.1 = (bf16[128,512]{1,0:T(8,128)(2,1)S(1)}, bf16[128,512]{1,0:T(8,128)(2,1)S(1)}, u32[]{:S(2)}, u32[]{:S(2)}) collective-permute-start(bf16[128,512]{1,0:T(8,128)(2,1)S(1)} %pad_maximum_fusion.6), channel_id=1, source_target_pairs={{0,8},{1,9},{2,10},{3,11},{4,12},{5,13},{6,14},{7,15},{8,0},{9,1},... | collective-permute-start | bytes 393224 | tf_op jit(solution)/shard_map/ppermute | solution.py:91
  40.4 2.4 copy-start.2
  50.3 1.6 copy-start.3
  52.6 7.5 %copy-start.4 = (bf16[256,512]{1,0:T(8,128)(2,1)S(1)}, bf16[256,512]{1,0:T(8,128)(2,1)}, u32[]{:S(2)}) copy-start(bf16[256,512]{1,0:T(8,128)(2,1)} %pad_maximum_fusion.5) | copy-start | bytes 786436
  54.1 20.3 %all-to-all-start.2 = ((bf16[128,2,1024]{2,1,0:T(2,128)(2,1)}), bf16[128,2,1024]{2,1,0:T(2,128)(2,1)S(1)}, u32[]{:S(2)}, u32[]{:S(2)}) async-start(bf16[128,2,1024]{2,1,0:T(2,128)(2,1)} %bitcast.25), calls=%async_computation.2 | async-start | bytes 1048576 | tf_op jit(solution)/shard_map/all_to_all | solution.py:58
  60.2 37.9 %copy-start.5 = (bf16[2,1,8192]{2,0,1:T(2,128)(2,1)S(1)}, bf16[2,1,8192]{2,0,1:T(2,128)(2,1)}, u32[]{:S(2)}) copy-start(bf16[2,1,8192]{2,0,1:T(2,128)(2,1)} %param.16) | copy-start | bytes 98308
  60.2 14.1 %collective-permute-start.2 = (bf16[256,512]{1,0:T(8,128)(2,1)S(1)}, bf16[256,512]{1,0:T(8,128)(2,1)S(1)}, u32[]{:S(2)}, u32[]{:S(2)}) collective-permute-start(bf16[256,512]{1,0:T(8,128)(2,1)S(1)} %copy-done.4), channel_id=1, source_target_pairs={{0,64},{1,65},{2,66},{3,67},{4,68},{5,69},{6,70},{7,71},{8,72},{9,... | collective-permute-start | bytes 786440 | tf_op jit(solution)/shard_map/ppermute | solution.py:91
  74.3 23.9 %copy-start.7 = (f32[8192]{0:T(1024)S(1)}, f32[8192]{0:T(1024)}, u32[]{:S(2)}) copy-start(f32[8192]{0:T(1024)} %param.26) | copy-start | bytes 98308
  77.1 20.1 %all-to-all-start.3 = ((bf16[128,2,512]{2,1,0:T(2,128)(2,1)}), bf16[128,2,512]{2,1,0:T(2,128)(2,1)S(1)}, u32[]{:S(2)}, u32[]{:S(2)}) async-start(bf16[128,2,512]{2,1,0:T(2,128)(2,1)} %copy.81), calls=%async_computation.3 | async-start | bytes 524288 | tf_op jit(solution)/shard_map/all_to_all | solution.py:63
  85.3 15.4 %collective-permute-start.3 = (bf16[512,512]{1,0:T(8,128)(2,1)S(1)}, bf16[512,512]{1,0:T(8,128)(2,1)S(1)}, u32[]{:S(2)}, u32[]{:S(2)}) collective-permute-start(bf16[512,512]{1,0:T(8,128)(2,1)S(1)} %pad_maximum_fusion.4), channel_id=1, source_target_pairs={{0,32},{1,33},{2,34},{3,35},{4,36},{5,37},{6,38},{7,39},{8,40},{9,... | collective-permute-start | bytes 1572872 | tf_op jit(solution)/shard_map/ppermute | solution.py:91
  100.8 30.3 %copy-start.1 = (bf16[1024,512]{1,0:T(8,128)(2,1)}, bf16[1024,512]{1,0:T(8,128)(2,1)S(1)}, u32[]{:S(2)}) copy-start(bf16[1024,512]{1,0:T(8,128)(2,1)S(1)} %pad_maximum_fusion.3) | copy-start | bytes 3145732
  102.0 24.0 %all-to-all-start.4 = ((bf16[128,2,1024]{2,1,0:T(2,128)(2,1)}), bf16[128,2,1024]{2,1,0:T(2,128)(2,1)S(1)}, u32[]{:S(2)}, u32[]{:S(2)}) async-start(bf16[128,2,1024]{2,1,0:T(2,128)(2,1)} %bitcast.32), calls=%async_computation.4 | async-start | bytes 1048576 | tf_op jit(solution)/shard_map/all_to_all | solution.py:58
  111.9 30.0 %collective-permute-start.4 = (bf16[1024,512]{1,0:T(8,128)(2,1)S(1)}, bf16[1024,512]{1,0:T(8,128)(2,1)}, u32[]{:S(2)}, u32[]{:S(2)}) collective-permute-start(bf16[1024,512]{1,0:T(8,128)(2,1)S(1)} %pad_maximum_fusion.3), channel_id=1, source_target_pairs={{0,4},{1,5},{2,6},{3,7},{4,0},{5,1},{6,2},{7,3},{8,12},{9,13},{10,... | collective-permute-start | bytes 3145736 | tf_op jit(solution)/shard_map/ppermute | solution.py:91
  146.7 36.4 %all-to-all-start.5 = ((bf16[128,2,3584]{2,1,0:T(2,128)(2,1)}), bf16[128,2,3584]{2,1,0:T(2,128)(2,1)}, u32[]{:S(2)}, u32[]{:S(2)}) async-start(bf16[128,2,3584]{2,1,0:T(2,128)(2,1)} %copy.84), calls=%async_computation.5 | async-start | bytes 3670016 | tf_op jit(solution)/shard_map/all_to_all | solution.py:63
  156.8 65.7 %collective-permute-start.5 = (bf16[2048,512]{1,0:T(8,128)(2,1)S(1)}, bf16[2048,512]{1,0:T(8,128)(2,1)}, u32[]{:S(2)}, u32[]{:S(2)}) collective-permute-start(bf16[2048,512]{1,0:T(8,128)(2,1)S(1)} %pad_maximum_fusion.2), channel_id=1, source_target_pairs={{0,1},{1,0},{2,3},{3,2},{4,5},{5,4},{6,7},{7,6},{8,9},{9,8},{10,11... | collective-permute-start | bytes 6291464 | tf_op jit(solution)/shard_map/ppermute | solution.py:91
  226.2 42.1 %collective-permute-start.6 = (bf16[4096,512]{1,0:T(8,128)(2,1)}, bf16[4096,512]{1,0:T(8,128)(2,1)}, u32[]{:S(2)}, u32[]{:S(2)}) collective-permute-start(bf16[4096,512]{1,0:T(8,128)(2,1)} %pad_maximum_fusion.1), channel_id=1, source_target_pairs={{0,16},{1,17},{2,18},{3,19},{4,20},{5,21},{6,22},{7,23},{8,24},{9,... | collective-permute-start | bytes 12582920 | tf_op jit(solution)/shard_map/ppermute | solution.py:91
  229.4 9.8 %copy-start.11 = (s32[128]{0:T(128)S(1)}, s32[128]{0:T(128)}, u32[]{:S(2)}) copy-start(s32[128]{0:T(128)} %constant.56.clone) | copy-start | bytes 1540
  229.4 10.3 %copy-start.9 = (s32[512]{0:T(512)S(1)}, s32[512]{0:T(512)}, u32[]{:S(2)}) copy-start(s32[512]{0:T(512)} %param.21) | copy-start | bytes 6148
  229.4 10.3 %copy-start.12 = (s32[1,16]{1,0:T(1,128)S(1)}, s32[1,16]{1,0:T(1,128)}, u32[]{:S(2)}) copy-start(s32[1,16]{1,0:T(1,128)} %param.20) | copy-start | bytes 196
  229.4 35.7 %all-to-all-start.6 = ((bf16[128,2,3584]{2,1,0:T(2,128)(2,1)}), bf16[128,2,3584]{2,1,0:T(2,128)(2,1)S(1)}, u32[]{:S(2)}, u32[]{:S(2)}) async-start(bf16[128,2,3584]{2,1,0:T(2,128)(2,1)} %bitcast.40), calls=%async_computation.6 | async-start | bytes 3670016 | tf_op jit(solution)/shard_map/all_to_all | solution.py:58
  268.3 13.2 %copy-start.10 = (s32[128]{0:T(128)S(1)}, s32[128]{0:T(128)}, u32[]{:S(2)}) copy-start(s32[128]{0:T(128)} %get-tuple-element.35) | copy-start | bytes 1540
  268.3 13.4 %copy-start.8 = (f32[8192]{0:T(1024)S(1)}, f32[8192]{0:T(1024)}, u32[]{:S(2)}) copy-start(f32[8192]{0:T(1024)} %param.29) | copy-start | bytes 98308
  268.3 13.8 %copy-start.6 = (f32[2,16,512]{2,0,1:T(2,128)S(1)}, f32[2,16,512]{2,0,1:T(2,128)}, u32[]{:S(2)}) copy-start(f32[2,16,512]{2,0,1:T(2,128)} %get-tuple-element.42) | copy-start | bytes 196612
  276.6 16.5 %all-to-all-start.7 = ((bf16[128,2,512]{2,1,0:T(2,128)(2,1)}), bf16[128,2,512]{2,1,0:T(2,128)(2,1)S(1)}, u32[]{:S(2)}, u32[]{:S(2)}) async-start(bf16[128,2,512]{2,1,0:T(2,128)(2,1)} %copy.86), calls=%async_computation.7 | async-start | bytes 524288 | tf_op jit(solution)/shard_map/all_to_all | solution.py:63

commit v7 on v4

--- a/solution.py
+++ b/solution.py
@@ -50,7 +50,7 @@
 def spread_rows(inputs, groups):
     rows_here, width = inputs.shape
     block = width // groups
-    blocks = inputs.reshape(rows_here, groups, block).transpose(1, 0, 2)
+    blocks = jnp.stack([inputs[:, g * block : (g + 1) * block] for g in range(groups)])
     devices = lax.psum(1, ALL)
     send = jnp.broadcast_to(
         blocks[:, None], (groups, devices // groups, rows_here, block)
@@ -117,25 +117,18 @@
     return result.reshape(steps, HEADS * HEAD).astype(jnp.bfloat16)
 
 
-def element_table(token_elem):
-    return (token_elem[:, None] == jnp.arange(ELEMENTS, dtype=jnp.int32)[None, :]).astype(
-        jnp.float32
-    )
-
-
-def masked_log_probs(logits, remaining, token_elem):
-    element_hot = element_table(token_elem)
-    per_token = jnp.dot(remaining, element_hot.T)
-    allowed = (per_token > 0.5) | (token_elem == ELEMENTS)[None, :]
+def allowed_tokens(remaining, token_elem):
+    elements = remaining.shape[-1]
+    has_element = token_elem < elements
+    picked = jnp.take(remaining, jnp.minimum(token_elem, elements - 1), axis=1)
+    return (picked > 0.5) & has_element[None, :] | (token_elem == ELEMENTS)[None, :]
+
+
+def masked_log_probs(logits, allowed):
     largest = jnp.max(jnp.where(allowed, logits, -jnp.inf), -1, keepdims=True)
     shifted = logits - largest
     denominator = jnp.sum(jnp.where(allowed, jnp.exp(shifted), 0.0), -1, keepdims=True)
     return jnp.where(allowed, shifted - jnp.log(denominator), 0.0)
-
-
-def used_elements(tokens, token_elem):
-    token_hot = (tokens[:, None] == jnp.arange(VOCAB, dtype=jnp.int32)[None, :]).astype(jnp.float32)
-    return jnp.dot(token_hot, element_table(token_elem))
 
 
 def per_device(
@@ -177,11 +170,13 @@
     lowered = project(hidden_units, down_weight)
     result = (residual.astype(jnp.float32) + lowered.astype(jnp.float32)).astype(jnp.bfloat16)
     logits = head_logits(norm_rows(result, final_gain), lm_full)
-    remaining = counts.astype(jnp.float32)
-    first_log = masked_log_probs(logits[0:1], remaining, token_elem)
-    remaining = remaining - used_elements(tokens, token_elem)
-    second_log = masked_log_probs(logits[1:2], remaining, token_elem)
-    return (result[:, None, :], jnp.stack([first_log, second_log]))
+    start_counts = counts.astype(jnp.float32)
+    used = (jnp.arange(ELEMENTS, dtype=jnp.int32)[None, :] == token_elem[tokens][:, None]).astype(
+        jnp.float32
+    )
+    remaining = jnp.concatenate([start_counts, start_counts - used], axis=0)
+    log_probs = masked_log_probs(logits, allowed_tokens(remaining, token_elem))
+    return (result[:, None, :], log_probs[:, None, :])
 
 
 def solution(mesh):

time: 233 us -> 231 us (level)
  waiting for transfers between devices: 71.8 us -> 89.7 us
  blocking collectives: 66.7 us -> 50.9 us
  other arithmetic: 12.7 us -> 9.03 us
    all_to_all x1, blocking collectives: 30.4 us -> 15.2 us  [gather_rows(): got = lax.all_to_all(partial.astype(link_type), ALL, 0, 0, tiled=True)]
    all_to_all x3, waiting for transfers between devices: 37.8 us -> 51.3 us  [gather_rows(): got = lax.all_to_all(partial.astype(link_type), ALL, 0, 0, tiled=True)]
    all_to_all x2, waiting for transfers between devices: 33.4 us -> 36.2 us  [spread_rows(): return lax.all_to_all(send, ALL, 0, 0, tiled=True)]
    unnamed x23 -> x51, local copies, waits for them, and re-layouts: 5.05 us -> 5.47 us
  transfers between devices with their start and end apart: 6 -> 6, of which waited for: 5 -> 6; matrix products, arithmetic and copies ran while one was open for 14% -> 7% of each run, Pallas kernels for 0% -> 0%
where the time goes in v7:
time: 231 us; the launch traced here: 230 us
  waiting for transfers between devices  89.7 us (39%)
  blocking collectives  50.9 us (22%)
  starting transfers between devices  31.1 us (13%)
  matrix products  17.2 us (7%)
  local copies, waits for them, and re-layouts  16.7 us (7%)
  between operations  15.9 us (7%)
  other arithmetic  9.03 us (4%)
    all_to_all x3, waiting for transfers between devices, gather_rows(): got = lax.all_to_all(partial.astype(link_type), ALL, 0, 0, tiled=True)  51.3 us
    all_to_all x2, waiting for transfers between devices, spread_rows(): return lax.all_to_all(send, ALL, 0, 0, tiled=True)  36.2 us
    all_to_all x2, blocking collectives, spread_rows(): return lax.all_to_all(send, ALL, 0, 0, tiled=True)  35.7 us
    all_to_all x2, starting transfers between devices, spread_rows(): return lax.all_to_all(send, ALL, 0, 0, tiled=True)  17.1 us
    all_to_all x1, blocking collectives, gather_rows(): got = lax.all_to_all(partial.astype(link_type), ALL, 0, 0, tiled=True)  15.2 us
    all_to_all x3, starting transfers between devices, gather_rows(): got = lax.all_to_all(partial.astype(link_type), ALL, 0, 0, tiled=True)  14 us
    dot_general x4, matrix products, project(): jnp.einsum('dsk,kn->dsn', spread, weight, preferred_element_type=jnp.floa...  10.3 us
    convert_element_type x4, local copies, waits for them, and re-layouts, gather_rows(): got = lax.all_to_all(partial.astype(link_type), ALL, 0, 0, tiled=True)  5.51 us
  transfers between devices with their start and end apart: 6, of which 6 were waited for; matrix products, arithmetic and copies ran while one was open for 7% of the time, Pallas kernels for 0%

profile of v7, /device:TPU:1, one launch (start us, length us, event | category | flops | bytes accessed | tf_op | source)
XLA Modules:
  0.0 230.5 jit_solution(7366382858975199435)
XLA Ops:
  7.2 0.0 copy-start
  7.2 1.0 fusion.54
  8.2 0.9 fusion.56
  9.2 1.1 broadcast_in_dim.119
  10.3 11.9 %all-to-all-start = ((bf16[128,2,1024]{2,1,0:T(2,128)(2,1)}), bf16[128,2,1024]{2,1,0:T(2,128)(2,1)}, u32[]{:S(2)}, u32[]{:S(2)}) async-start(bf16[128,2,1024]{2,1,0:T(2,128)(2,1)} %bitcast.10), calls=%async_computation | async-start | bytes 1048576 | tf_op jit(solution)/shard_map/all_to_all | solution.py:58
  22.3 3.7 %copy.97 = bf16[128,8,8,128]{3,2,1,0:T(8,128)(2,1)} copy(bf16[128,8,8,128]{3,1,2,0:T(8,128)(2,1)} %bitcast.266) | data formatting | bytes 4194304
  26.0 0.6 copy.96
  27.3 8.6 %all-to-all-done = bf16[128,2,1024]{2,1,0:T(2,128)(2,1)} async-done(((bf16[128,2,1024]{2,1,0:T(2,128)(2,1)}), bf16[128,2,1024]{2,1,0:T(2,128)(2,1)}, u32[]{:S(2)}, u32[]{:S(2)}) %all-to-all-start) | async-done | bytes 524320 | tf_op jit(solution)/shard_map/all_to_all | solution.py:58
  36.0 1.6 fusion.23
  37.6 1.1 copy.71
  38.7 5.0 %all-to-all-start.1 = ((bf16[128,2,640]{2,1,0:T(2,128)(2,1)}), bf16[128,2,640]{2,1,0:T(2,128)(2,1)}, u32[]{:S(2)}, u32[]{:S(2)}) async-start(bf16[128,2,640]{2,1,0:T(2,128)(2,1)} %copy.71), calls=%async_computation.1 | async-start | bytes 655360 | tf_op jit(solution)/shard_map/all_to_all | solution.py:63
  43.7 0.1 multiply_cosine_fusion
  43.8 11.8 %all-to-all-done.1 = bf16[128,2,640]{2,1,0:T(2,128)(2,1)} async-done(((bf16[128,2,640]{2,1,0:T(2,128)(2,1)}), bf16[128,2,640]{2,1,0:T(2,128)(2,1)}, u32[]{:S(2)}, u32[]{:S(2)}) %all-to-all-start.1) | async-done | bytes 327712 | tf_op jit(solution)/shard_map/all_to_all | solution.py:63
  55.6 1.3 reduce
  56.9 0.1 fusion.68
  57.0 0.1 subtract_convert_fusion.1
  57.1 0.8 fusion.87
  57.9 0.4 fusion.88
  58.3 0.2 fusion.42
  58.5 0.1 fusion.81
  58.7 0.1 copy-done.2
  58.7 0.7 fusion.32
  59.4 0.3 fusion.35
  59.9 0.3 broadcast_in_dim.125
  60.2 0.0 copy-start.3
  60.2 0.0 copy-start.5
  60.2 17.8 %all_to_all.40 = bf16[128,2,1024]{2,1,0:T(2,128)(2,1)S(1)} all-to-all(bf16[128,2,1024]{2,1,0:T(2,128)(2,1)S(1)} %bitcast.269), channel_id=1, replica_groups=mesh['gx'=8,'yz'=16] {'gx','yz'}, dimensions={0} | all-to-all | bytes 1048576 | tf_op jit(solution)/shard_map/all_to_all | solution.py:58
  78.0 0.4 convolution_convert_fusion
  78.5 0.3 copy.78
  78.8 15.2 %all_to_all.41 = bf16[128,2,512]{2,1,0:T(2,128)(2,1)S(1)} all-to-all(bf16[128,2,512]{2,1,0:T(2,128)(2,1)S(1)} %copy.78), channel_id=1, replica_groups=mesh['gx'=8,'yz'=16] {'gx','yz'}, dimensions={0} | all-to-all | bytes 524288 | tf_op jit(solution)/shard_map/all_to_all | solution.py:63
  94.0 0.2 reduce.1
  94.2 0.2 fusion.62
  94.4 0.1 fusion.64
  94.7 0.3 broadcast_in_dim.126
  95.0 17.9 %all_to_all.42 = bf16[128,2,1024]{2,1,0:T(2,128)(2,1)S(1)} all-to-all(bf16[128,2,1024]{2,1,0:T(2,128)(2,1)S(1)} %bitcast.270), channel_id=1, replica_groups=mesh['gx'=8,'yz'=16] {'gx','yz'}, dimensions={0} | all-to-all | bytes 1048576 | tf_op jit(solution)/shard_map/all_to_all | solution.py:58
  112.8 5.1 %fusion.2 = bf16[128,2,3584]{2,0,1:T(8,128)(2,1)S(1)} fusion(bf16[1024,3584]{1,0:T(8,128)(2,1)} %param.26, bf16[128,2,1024]{2,1,0:T(2,128)(2,1)S(1)} %all_to_all.42), kind=kOutput, calls=%fused_computation.3 | convolution fusion | flops 1879965696 | bytes 9699328 | tf_op jit(solution)/shard_map/dsk,kn->dsn/dot_general | solution.py:73
  118.0 3.2 %copy.80 = bf16[128,2,3584]{2,1,0:T(2,128)(2,1)} copy(bf16[128,2,3584]{2,0,1:T(8,128)(2,1)S(1)} %fusion.2) | data formatting | bytes 3670016 | tf_op jit(solution)/shard_map/convert_element_type | solution.py:63
  121.2 4.0 %all-to-all-start.5 = ((bf16[128,2,3584]{2,1,0:T(2,128)(2,1)}), bf16[128,2,3584]{2,1,0:T(2,128)(2,1)S(1)}, u32[]{:S(2)}, u32[]{:S(2)}) async-start(bf16[128,2,3584]{2,1,0:T(2,128)(2,1)} %copy.80), calls=%async_computation.5 | async-start | bytes 3670016 | tf_op jit(solution)/shard_map/all_to_all | solution.py:63
  125.2 0.0 all-gather.2.cloned.1.call-start
  125.2 0.7 all-gather.2.cloned.1.call-update
  125.9 26.3 %all-to-all-done.5 = bf16[128,2,3584]{2,1,0:T(2,128)(2,1)S(1)} async-done(((bf16[128,2,3584]{2,1,0:T(2,128)(2,1)}), bf16[128,2,3584]{2,1,0:T(2,128)(2,1)S(1)}, u32[]{:S(2)}, u32[]{:S(2)}) %all-to-all-start.5) | async-done | bytes 1835040 | tf_op jit(solution)/shard_map/all_to_all | solution.py:63
  152.3 2.2 reduce.2
  154.4 0.3 fusion.50
  154.9 2.3 broadcast_in_dim.127
  157.2 5.1 %all-to-all-start.6 = ((bf16[128,2,3584]{2,1,0:T(2,128)(2,1)}), bf16[128,2,3584]{2,1,0:T(2,128)(2,1)S(1)}, u32[]{:S(2)}, u32[]{:S(2)}) async-start(bf16[128,2,3584]{2,1,0:T(2,128)(2,1)} %bitcast.67), calls=%async_computation.6 | async-start | bytes 3670016 | tf_op jit(solution)/shard_map/all_to_all | solution.py:58
  163.0 0.6 dynamic-slice.2
  163.6 0.7 fusion.80
  164.3 0.0 copy-start.4
  164.3 27.6 %all-to-all-done.6 = bf16[128,2,3584]{2,1,0:T(2,128)(2,1)S(1)} async-done(((bf16[128,2,3584]{2,1,0:T(2,128)(2,1)}), bf16[128,2,3584]{2,1,0:T(2,128)(2,1)S(1)}, u32[]{:S(2)}, u32[]{:S(2)}) %all-to-all-start.6) | async-done | bytes 1835040 | tf_op jit(solution)/shard_map/all_to_all | solution.py:58
  191.9 3.1 %fusion.26 = bf16[128,2,512]{2,0,1:T(8,128)(2,1)S(1)} fusion(bf16[3584,512]{1,0:T(8,128)(2,1)} %param.27, bf16[128,2,3584]{2,1,0:T(2,128)(2,1)S(1)} %all-to-all-done.6), kind=kOutput, calls=%fused_computation.17 | convolution fusion | flops 939655168 | bytes 5767168 | tf_op jit(solution)/shard_map/dsk,kn->dsn/dot_general | solution.py:73
  195.0 1.0 copy.82
  196.0 4.9 %all-to-all-start.7 = ((bf16[128,2,512]{2,1,0:T(2,128)(2,1)}), bf16[128,2,512]{2,1,0:T(2,128)(2,1)S(1)}, u32[]{:S(2)}, u32[]{:S(2)}) async-start(bf16[128,2,512]{2,1,0:T(2,128)(2,1)} %copy.82), calls=%async_computation.7 | async-start | bytes 524288 | tf_op jit(solution)/shard_map/all_to_all | solution.py:63
  201.0 0.1 copy.83
  201.0 1.0 gather_fusion
  202.1 0.1 copy.84
  202.2 13.1 %all-to-all-done.7 = bf16[128,2,512]{2,1,0:T(2,128)(2,1)S(1)} async-done(((bf16[128,2,512]{2,1,0:T(2,128)(2,1)}), bf16[128,2,512]{2,1,0:T(2,128)(2,1)S(1)}, u32[]{:S(2)}, u32[]{:S(2)}) %all-to-all-start.7) | async-done | bytes 262176 | tf_op jit(solution)/shard_map/all_to_all | solution.py:63
  215.3 0.3 reduce.3
  215.6 0.2 fusion.59
  215.8 0.7 add_convert_fusion
  216.5 1.5 all-gather.2.cloned.1.call-done
  218.0 4.7 %fusion.74 = (f32[2]{0:T(128)S(1)}, pred[512,2]{0,1:T(4,128)(4,1)S(1)}, f32[2,512]{1,0:T(2,128)S(1)}) fusion(pred[512]{0:T(512)(128)(4,1)S(1)} %get-tuple-element.30, pred[512]{0:T(512)(128)(4,1)S(1)} %get-tuple-element.31, f32[512,2]{0,1:T(2,128)S(1)} %copy.84, pred[512]{0:T(512)(128)(4,1)S(1)} %get-tuple-element.29, ...), kind=kOutput, calls=%fused_computation.129 | convolution fusion | flops 16898046 | bytes 8530448 | tf_op jit(solution)/shard_map/dot_general | solution.py:78
  222.8 0.2 fusion.75
  223.0 0.1 fusion.76
  223.0 0.6 copy.85
  (67 shorter events, 0.7 us)
Async XLA Ops:
  7.2 28.8 %copy-start = (bf16[1024,640]{1,0:T(8,128)(2,1)S(1)}, bf16[1024,640]{1,0:T(8,128)(2,1)}, u32[]{:S(2)}) copy-start(bf16[1024,640]{1,0:T(8,128)(2,1)} %param.23) | copy-start | bytes 3932164
  10.3 25.7 %all-to-all-start = ((bf16[128,2,1024]{2,1,0:T(2,128)(2,1)}), bf16[128,2,1024]{2,1,0:T(2,128)(2,1)}, u32[]{:S(2)}, u32[]{:S(2)}) async-start(bf16[128,2,1024]{2,1,0:T(2,128)(2,1)} %bitcast.10), calls=%async_computation | async-start | bytes 1048576 | tf_op jit(solution)/shard_map/all_to_all | solution.py:58
  22.3 3.7 %copy-start.1 = (bf16[1,1024,1024]{2,1,0:T(8,128)(2,1)S(1)}, bf16[1,1024,1024]{2,1,0:T(8,128)(2,1)}, u32[]{:S(2)}) copy-start(bf16[1,1024,1024]{2,1,0:T(8,128)(2,1)} %param.16) | copy-start | bytes 6291460
  38.7 16.9 %all-to-all-start.1 = ((bf16[128,2,640]{2,1,0:T(2,128)(2,1)}), bf16[128,2,640]{2,1,0:T(2,128)(2,1)}, u32[]{:S(2)}, u32[]{:S(2)}) async-start(bf16[128,2,640]{2,1,0:T(2,128)(2,1)} %copy.71), calls=%async_computation.1 | async-start | bytes 655360 | tf_op jit(solution)/shard_map/all_to_all | solution.py:63
  57.1 1.6 copy-start.2
  59.4 18.6 %copy-start.7 = (bf16[1024,512]{1,0:T(8,128)(2,1)S(1)}, bf16[1024,512]{1,0:T(8,128)(2,1)}, u32[]{:S(2)}) copy-start(bf16[1024,512]{1,0:T(8,128)(2,1)} %param.24) | copy-start | bytes 3145732
  60.2 34.1 %copy-start.3 = (bf16[2,1,8192]{2,0,1:T(2,128)(2,1)S(1)}, bf16[2,1,8192]{2,0,1:T(2,128)(2,1)}, u32[]{:S(2)}) copy-start(bf16[2,1,8192]{2,0,1:T(2,128)(2,1)} %param.15) | copy-start | bytes 98308
  60.2 34.3 %copy-start.5 = (f32[8192]{0:T(1024)S(1)}, f32[8192]{0:T(1024)}, u32[]{:S(2)}) copy-start(f32[8192]{0:T(1024)} %param.25) | copy-start | bytes 98308
  121.2 31.1 %all-to-all-start.5 = ((bf16[128,2,3584]{2,1,0:T(2,128)(2,1)}), bf16[128,2,3584]{2,1,0:T(2,128)(2,1)S(1)}, u32[]{:S(2)}, u32[]{:S(2)}) async-start(bf16[128,2,3584]{2,1,0:T(2,128)(2,1)} %copy.80), calls=%async_computation.5 | async-start | bytes 3670016 | tf_op jit(solution)/shard_map/all_to_all | solution.py:63
  125.2 92.8 %all-gather.2.cloned.1.call-start = ((), (), s32[]{:S(2)}) async-start(), calls=%async_computation.8 | async-start | bytes 8454144 | tf_op jit(solution)/shard_map/all_gather | solution.py:154
  157.2 5.8 %copy-start.8 = (s32[1,16]{1,0:T(1,128)S(1)}, s32[1,16]{1,0:T(1,128)}, u32[]{:S(2)}) copy-start(s32[1,16]{1,0:T(1,128)} %param.19) | copy-start | bytes 196
  157.2 5.8 %copy-start.6 = (s32[512]{0:T(512)S(1)}, s32[512]{0:T(512)}, u32[]{:S(2)}) copy-start(s32[512]{0:T(512)} %param.20) | copy-start | bytes 6148
  157.2 34.7 %all-to-all-start.6 = ((bf16[128,2,3584]{2,1,0:T(2,128)(2,1)}), bf16[128,2,3584]{2,1,0:T(2,128)(2,1)S(1)}, u32[]{:S(2)}, u32[]{:S(2)}) async-start(bf16[128,2,3584]{2,1,0:T(2,128)(2,1)} %bitcast.67), calls=%async_computation.6 | async-start | bytes 3670016 | tf_op jit(solution)/shard_map/all_to_all | solution.py:58
  164.3 53.8 %copy-start.4 = (f32[8192]{0:T(1024)S(1)}, f32[8192]{0:T(1024)}, u32[]{:S(2)}) copy-start(f32[8192]{0:T(1024)} %param.28) | copy-start | bytes 98308
  196.0 19.4 %all-to-all-start.7 = ((bf16[128,2,512]{2,1,0:T(2,128)(2,1)}), bf16[128,2,512]{2,1,0:T(2,128)(2,1)S(1)}, u32[]{:S(2)}, u32[]{:S(2)}) async-start(bf16[128,2,512]{2,1,0:T(2,128)(2,1)} %copy.82), calls=%async_computation.7 | async-start | bytes 524288 | tf_op jit(solution)/shard_map/all_to_all | solution.py:63
Sparse Core Ops, SparseCore 0:
  129.2 88.8 all-gather.1

commit v8 on v7

--- a/solution.py
+++ b/solution.py
@@ -47,10 +47,13 @@
 ALL = ("gx", "yz")
 
 
-def spread_rows(inputs, groups):
+def spread_rows(inputs, groups, sliced=False):
     rows_here, width = inputs.shape
     block = width // groups
-    blocks = jnp.stack([inputs[:, g * block : (g + 1) * block] for g in range(groups)])
+    if sliced:
+        blocks = jnp.stack([inputs[:, g * block : (g + 1) * block] for g in range(groups)])
+    else:
+        blocks = inputs.reshape(rows_here, groups, block).transpose(1, 0, 2)
     devices = lax.psum(1, ALL)
     send = jnp.broadcast_to(
         blocks[:, None], (groups, devices // groups, rows_here, block)
@@ -67,9 +70,9 @@
     return summed.transpose(1, 0, 2).reshape(rows_here, (devices // groups) * width)
 
 
-def project(inputs, weight, link_type=jnp.bfloat16):
+def project(inputs, weight, link_type=jnp.bfloat16, sliced=False):
     groups = lax.psum(1, "gx")
-    spread = spread_rows(inputs, groups)
+    spread = spread_rows(inputs, groups, sliced)
     partial = jnp.einsum("dsk,kn->dsn", spread, weight, preferred_element_type=jnp.float32)
     return gather_rows(partial, groups, link_type).astype(jnp.bfloat16)
 
@@ -154,7 +157,7 @@
     lm_full = lax.all_gather(lm_weight, ALL, axis=0, tiled=True)
     layer_in = hidden_in[:, 0, :]
     positions = lengths[0] + jnp.arange(steps, dtype=jnp.int32)
-    mixed = project(norm_rows(layer_in, attn_gain), qkv_weight)
+    mixed = project(norm_rows(layer_in, attn_gain), qkv_weight, sliced=True)
     queries = rotate(mixed[:, :q_width].reshape(-1, HEADS, HEAD), positions).reshape(-1, q_width)
     keys_now = rotate(
         mixed[:, q_width : q_width + kv_width].reshape(-1, KV_HEADS, HEAD), positions

time: 231 us -> 227 us (0.983)
  waiting for transfers between devices: 89.7 us -> 70 us
  blocking collectives: 50.9 us -> 67 us
    all_to_all x1, blocking collectives: 15.2 us -> 30.4 us  [gather_rows(): got = lax.all_to_all(partial.astype(link_type), ALL, 0, 0, tiled=True)]
    all_to_all x3, waiting for transfers between devices: 51.3 us -> 36.5 us  [gather_rows(): got = lax.all_to_all(partial.astype(link_type), ALL, 0, 0, tiled=True)]
    all_to_all x2, waiting for transfers between devices: 36.2 us -> 32.7 us  [spread_rows(): return lax.all_to_all(send, ALL, 0, 0, tiled=True)]
    unnamed x51 -> x29, local copies, waits for them, and re-layouts: 5.47 us -> 5.19 us
  transfers between devices with their start and end apart: 6 -> 6, of which waited for: 6 -> 5; matrix products, arithmetic and copies ran while one was open for 7% -> 15% of each run, Pallas kernels for 0% -> 0%
where the time goes in v8:
time: 227 us; the launch traced here: 226 us
  waiting for transfers between devices  70 us (31%)
  blocking collectives  67 us (30%)
  starting transfers between devices  31.1 us (14%)
  matrix products  17.2 us (8%)
  local copies, waits for them, and re-layouts  15.9 us (7%)
  between operations  15.8 us (7%)
  other arithmetic  9.04 us (4%)
    all_to_all x2, blocking collectives, spread_rows(): return lax.all_to_all(send, ALL, 0, 0, tiled=True)  36.6 us
    all_to_all x3, waiting for transfers between devices, gather_rows(): got = lax.all_to_all(partial.astype(link_type), ALL, 0, 0, tiled=True)  36.5 us
    all_to_all x2, waiting for transfers between devices, spread_rows(): return lax.all_to_all(send, ALL, 0, 0, tiled=True)  32.7 us
    all_to_all x1, blocking collectives, gather_rows(): got = lax.all_to_all(partial.astype(link_type), ALL, 0, 0, tiled=True)  30.4 us
    all_to_all x2, starting transfers between devices, spread_rows(): return lax.all_to_all(send, ALL, 0, 0, tiled=True)  17.1 us
    all_to_all x3, starting transfers between devices, gather_rows(): got = lax.all_to_all(partial.astype(link_type), ALL, 0, 0, tiled=True)  14 us
    dot_general x4, matrix products, project(): jnp.einsum('dsk,kn->dsn', spread, weight, preferred_element_type=jnp.floa...  10.4 us
    unnamed x29, local copies, waits for them, and re-layouts  5.19 us
  transfers between devices with their start and end apart: 6, of which 5 were waited for; matrix products, arithmetic and copies ran while one was open for 15% of the time, Pallas kernels for 0%

profile of v8, /device:TPU:1, one launch (start us, length us, event | category | flops | bytes accessed | tf_op | source)
XLA Modules:
  0.0 225.9 jit_solution(9856950572791124516)
XLA Ops:
  7.2 0.0 copy-start
  7.2 1.0 fusion.57
  8.2 0.9 fusion.59
  9.2 1.1 broadcast_in_dim.119
  10.3 11.9 %all-to-all-start = ((bf16[128,2,1024]{2,1,0:T(2,128)(2,1)}), bf16[128,2,1024]{2,1,0:T(2,128)(2,1)}, u32[]{:S(2)}, u32[]{:S(2)}) async-start(bf16[128,2,1024]{2,1,0:T(2,128)(2,1)} %bitcast.10), calls=%async_computation | async-start | bytes 1048576 | tf_op jit(solution)/shard_map/all_to_all | solution.py:61
  22.3 0.0 all-gather.2.cloned.1.call-start
  22.3 0.7 all-gather.2.cloned.1.call-update
  23.7 0.0 copy-start.1
  23.7 2.4 %copy.96 = bf16[128,8,8,128]{3,2,1,0:T(8,128)(2,1)S(1)} copy(bf16[128,8,8,128]{3,1,2,0:T(8,128)(2,1)} %bitcast.184) | data formatting | bytes 4194304
  26.0 2.0 copy.97
  28.1 7.9 %all-to-all-done = bf16[128,2,1024]{2,1,0:T(2,128)(2,1)} async-done(((bf16[128,2,1024]{2,1,0:T(2,128)(2,1)}), bf16[128,2,1024]{2,1,0:T(2,128)(2,1)}, u32[]{:S(2)}, u32[]{:S(2)}) %all-to-all-start) | async-done | bytes 524320 | tf_op jit(solution)/shard_map/all_to_all | solution.py:61
  36.0 1.6 fusion.23
  37.6 1.1 copy.70
  38.7 5.0 %all-to-all-start.1 = ((bf16[128,2,640]{2,1,0:T(2,128)(2,1)}), bf16[128,2,640]{2,1,0:T(2,128)(2,1)}, u32[]{:S(2)}, u32[]{:S(2)}) async-start(bf16[128,2,640]{2,1,0:T(2,128)(2,1)} %copy.70), calls=%async_computation.1 | async-start | bytes 655360 | tf_op jit(solution)/shard_map/all_to_all | solution.py:66
  43.7 0.1 multiply_cosine_fusion
  43.8 11.9 %all-to-all-done.1 = bf16[128,2,640]{2,1,0:T(2,128)(2,1)} async-done(((bf16[128,2,640]{2,1,0:T(2,128)(2,1)}), bf16[128,2,640]{2,1,0:T(2,128)(2,1)}, u32[]{:S(2)}, u32[]{:S(2)}) %all-to-all-start.1) | async-done | bytes 327712 | tf_op jit(solution)/shard_map/all_to_all | solution.py:66
  55.7 1.3 reduce
  57.0 0.1 fusion.63
  57.1 0.1 subtract_convert_fusion.1
  57.2 0.8 fusion.83
  58.0 0.4 fusion.84
  58.4 0.1 fusion.77
  58.5 0.2 fusion.42
  58.8 0.1 copy-done.2
  58.8 0.7 fusion.32
  59.5 0.3 fusion.35
  59.8 0.3 broadcast_in_dim.125
  60.1 0.0 copy-start.3
  60.1 0.0 copy-start.5
  60.1 18.8 %all_to_all.40 = bf16[128,2,1024]{2,1,0:T(2,128)(2,1)S(1)} all-to-all(bf16[128,2,1024]{2,1,0:T(2,128)(2,1)S(1)} %bitcast.187), channel_id=1, replica_groups=mesh['gx'=8,'yz'=16] {'gx','yz'}, dimensions={0} | all-to-all | bytes 1048576 | tf_op jit(solution)/shard_map/all_to_all | solution.py:61
  78.9 0.4 convolution_convert_fusion
  79.3 1.0 copy.76
  80.3 4.1 %all-to-all-start.3 = ((bf16[128,2,512]{2,1,0:T(2,128)(2,1)}), bf16[128,2,512]{2,1,0:T(2,128)(2,1)S(1)}, u32[]{:S(2)}, u32[]{:S(2)}) async-start(bf16[128,2,512]{2,1,0:T(2,128)(2,1)} %copy.76), calls=%async_computation.3 | async-start | bytes 524288 | tf_op jit(solution)/shard_map/all_to_all | solution.py:66
  84.5 14.3 %all-to-all-done.3 = bf16[128,2,512]{2,1,0:T(2,128)(2,1)S(1)} async-done(((bf16[128,2,512]{2,1,0:T(2,128)(2,1)}), bf16[128,2,512]{2,1,0:T(2,128)(2,1)S(1)}, u32[]{:S(2)}, u32[]{:S(2)}) %all-to-all-start.3) | async-done | bytes 262176 | tf_op jit(solution)/shard_map/all_to_all | solution.py:66
  98.8 0.2 reduce.1
  99.2 0.2 fusion.51
  99.3 0.1 fusion.65
  99.5 0.3 broadcast_in_dim.126
  99.8 17.8 %all_to_all.41 = bf16[128,2,1024]{2,1,0:T(2,128)(2,1)S(1)} all-to-all(bf16[128,2,1024]{2,1,0:T(2,128)(2,1)S(1)} %bitcast.188), channel_id=1, replica_groups=mesh['gx'=8,'yz'=16] {'gx','yz'}, dimensions={0} | all-to-all | bytes 1048576 | tf_op jit(solution)/shard_map/all_to_all | solution.py:61
  117.6 5.1 %fusion.2 = bf16[128,2,3584]{2,0,1:T(8,128)(2,1)S(1)} fusion(bf16[1024,3584]{1,0:T(8,128)(2,1)} %param.26, bf16[128,2,1024]{2,1,0:T(2,128)(2,1)S(1)} %all_to_all.41), kind=kOutput, calls=%fused_computation.3 | convolution fusion | flops 1879965696 | bytes 9699328 | tf_op jit(solution)/shard_map/dsk,kn->dsn/dot_general | solution.py:76
  122.7 1.9 copy.80
  124.6 30.4 %all_to_all.42 = bf16[128,2,3584]{2,1,0:T(2,128)(2,1)S(1)} all-to-all(bf16[128,2,3584]{2,1,0:T(2,128)(2,1)S(1)} %copy.80), channel_id=1, replica_groups=mesh['gx'=8,'yz'=16] {'gx','yz'}, dimensions={0} | all-to-all | bytes 3670016 | tf_op jit(solution)/shard_map/all_to_all | solution.py:66
  155.0 2.2 reduce.2
  157.2 0.3 fusion.50
  157.5 2.3 broadcast_in_dim.127
  159.8 5.1 %all-to-all-start.6 = ((bf16[128,2,3584]{2,1,0:T(2,128)(2,1)}), bf16[128,2,3584]{2,1,0:T(2,128)(2,1)S(1)}, u32[]{:S(2)}, u32[]{:S(2)}) async-start(bf16[128,2,3584]{2,1,0:T(2,128)(2,1)} %bitcast.47), calls=%async_computation.6 | async-start | bytes 3670016 | tf_op jit(solution)/shard_map/all_to_all | solution.py:61
  165.6 0.6 dynamic-slice.2
  166.2 0.7 fusion.76
  166.8 24.9 %all-to-all-done.6 = bf16[128,2,3584]{2,1,0:T(2,128)(2,1)S(1)} async-done(((bf16[128,2,3584]{2,1,0:T(2,128)(2,1)}), bf16[128,2,3584]{2,1,0:T(2,128)(2,1)S(1)}, u32[]{:S(2)}, u32[]{:S(2)}) %all-to-all-start.6) | async-done | bytes 1835040 | tf_op jit(solution)/shard_map/all_to_all | solution.py:61
  191.7 3.1 %fusion.26 = bf16[128,2,512]{2,0,1:T(8,128)(2,1)S(1)} fusion(bf16[3584,512]{1,0:T(8,128)(2,1)} %param.27, bf16[128,2,3584]{2,1,0:T(2,128)(2,1)S(1)} %all-to-all-done.6), kind=kOutput, calls=%fused_computation.17 | convolution fusion | flops 939655168 | bytes 5767168 | tf_op jit(solution)/shard_map/dsk,kn->dsn/dot_general | solution.py:76
  194.8 0.0 copy-start.4
  194.8 1.0 copy.82
  195.8 4.9 %all-to-all-start.7 = ((bf16[128,2,512]{2,1,0:T(2,128)(2,1)}), bf16[128,2,512]{2,1,0:T(2,128)(2,1)S(1)}, u32[]{:S(2)}, u32[]{:S(2)}) async-start(bf16[128,2,512]{2,1,0:T(2,128)(2,1)} %copy.82), calls=%async_computation.7 | async-start | bytes 524288 | tf_op jit(solution)/shard_map/all_to_all | solution.py:66
  200.8 0.1 copy.83
  200.9 1.0 gather_fusion
  201.9 0.1 copy.84
  202.0 10.3 %all-to-all-done.7 = bf16[128,2,512]{2,1,0:T(2,128)(2,1)S(1)} async-done(((bf16[128,2,512]{2,1,0:T(2,128)(2,1)}), bf16[128,2,512]{2,1,0:T(2,128)(2,1)S(1)}, u32[]{:S(2)}, u32[]{:S(2)}) %all-to-all-start.7) | async-done | bytes 262176 | tf_op jit(solution)/shard_map/all_to_all | solution.py:66
  212.3 0.3 reduce.3
  212.6 0.2 fusion.53
  212.8 0.7 add_convert_fusion
  213.5 4.7 %fusion.70 = (f32[2]{0:T(128)S(1)}, pred[512,2]{0,1:T(4,128)(4,1)S(1)}, f32[2,512]{1,0:T(2,128)S(1)}) fusion(pred[512]{0:T(512)(128)(4,1)S(1)} %get-tuple-element.34, pred[512]{0:T(512)(128)(4,1)S(1)} %get-tuple-element.35, f32[512,2]{0,1:T(2,128)S(1)} %copy.84, pred[512]{0:T(512)(128)(4,1)S(1)} %get-tuple-element.33, ...), kind=kOutput, calls=%fused_computation.95 | convolution fusion | flops 16848894 | bytes 8464912 | tf_op jit(solution)/shard_map/dot_general | solution.py:81
  218.2 0.2 fusion.71
  218.4 0.1 fusion.72
  218.5 0.6 copy.85
  (47 shorter events, 0.5 us)
Async XLA Ops:
  7.2 28.8 %copy-start = (bf16[1024,640]{1,0:T(8,128)(2,1)S(1)}, bf16[1024,640]{1,0:T(8,128)(2,1)}, u32[]{:S(2)}) copy-start(bf16[1024,640]{1,0:T(8,128)(2,1)} %param.23) | copy-start | bytes 3932164
  10.3 25.7 %all-to-all-start = ((bf16[128,2,1024]{2,1,0:T(2,128)(2,1)}), bf16[128,2,1024]{2,1,0:T(2,128)(2,1)}, u32[]{:S(2)}, u32[]{:S(2)}) async-start(bf16[128,2,1024]{2,1,0:T(2,128)(2,1)} %bitcast.10), calls=%async_computation | async-start | bytes 1048576 | tf_op jit(solution)/shard_map/all_to_all | solution.py:61
  22.3 191.2 %all-gather.2.cloned.1.call-start = ((), (), s32[]{:S(2)}) async-start(), calls=%async_computation.8 | async-start | bytes 8454144 | tf_op jit(solution)/shard_map/all_gather | solution.py:157
  23.7 2.4 %copy-start.1 = (bf16[1,1024,1024]{2,1,0:T(8,128)(2,1)S(1)}, bf16[1,1024,1024]{2,1,0:T(8,128)(2,1)}, u32[]{:S(2)}) copy-start(bf16[1,1024,1024]{2,1,0:T(8,128)(2,1)} %param.17) | copy-start | bytes 6291460
  38.7 17.0 %all-to-all-start.1 = ((bf16[128,2,640]{2,1,0:T(2,128)(2,1)}), bf16[128,2,640]{2,1,0:T(2,128)(2,1)}, u32[]{:S(2)}, u32[]{:S(2)}) async-start(bf16[128,2,640]{2,1,0:T(2,128)(2,1)} %copy.70), calls=%async_computation.1 | async-start | bytes 655360 | tf_op jit(solution)/shard_map/all_to_all | solution.py:66
  57.2 1.6 copy-start.2
  58.8 20.1 %copy-start.7 = (bf16[1024,512]{1,0:T(8,128)(2,1)S(1)}, bf16[1024,512]{1,0:T(8,128)(2,1)}, u32[]{:S(2)}) copy-start(bf16[1024,512]{1,0:T(8,128)(2,1)} %param.24) | copy-start | bytes 3145732
  60.1 24.3 %copy-start.3 = (bf16[2,1,8192]{2,0,1:T(2,128)(2,1)S(1)}, bf16[2,1,8192]{2,0,1:T(2,128)(2,1)}, u32[]{:S(2)}) copy-start(bf16[2,1,8192]{2,0,1:T(2,128)(2,1)} %param.15) | copy-start | bytes 98308
  60.1 24.4 %copy-start.5 = (f32[8192]{0:T(1024)S(1)}, f32[8192]{0:T(1024)}, u32[]{:S(2)}) copy-start(f32[8192]{0:T(1024)} %param.25) | copy-start | bytes 98308
  80.3 18.5 %all-to-all-start.3 = ((bf16[128,2,512]{2,1,0:T(2,128)(2,1)}), bf16[128,2,512]{2,1,0:T(2,128)(2,1)S(1)}, u32[]{:S(2)}, u32[]{:S(2)}) async-start(bf16[128,2,512]{2,1,0:T(2,128)(2,1)} %copy.76), calls=%async_computation.3 | async-start | bytes 524288 | tf_op jit(solution)/shard_map/all_to_all | solution.py:66
  159.7 5.8 %copy-start.8 = (s32[1,16]{1,0:T(1,128)S(1)}, s32[1,16]{1,0:T(1,128)}, u32[]{:S(2)}) copy-start(s32[1,16]{1,0:T(1,128)} %param.19) | copy-start | bytes 196
  159.8 5.8 %copy-start.6 = (s32[512]{0:T(512)S(1)}, s32[512]{0:T(512)}, u32[]{:S(2)}) copy-start(s32[512]{0:T(512)} %param.20) | copy-start | bytes 6148
  159.8 31.9 %all-to-all-start.6 = ((bf16[128,2,3584]{2,1,0:T(2,128)(2,1)}), bf16[128,2,3584]{2,1,0:T(2,128)(2,1)S(1)}, u32[]{:S(2)}, u32[]{:S(2)}) async-start(bf16[128,2,3584]{2,1,0:T(2,128)(2,1)} %bitcast.47), calls=%async_computation.6 | async-start | bytes 3670016 | tf_op jit(solution)/shard_map/all_to_all | solution.py:61
  194.8 18.7 %copy-start.4 = (f32[8192]{0:T(1024)S(1)}, f32[8192]{0:T(1024)}, u32[]{:S(2)}) copy-start(f32[8192]{0:T(1024)} %param.28) | copy-start | bytes 98308
  195.8 16.5 %all-to-all-start.7 = ((bf16[128,2,512]{2,1,0:T(2,128)(2,1)}), bf16[128,2,512]{2,1,0:T(2,128)(2,1)S(1)}, u32[]{:S(2)}, u32[]{:S(2)}) async-start(bf16[128,2,512]{2,1,0:T(2,128)(2,1)} %copy.82), calls=%async_computation.7 | async-start | bytes 524288 | tf_op jit(solution)/shard_map/all_to_all | solution.py:66
Sparse Core Ops, SparseCore 0:
  26.2 78.3 all-gather.1
